TPU v7x, 32 devices: a whole 2x2x4 slice. The times are simulated.
32 devices in a mesh: ctx: 16 (over z, y, core), head: 2 (over x).
Axes of the slice: x: 2, y: 2, z: 4, core: 2. Of those that a mesh axis runs over, the one named last changes fastest.
Arguments:
- queries: bfloat16 [2048, 1536], P('ctx', 'head'), may hold values from -45 to 45
- key_rows: bfloat16 [2048, 256], P('ctx', 'head'), may hold values from -5 to 5
- value_rows: bfloat16 [2048, 256], P('ctx', 'head'), may hold values from -18 to 18
- cotangent: bfloat16 [2048, 1536], P('ctx', 'head'), may hold values from -6 to 6
- trace_ids: int32 [2048], P('ctx'), may hold values from 0 to 15, never falling along the last dimension, each value on 1 to 512 neighbouring positions
- correct: int32 [16], replicated, may hold values from 0 to 16, as said below
- group_size: int32 [16], replicated, may hold values from 4 to 16
Outputs:
- log_totals: float32 [2048, 12], P('ctx', 'head')
- grad_queries: float32 [2048, 1536], P('ctx', 'head')
- grad_keys: bfloat16 [2048, 256], P('ctx', 'head')
- grad_values: bfloat16 [2048, 256], P('ctx', 'head')
Inputs may be any that keep to these rules, and one draw needn't show every extreme that they name: correct[g] is at most group_size[g].
All inputs are finite; a program needn't handle non-finite values.
Results may differ from a plain program's by a relative error of at most 0.0054.
Values may be sent and summed in bfloat16 or wider, within the bound.
No kernel may reach another device: no remote copies, remote signals or barrier semaphores. Data moves between devices by JAX's collectives and lax.ppermute only.
A program may use at most 64 MiB of HBM per device.

v0:
```python
import math

import jax
import jax.numpy as jnp
from jax import lax
from jax.sharding import PartitionSpec as P

PASSK = 4


def pass_rate(correct, group_size):
    counts = group_size.astype(jnp.float32)
    hit_counts = correct.astype(jnp.float32)
    product = jnp.ones_like(counts)
    for offset in range(PASSK):
        product = product * (counts - hit_counts - offset) / (counts - offset)
    return 1.0 - product


def body(queries, key_rows, value_rows, cotangent, trace_ids, correct, group_size):
    tok_rows = queries.shape[0]
    half_rows = tok_rows // 2
    row_width = queries.shape[1]
    head_dim = key_rows.shape[1]
    head_count = row_width // head_dim
    ctx_count = lax.axis_size("ctx")
    my_index = lax.axis_index("ctx")
    length = tok_rows * ctx_count
    score_scale = 1.0 / math.sqrt(head_dim)
    pass_rates = pass_rate(correct, group_size)
    traces = jnp.arange(pass_rates.shape[0], dtype=jnp.int32)
    weights = jnp.sum(
        jnp.where(trace_ids[:, None] == traces[None, :], pass_rates[None, :], 0.0), axis=1
    )
    out_grads = (weights[:, None] * cotangent.astype(jnp.float32)).astype(jnp.bfloat16)
    first_base = my_index * tok_rows
    second_base = first_base + half_rows
    local_pos = jnp.arange(half_rows, dtype=jnp.int32)
    positions = jnp.concatenate([first_base + local_pos, second_base + local_pos], 0)
    last_first = first_base + half_rows - 1
    last_second = second_base + half_rows - 1
    query_all = queries.reshape(tok_rows, head_count, head_dim)
    grad_all = out_grads.reshape(tok_rows, head_count, head_dim)

    def run_block(running, key_block, value_block, key_start, block_fn):
        need_first = (key_start <= last_first).astype(jnp.int32)
        need_second = (key_start <= last_second).astype(jnp.int32)
        branch_index = need_first + 2 * need_second

        def skip_block(values_in):
            return values_in

        def first_only(values_in):
            return block_fn((0, half_rows), values_in, key_block, value_block, key_start)

        def second_only(values_in):
            return block_fn((half_rows, tok_rows), values_in, key_block, value_block, key_start)

        def both_halves(values_in):
            return block_fn((0, tok_rows), values_in, key_block, value_block, key_start)

        return lax.switch(branch_index, [skip_block, first_only, second_only, both_halves], running)

    def forward_block(row_span, running, key_block, value_block, key_start):
        row_begin, row_end = row_span
        row_peak, row_total, weighted = running
        query_part = query_all[row_begin:row_end]
        grad_part = grad_all[row_begin:row_end]
        query_pos = positions[row_begin:row_end]
        scores = (
            jnp.einsum("tqd,kd->tqk", query_part, key_block, preferred_element_type=jnp.float32)
            * score_scale
        )
        key_pos = key_start + jnp.arange(key_block.shape[0], dtype=jnp.int32)
        visible = key_pos[None, None, :] <= query_pos[:, None, None]
        block_peak = jnp.max(jnp.where(visible, scores, -1e30), axis=2)
        old_peak = row_peak[row_begin:row_end]
        new_peak = jnp.maximum(old_peak, block_peak)
        exp_terms = jnp.where(visible, jnp.exp(scores - new_peak[:, :, None]), 0.0)
        grad_probs = jnp.einsum(
            "tqd,kd->tqk", grad_part, value_block, preferred_element_type=jnp.float32
        )
        shrink = jnp.exp(old_peak - new_peak)
        new_total = row_total[row_begin:row_end] * shrink + jnp.sum(exp_terms, axis=2)
        new_weighted = weighted[row_begin:row_end] * shrink + jnp.sum(
            exp_terms * grad_probs, axis=2
        )
        return (
            row_peak.at[row_begin:row_end].set(new_peak),
            row_total.at[row_begin:row_end].set(new_total),
            weighted.at[row_begin:row_end].set(new_weighted),
        )

    row_peak = jnp.full((tok_rows, head_count), -1e30, jnp.float32)
    row_total = jnp.zeros((tok_rows, head_count), jnp.float32)
    weighted = jnp.zeros((tok_rows, head_count), jnp.float32)
    key_piece = lax.all_gather(key_rows, "ctx", axis=0, tiled=True)
    value_piece = lax.all_gather(value_rows, "ctx", axis=0, tiled=True)
    piece_rows = key_piece.shape[0]
    block_rows = math.gcd(piece_rows, 512)

    def forward_step(step_index, statistics):
        offset = step_index * block_rows
        key_block = lax.dynamic_slice_in_dim(key_piece, offset, block_rows, 0)
        value_block = lax.dynamic_slice_in_dim(value_piece, offset, block_rows, 0)
        return run_block(statistics, key_block, value_block, offset, forward_block)

    statistics = lax.fori_loop(
        0, piece_rows // block_rows, forward_step, (row_peak, row_total, weighted)
    )
    folded = statistics + (key_piece, value_piece)
    row_peak, row_total, weighted, key_store, value_store = folded
    log_totals = row_peak + jnp.log(row_total)
    delta_rows = weighted / row_total

    def backward_block(row_span, running, key_block, value_block, key_start):
        row_begin, row_end = row_span
        grad_query, zero_block = running
        query_part = query_all[row_begin:row_end]
        grad_part = grad_all[row_begin:row_end]
        query_pos = positions[row_begin:row_end]
        scores = (
            jnp.einsum("tqd,kd->tqk", query_part, key_block, preferred_element_type=jnp.float32)
            * score_scale
        )
        key_pos = key_start + jnp.arange(key_block.shape[0], dtype=jnp.int32)
        visible = key_pos[None, None, :] <= query_pos[:, None, None]
        probabilities = jnp.where(
            visible, jnp.exp(scores - log_totals[row_begin:row_end][:, :, None]), 0.0
        )
        prob_bf16 = probabilities.astype(jnp.bfloat16)
        grad_probs = jnp.einsum(
            "tqd,kd->tqk", grad_part, value_block, preferred_element_type=jnp.float32
        )
        grad_scores = (
            probabilities * (grad_probs - delta_rows[row_begin:row_end][:, :, None])
        ).astype(jnp.bfloat16)
        query_add = (
            jnp.einsum("tqk,kd->tqd", grad_scores, key_block, preferred_element_type=jnp.float32)
            * score_scale
        )
        key_add = (
            jnp.einsum("tqk,tqd->kd", grad_scores, query_part, preferred_element_type=jnp.float32)
            * score_scale
        )
        value_add = jnp.einsum(
            "tqk,tqd->kd", prob_bf16, grad_part, preferred_element_type=jnp.float32
        )
        return (
            grad_query.at[row_begin:row_end].add(query_add),
            jnp.concatenate([key_add, value_add], 1),
        )

    query_zero = jnp.zeros((tok_rows, head_count, head_dim), jnp.float32)
    key_block_rows = math.gcd(length, 512)

    def backward_step(step_index, running):
        grad_query, partial_sums = running
        key_start = step_index * key_block_rows
        key_block = lax.dynamic_slice_in_dim(key_store, key_start, key_block_rows, 0)
        value_block = lax.dynamic_slice_in_dim(value_store, key_start, key_block_rows, 0)
        zero_block = jnp.zeros((key_block_rows, 2 * head_dim), jnp.float32)
        grad_query, block_sums = run_block(
            (grad_query, zero_block), key_block, value_block, key_start, backward_block
        )
        partial_sums = lax.dynamic_update_slice_in_dim(partial_sums, block_sums, key_start, 0)
        return (grad_query, partial_sums)

    grad_query, partial_sums = lax.fori_loop(
        0,
        length // key_block_rows,
        backward_step,
        (query_zero, jnp.zeros((length, 2 * head_dim), jnp.float32)),
    )
    reduced = jnp.sum(
        lax.all_to_all(
            partial_sums.reshape(ctx_count, tok_rows, 2 * head_dim),
            "ctx",
            split_axis=0,
            concat_axis=0,
            tiled=True,
        ),
        axis=0,
    )
    grad_keys = reduced[:, :head_dim].astype(jnp.bfloat16)
    grad_values = reduced[:, head_dim:].astype(jnp.bfloat16)
    query_grads = grad_query.reshape(tok_rows, row_width)
    return (log_totals, query_grads, grad_keys, grad_values)


def solution(mesh):
    return jax.shard_map(
        body,
        mesh=mesh,
        in_specs=(
            P("ctx", "head"),
            P("ctx", "head"),
            P("ctx", "head"),
            P("ctx", "head"),
            P("ctx"),
            P(),
            P(),
        ),
        out_specs=(P("ctx", "head"), P("ctx", "head"), P("ctx", "head"), P("ctx", "head")),
        check_vma=False,
    )
```

profile of v0, /device:TPU:13, one launch (start us, length us, event | category | flops | bytes accessed | tf_op | source)
XLA Modules:
  0.0 124.0 jit_solution(4631487437105801853)
XLA Ops:
  0.7 0.7 fusion.61
  1.4 0.7 select_reduce_fusion.3
  2.1 1.0 multiply_convert_fusion.1
  3.5 1.1 copy.72
  4.8 17.1 %all_gather.6 = bf16[2048,128]{1,0:T(8,128)(2,1)S(1)} all-gather(bf16[128,128]{1,0:T(8,128)(2,1)S(1)} %copy-done.1), channel_id=1, replica_groups=mesh['ctx'=16,'head'=2] {'ctx'}, dimensions={0}, use_global_device_ids=true | all-gather | bytes 557056 | tf_op jit(solution)/shard_map/all_gather | solution.py:97
  21.9 22.8 %all_gather.7 = bf16[2048,128]{1,0:T(8,128)(2,1)S(1)} all-gather(bf16[128,128]{1,0:T(8,128)(2,1)S(1)} %copy-done.2), channel_id=1, replica_groups=mesh['ctx'=16,'head'=2] {'ctx'}, dimensions={0}, use_global_device_ids=true | all-gather | bytes 557056 | tf_op jit(solution)/shard_map/all_gather | solution.py:98
  44.8 3.9 %while.53 = (s32[]{:T(128)}, f32[128,6]{0,1:T(8,128)S(1)}, f32[128,6]{0,1:T(8,128)S(1)}, f32[128,6]{0,1:T(8,128)S(1)}, s32[]{:T(128)}, /*index=5*/s32[]{:T(128)}...) while((s32[]{:T(128)}, f32[128,6]{0,1:T(8,128)S(1)}, ...), condition=%wide.region_15.0_spmd.clone, body=%wide.region_1.15_spmd.clone.sunk | while | flops 205327120 | bytes 6221379 | solution.py:108
  44.8 1.7 %conditional.6 = ((f32[128,6]{0,1:T(8,128)S(1)}, f32[128,6]{0,1:T(8,128)S(1)}, f32[128,6]{0,1:T(8,128)S(1)})) conditional(s32[]{:T(128)} %clamp.18, (f32[128,6]{0,1:T(8,128)S(1)}, f32[128,6]{0,1:T(8,128)S(1)}, f32[128,6]{0,1:T(8,128)S(1)}) %tuple.202, (f32[128,6]{0,1:T(8,128)S(1)}, s32[]{:T(128)}, s32[]{:T(128)}, ...), branch_computations={%region_2.2_spmd, %region_3.6_spmd, %region_7.10_spmd, %region_11.... | conditional | flops 205327104 | bytes 5696036 | solution.py:62
  45.0 0.5 select_reduce_fusion.2
  45.4 0.6 multiply_reduce_fusion
  46.0 0.5 fusion.20
  46.6 1.7 %conditional.6 = ((f32[128,6]{0,1:T(8,128)S(1)}, f32[128,6]{0,1:T(8,128)S(1)}, f32[128,6]{0,1:T(8,128)S(1)})) conditional(s32[]{:T(128)} %clamp.18, (f32[128,6]{0,1:T(8,128)S(1)}, f32[128,6]{0,1:T(8,128)S(1)}, f32[128,6]{0,1:T(8,128)S(1)}) %tuple.202, (f32[128,6]{0,1:T(8,128)S(1)}, s32[]{:T(128)}, s32[]{:T(128)}, ...), branch_computations={%region_2.2_spmd, %region_3.6_spmd, %region_7.10_spmd, %region_11.... | conditional | flops 205327104 | bytes 5696036 | solution.py:62
  46.8 0.5 select_reduce_fusion.2
  47.3 0.6 multiply_reduce_fusion
  47.8 0.5 fusion.20
  48.7 1.5 %broadcast_in_dim.124.clone = f32[2048,256]{1,0:T(8,128)} broadcast(f32[]{:T(128)} %constant.488.clone.1), dimensions={} | broadcast | bytes 2097156 | tf_op jit(solution)/shard_map/broadcast_in_dim | solution.py:173
  50.2 8.7 %while.54 = (s32[]{:T(128)}, f32[128,6,128]{2,0,1:T(8,128)S(1)}, f32[2048,256]{1,0:T(8,128)}, s32[]{:T(128)}, s32[]{:T(128)}, /*index=5*/bf16[2048,128]{1,0:T(8,...) while((s32[]{:T(128)}, f32[128,6,128]{2,0,1:T(8,128)S(1)}, ...), condition=%wide.region_21.22_spmd.clone, body=%wide.region_16.21_spmd.clone.sunk | while | flops 506528256 | bytes 13381159 | solution.py:169
  50.2 2.1 %conditional.7 = (f32[128,6,128]{2,0,1:T(8,128)S(1)}, f32[512,256]{0,1:T(8,128)S(1)}) conditional(s32[]{:T(128)} %clamp.19, f32[128,6,128]{2,0,1:T(8,128)S(1)} %get-tuple-element.1421, (f32[128,6,128]{2,0,1:T(8,128)S(1)}, s32[]{:T(128)}, s32[]{:T(128)}, bf16[128,6,128]{0,2,1:T(8,128)(2,1)S(1)}, ...), branch_computations={%region_17.17_spmd, %region_18.18_spmd, %region_19.19_spmd, %regio... | conditional | flops 506528256 | bytes 10758676 | solution.py:62
  50.4 0.5 exponential_select_fusion.3
  51.2 0.4 multiply_convert_fusion
  52.5 0.8 constant_dynamic-update-slice_fusion.2
  53.4 2.1 %conditional.7 = (f32[128,6,128]{2,0,1:T(8,128)S(1)}, f32[512,256]{0,1:T(8,128)S(1)}) conditional(s32[]{:T(128)} %clamp.19, f32[128,6,128]{2,0,1:T(8,128)S(1)} %get-tuple-element.1421, (f32[128,6,128]{2,0,1:T(8,128)S(1)}, s32[]{:T(128)}, s32[]{:T(128)}, bf16[128,6,128]{0,2,1:T(8,128)(2,1)S(1)}, ...), branch_computations={%region_17.17_spmd, %region_18.18_spmd, %region_19.19_spmd, %regio... | conditional | flops 506528256 | bytes 10758676 | solution.py:62
  53.5 0.5 exponential_select_fusion.3
  55.7 0.9 constant_dynamic-update-slice_fusion.2
  56.9 0.9 constant_dynamic-update-slice_fusion.2
  58.1 0.9 constant_dynamic-update-slice_fusion.2
  58.9 2.9 %copy.78 = f32[16,128,256]{1,2,0:T(8,128)} copy(f32[16,128,256]{2,1,0:T(8,128)} %bitcast.88) | data formatting | bytes 4194304 | tf_op jit(solution)/shard_map/reshape | solution.py:177
  61.8 13.2 %all-to-all-start = ((f32[16,128,256]{1,2,0:T(8,128)}), f32[16,128,256]{1,2,0:T(8,128)S(1)}, u32[]{:S(2)}, u32[]{:S(2)}) async-start(f32[16,128,256]{1,2,0:T(8,128)} %copy.78), calls=%async_computation | async-start | bytes 4194304 | tf_op jit(solution)/shard_map/all_to_all | solution.py:176
  75.2 0.9 copy.80
  76.1 46.3 %all-to-all-done = f32[16,128,256]{1,2,0:T(8,128)S(1)} async-done(((f32[16,128,256]{1,2,0:T(8,128)}), f32[16,128,256]{1,2,0:T(8,128)S(1)}, u32[]{:S(2)}, u32[]{:S(2)}) %all-to-all-start) | async-done | bytes 2097184 | tf_op jit(solution)/shard_map/all_to_all | solution.py:176
  122.5 0.7 copy.82
  123.2 0.7 copy.81
  (76 shorter events, 5.1 us)
Async XLA Ops:
  0.6 4.1 %copy-start.1 = (bf16[128,128]{1,0:T(8,128)(2,1)S(1)}, bf16[128,128]{1,0:T(8,128)(2,1)}, u32[]{:S(2)}) copy-start(bf16[128,128]{1,0:T(8,128)(2,1)} %param.52) | copy-start | bytes 98308
  0.6 21.2 %copy-start.2 = (bf16[128,128]{1,0:T(8,128)(2,1)S(1)}, bf16[128,128]{1,0:T(8,128)(2,1)}, u32[]{:S(2)}) copy-start(bf16[128,128]{1,0:T(8,128)(2,1)} %param.53) | copy-start | bytes 98308
  58.9 2.9 %copy-start = (f32[128,6]{0,1:T(8,128)}, f32[128,6]{0,1:T(8,128)S(1)}, u32[]{:S(2)}) copy-start(f32[128,6]{0,1:T(8,128)S(1)} %get-tuple-element.1469) | copy-start | bytes 9220
  61.8 60.6 %all-to-all-start = ((f32[16,128,256]{1,2,0:T(8,128)}), f32[16,128,256]{1,2,0:T(8,128)S(1)}, u32[]{:S(2)}, u32[]{:S(2)}) async-start(f32[16,128,256]{1,2,0:T(8,128)} %copy.78), calls=%async_computation | async-start | bytes 4194304 | tf_op jit(solution)/shard_map/all_to_all | solution.py:176
where the time goes:
time: 124 us
  waiting for transfers between devices  46.3 us (37%)
  blocking collectives  39.9 us (32%)
  starting transfers between devices  13.2 us (11%)
  local copies, waits for them, and re-layouts  13.1 us (11%)
  matrix products  5.79 us (5%)
  other arithmetic  4.14 us (3%)
    all_to_all x1, waiting for transfers between devices, body(): lax.all_to_all(partial_sums.reshape(ctx_count, tok_rows, 2 * head_dim), '...  46.3 us
    all_gather x1, blocking collectives, body(): value_piece = lax.all_gather(value_rows, 'ctx', axis=0, tiled=True)  22.8 us
    all_gather x1, blocking collectives, body(): key_piece = lax.all_gather(key_rows, 'ctx', axis=0, tiled=True)  17.1 us
    all_to_all x1, starting transfers between devices, body(): lax.all_to_all(partial_sums.reshape(ctx_count, tok_rows, 2 * head_dim), '...  13.2 us
    dynamic_update_slice x8, local copies, waits for them, and re-layouts, backward_step(): lax.dynamic_update_slice_in_dim(partial_sums, block_sums, key_start, 0)  4.17 us
    unnamed x12, local copies, waits for them, and re-layouts  3.83 us
    reshape x1, local copies, waits for them, and re-layouts, body(): partial_sums.reshape(ctx_count, tok_rows, 2 * head_dim)  2.89 us
  transfers between devices with their start and end apart: 1, of which 1 were waited for; matrix products, arithmetic and copies ran while one was open for 1% of the time, Pallas kernels for 0%

commit v1 on v0

--- a/solution.py
+++ b/solution.py
@@ -3,7 +3,7 @@
 import jax
 import jax.numpy as jnp
 from jax import lax
-from jax.sharding import PartitionSpec as P
+from jax.sharding import Mesh, PartitionSpec as P
 
 PASSK = 4
 
@@ -23,8 +23,10 @@
     row_width = queries.shape[1]
     head_dim = key_rows.shape[1]
     head_count = row_width // head_dim
-    ctx_count = lax.axis_size("ctx")
-    my_index = lax.axis_index("ctx")
+    chip_count = lax.axis_size("chip")
+    ctx_count = chip_count * 2
+    core = lax.axis_index("core")
+    my_index = lax.axis_index("chip") * 2 + core
     length = tok_rows * ctx_count
     score_scale = 1.0 / math.sqrt(head_dim)
     pass_rates = pass_rate(correct, group_size)
@@ -94,8 +96,11 @@
     row_peak = jnp.full((tok_rows, head_count), -1e30, jnp.float32)
     row_total = jnp.zeros((tok_rows, head_count), jnp.float32)
     weighted = jnp.zeros((tok_rows, head_count), jnp.float32)
-    key_piece = lax.all_gather(key_rows, "ctx", axis=0, tiled=True)
-    value_piece = lax.all_gather(value_rows, "ctx", axis=0, tiled=True)
+    joined = jnp.concatenate([key_rows, value_rows], 1)
+    spread = jnp.broadcast_to(joined[None], (ctx_count,) + joined.shape)
+    gathered = lax.all_to_all(spread, ("chip", "core"), 0, 0, tiled=True).reshape(length, 2 * head_dim)
+    key_piece = gathered[:, :head_dim]
+    value_piece = gathered[:, head_dim:]
     piece_rows = key_piece.shape[0]
     block_rows = math.gcd(piece_rows, 512)
 
@@ -172,35 +177,33 @@
         backward_step,
         (query_zero, jnp.zeros((length, 2 * head_dim), jnp.float32)),
     )
-    reduced = jnp.sum(
-        lax.all_to_all(
-            partial_sums.reshape(ctx_count, tok_rows, 2 * head_dim),
-            "ctx",
-            split_axis=0,
-            concat_axis=0,
-            tiled=True,
-        ),
-        axis=0,
-    )
-    grad_keys = reduced[:, :head_dim].astype(jnp.bfloat16)
-    grad_values = reduced[:, head_dim:].astype(jnp.bfloat16)
+    chip_rows = 2 * tok_rows
+    chip_sums = partial_sums.reshape(chip_count, chip_rows, 2 * head_dim)
+    key_part = chip_sums[:, :, :head_dim]
+    value_part = chip_sums[:, :, head_dim:]
+    lead = core == 0
+    swapped = lax.ppermute(jnp.where(lead, value_part, key_part), "core", [(0, 1), (1, 0)])
+    own_part = jnp.where(lead, key_part, value_part) + swapped
+    reduced = jnp.sum(lax.all_to_all(own_part, "chip", 0, 0, tiled=True), axis=0).astype(jnp.bfloat16)
+    other = lax.ppermute(
+        jnp.where(lead, reduced[tok_rows:], reduced[:tok_rows]), "core", [(0, 1), (1, 0)]
+    )
+    grad_keys = jnp.where(lead, reduced[:tok_rows], other)
+    grad_values = jnp.where(lead, other, reduced[tok_rows:])
     query_grads = grad_query.reshape(tok_rows, row_width)
     return (log_totals, query_grads, grad_keys, grad_values)
 
 
 def solution(mesh):
+    order = [mesh.axis_names.index("ctx"), mesh.axis_names.index("head")]
+    devices = mesh.devices.transpose(order)
+    ctx_size, head_size = devices.shape
+    chip_mesh = Mesh(devices.reshape(ctx_size // 2, 2, head_size), ("chip", "core", "head"))
+    rows = P(("chip", "core"), "head")
     return jax.shard_map(
         body,
-        mesh=mesh,
-        in_specs=(
-            P("ctx", "head"),
-            P("ctx", "head"),
-            P("ctx", "head"),
-            P("ctx", "head"),
-            P("ctx"),
-            P(),
-            P(),
-        ),
-        out_specs=(P("ctx", "head"), P("ctx", "head"), P("ctx", "head"), P("ctx", "head")),
+        mesh=chip_mesh,
+        in_specs=(rows, rows, rows, rows, P(("chip", "core")), P(), P()),
+        out_specs=(rows, rows, rows, rows),
         check_vma=False,
     )

time: 124 us -> 95.5 us (0.77)
  the two profiles are of different devices: /device:TPU:13 before, /device:TPU:0 now
where the time goes in v1:
time: 95.5 us; the launch traced here: 95.2 us
  blocking collectives  43.6 us (46%)
  waiting for transfers between devices  24.3 us (25%)
  local copies, waits for them, and re-layouts  10.7 us (11%)
  starting transfers between devices  8.26 us (9%)
  other arithmetic  3.86 us (4%)
  matrix products  2.9 us (3%)
    all_to_all x1, blocking collectives, body(): lax.all_to_all(own_part, 'chip', 0, 0, tiled=True)  43.6 us
    all_to_all x1, waiting for transfers between devices, body(): lax.all_to_all(spread, ('chip', 'core'), 0, 0, tiled=True)  21.9 us
    all_to_all x1, starting transfers between devices, body(): lax.all_to_all(spread, ('chip', 'core'), 0, 0, tiled=True)  7.52 us
    dynamic_update_slice x8, local copies, waits for them, and re-layouts, backward_step(): lax.dynamic_update_slice_in_dim(partial_sums, block_sums, key_start, 0)  4.12 us
    unnamed x20, local copies, waits for them, and re-layouts  2.91 us
    ppermute x1, waiting for transfers between devices, body(): lax.ppermute(jnp.where(lead, value_part, key_part), 'core', [(0, 1), (1,...  2.29 us
  transfers between devices with their start and end apart: 3, of which 3 were waited for; matrix products, arithmetic and copies ran while one was open for 2% of the time, Pallas kernels for 0%

profile of v1, /device:TPU:0, one launch (start us, length us, event | category | flops | bytes accessed | tf_op | source)
XLA Modules:
  0.0 95.2 jit_solution(8354682267213618106)
XLA Ops:
  0.6 0.8 pad_maximum_fusion.3
  1.5 1.1 %broadcast_in_dim.127 = bf16[16,128,256]{2,1,0:T(8,128)(2,1)} broadcast(bf16[128,256]{1,0:T(8,128)(2,1)S(1)} %pad_maximum_fusion.3), dimensions={1,2} | broadcast | bytes 1114112 | tf_op jit(solution)/shard_map/broadcast_in_dim | solution.py:100
  2.5 7.5 %all-to-all-start = ((bf16[16,128,256]{2,1,0:T(8,128)(2,1)}), bf16[16,128,256]{2,1,0:T(8,128)(2,1)S(1)}, u32[]{:S(2)}, u32[]{:S(2)}) async-start(bf16[16,128,256]{2,1,0:T(8,128)(2,1)} %broadcast_in_dim.127), calls=%async_computation | async-start | bytes 2097152 | tf_op jit(solution)/shard_map/all_to_all | solution.py:101
  11.1 21.9 %all-to-all-done = bf16[16,128,256]{2,1,0:T(8,128)(2,1)S(1)} async-done(((bf16[16,128,256]{2,1,0:T(8,128)(2,1)}), bf16[16,128,256]{2,1,0:T(8,128)(2,1)S(1)}, u32[]{:S(2)}, u32[]{:S(2)}) %all-to-all-start) | async-done | bytes 1048608 | tf_op jit(solution)/shard_map/all_to_all | solution.py:101
  33.1 2.2 %while.53 = (s32[]{:T(128)}, f32[128,6]{0,1:T(8,128)S(1)}, f32[128,6]{0,1:T(8,128)S(1)}, f32[128,6]{0,1:T(8,128)S(1)}, s32[]{:T(128)}, /*index=5*/s32[]{:T(128)}...) while((s32[]{:T(128)}, f32[128,6]{0,1:T(8,128)S(1)}, ...), condition=%wide.region_15.0_spmd.clone, body=%wide.region_1.15_spmd.clone.sunk | while | flops 205327120 | bytes 6221379 | solution.py:113
  33.2 1.7 %conditional.6 = ((f32[128,6]{0,1:T(8,128)S(1)}, f32[128,6]{0,1:T(8,128)S(1)}, f32[128,6]{0,1:T(8,128)S(1)})) conditional(s32[]{:T(128)} %clamp.18, (f32[128,6]{0,1:T(8,128)S(1)}, f32[128,6]{0,1:T(8,128)S(1)}, f32[128,6]{0,1:T(8,128)S(1)}) %tuple.203, (f32[128,6]{0,1:T(8,128)S(1)}, s32[]{:T(128)}, s32[]{:T(128)}, ...), branch_computations={%region_2.2_spmd, %region_3.6_spmd, %region_7.10_spmd, %region_11.... | conditional | flops 205327104 | bytes 5696036 | solution.py:64
  33.4 0.5 select_reduce_fusion.2
  33.8 0.6 multiply_reduce_fusion
  34.4 0.5 fusion.20
  35.4 1.5 %broadcast_in_dim.131.clone = f32[2048,256]{1,0:T(8,128)} broadcast(f32[]{:T(128)} %constant.492.clone.1), dimensions={} | broadcast | bytes 2097156 | tf_op jit(solution)/shard_map/broadcast_in_dim | solution.py:178
  36.9 6.7 %while.54 = (s32[]{:T(128)}, f32[128,6,128]{2,0,1:T(8,128)S(1)}, f32[2048,256]{1,0:T(8,128)}, s32[]{:T(128)}, s32[]{:T(128)}, /*index=5*/bf16[2048,128]{1,0:T(8,...) while((s32[]{:T(128)}, f32[128,6,128]{2,0,1:T(8,128)S(1)}, ...), condition=%wide.region_21.22_spmd.clone, body=%wide.region_16.21_spmd.clone.sunk | while | flops 506528256 | bytes 13381159 | solution.py:174
  36.9 2.1 %conditional.7 = (f32[128,6,128]{2,0,1:T(8,128)S(1)}, f32[512,256]{0,1:T(8,128)S(1)}) conditional(s32[]{:T(128)} %clamp.19, f32[128,6,128]{2,0,1:T(8,128)S(1)} %get-tuple-element.1423, (f32[128,6,128]{2,0,1:T(8,128)S(1)}, s32[]{:T(128)}, s32[]{:T(128)}, bf16[128,6,128]{0,2,1:T(8,128)(2,1)S(1)}, ...), branch_computations={%region_17.17_spmd, %region_18.18_spmd, %region_19.19_spmd, %regio... | conditional | flops 506528256 | bytes 10758676 | solution.py:64
  37.1 0.5 exponential_select_fusion.3
  37.6 0.3 convolution_bitcast_fusion.4
  37.9 0.4 multiply_convert_fusion
  38.3 0.3 fusion.56
  38.6 0.4 fusion.55
  39.0 0.2 copy.91
  39.2 0.8 constant_dynamic-update-slice_fusion.2
  40.2 0.2 copy.91
  40.4 0.8 constant_dynamic-update-slice_fusion.2
  41.5 0.8 constant_dynamic-update-slice_fusion.2
  42.5 0.2 copy.91
  42.7 0.8 constant_dynamic-update-slice_fusion.2
  43.6 1.8 %slice_select_fusion = f32[8,256,128]{2,1,0:T(8,128)S(1)} fusion(f32[8,256,256]{2,1,0:T(8,128)} %bitcast.89, pred[]{:T(512)S(6)} %eq.19), kind=kLoop, calls=%fused_computation.120 | loop fusion | flops 262144 | bytes 3145729 | tf_op jit(solution)/shard_map/jit(_where)/select_n | solution.py:185
  45.4 0.7 collective-permute-start
  46.0 2.3 %collective-permute-done = f32[8,256,128]{2,1,0:T(8,128)S(1)} collective-permute-done((f32[8,256,128]{2,1,0:T(8,128)S(1)}, f32[8,256,128]{2,1,0:T(8,128)S(1)}, u32[]{:S(2)}, u32[]{:S(2)}) %collective-permute-start) | collective-permute-done | bytes 1048608 | tf_op jit(solution)/shard_map/ppermute | solution.py:185
  48.5 0.3 copy.78
  48.8 43.6 %all_to_all.10 = f32[8,256,128]{1,2,0:T(8,128)S(1)} all-to-all(f32[8,256,128]{1,2,0:T(8,128)S(1)} %copy.78), channel_id=1, replica_groups=mesh['chip'=8,'core'=2,'head'=2] {'chip'}, dimensions={0} | all-to-all | bytes 2097152 | tf_op jit(solution)/shard_map/all_to_all | solution.py:187
  92.7 0.9 copy.80
  93.8 0.7 copy.82
  94.5 0.7 copy.81
  (78 shorter events, 2.9 us)
Async XLA Ops:
  1.4 8.7 %copy-start.4 = (s32[16]{0:T(128)S(1)}, s32[16]{0:T(128)}, u32[]{:S(2)}) copy-start(s32[16]{0:T(128)} %param.56) | copy-start | bytes 196
  1.4 8.7 %copy-start.5 = (s32[16]{0:T(128)S(1)}, s32[16]{0:T(128)}, u32[]{:S(2)}) copy-start(s32[16]{0:T(128)} %param.57) | copy-start | bytes 196
  1.4 8.7 %copy-start.6 = (s32[128]{0:T(128)S(1)}, s32[128]{0:T(128)}, u32[]{:S(2)}) copy-start(s32[128]{0:T(128)} %param.55) | copy-start | bytes 1540
  1.4 8.8 %copy-start.1 = (bf16[128,768]{1,0:T(8,128)(2,1)S(1)}, bf16[128,768]{1,0:T(8,128)(2,1)}, u32[]{:S(2)}) copy-start(bf16[128,768]{1,0:T(8,128)(2,1)} %param.54) | copy-start | bytes 589828
  2.5 8.1 %copy-start.2 = (bf16[128,768]{1,0:T(8,128)(2,1)S(1)}, bf16[128,768]{1,0:T(8,128)(2,1)}, u32[]{:S(2)}) copy-start(bf16[128,768]{1,0:T(8,128)(2,1)} %param.51) | copy-start | bytes 589828
  2.5 30.5 %all-to-all-start = ((bf16[16,128,256]{2,1,0:T(8,128)(2,1)}), bf16[16,128,256]{2,1,0:T(8,128)(2,1)S(1)}, u32[]{:S(2)}, u32[]{:S(2)}) async-start(bf16[16,128,256]{2,1,0:T(8,128)(2,1)} %broadcast_in_dim.127), calls=%async_computation | async-start | bytes 2097152 | tf_op jit(solution)/shard_map/all_to_all | solution.py:101
  43.5 1.8 %copy-start.3 = (f32[128,6]{0,1:T(8,128)}, f32[128,6]{0,1:T(8,128)S(1)}, u32[]{:S(2)}) copy-start(f32[128,6]{0,1:T(8,128)S(1)} %get-tuple-element.1471) | copy-start | bytes 9220
  43.6 4.8 %copy-start = (f32[2048,256]{1,0:T(8,128)S(1)}, f32[2048,256]{1,0:T(8,128)}, u32[]{:S(2)}) copy-start(f32[2048,256]{1,0:T(8,128)} %get-tuple-element.812) | copy-start | bytes 6291460
  45.4 3.0 %collective-permute-start = (f32[8,256,128]{2,1,0:T(8,128)S(1)}, f32[8,256,128]{2,1,0:T(8,128)S(1)}, u32[]{:S(2)}, u32[]{:S(2)}) collective-permute-start(f32[8,256,128]{2,1,0:T(8,128)S(1)} %slice_select_fusion), channel_id=1, source_target_pairs={{0,2},{2,0},{1,3},{3,1},{4,6},{6,4},{5,7},{7,5},{8,10},{10,8},{9,1... | collective-permute-start | bytes 3145736 | tf_op jit(solution)/shard_map/ppermute | solution.py:185
  92.5 1.3 %collective-permute-start.1 = (bf16[128,128]{0,1:T(8,128)(2,1)S(1)}, bf16[128,128]{0,1:T(8,128)(2,1)S(1)}, u32[]{:S(2)}, u32[]{:S(2)}) collective-permute-start(bf16[128,128]{0,1:T(8,128)(2,1)S(1)} %broadcast_select_fusion.2), channel_id=1, source_target_pairs={{0,2},{2,0},{1,3},{3,1},{4,6},{6,4},{5,7},{7,5},{8,10},{10,8},{9,1... | collective-permute-start | bytes 98312 | tf_op jit(solution)/shard_map/ppermute | solution.py:188

commit v2 on v1

v2 whole, which is shorter than its diff:
```python
import functools
import math

import jax
import jax.numpy as jnp
from jax import lax
from jax.experimental import pallas as pl
from jax.experimental.pallas import tpu as pltpu
from jax.sharding import Mesh, PartitionSpec as P

PASSK = 4


def pass_rate(correct, group_size):
    counts = group_size.astype(jnp.float32)
    hit_counts = correct.astype(jnp.float32)
    product = jnp.ones_like(counts)
    for offset in range(PASSK):
        product = product * (counts - hit_counts - offset) / (counts - offset)
    return 1.0 - product


def attention_kernel(
    index_ref, query_ref, grad_ref, key_ref, value_ref,
    lse_ref, dq_ref, dk_ref, dv_ref, *, heads, head_dim, tok_rows, score_scale,
):
    index = index_ref[0]
    block_count = key_ref.shape[0] // tok_rows
    rows = heads * tok_rows
    queries = jnp.concatenate(
        [query_ref[:, h * head_dim:(h + 1) * head_dim] for h in range(heads)], 0
    )
    grads = jnp.concatenate(
        [grad_ref[:, h * head_dim:(h + 1) * head_dim] for h in range(heads)], 0
    )
    row_tok = lax.broadcasted_iota(jnp.int32, (heads, tok_rows, tok_rows), 1).reshape(rows, tok_rows)
    col_tok = lax.broadcasted_iota(jnp.int32, (rows, tok_rows), 1)
    visible = col_tok <= row_tok
    contract_last = (((1,), (1,)), ((), ()))
    contract_first = (((0,), (0,)), ((), ()))

    def scores_of(start):
        key_block = key_ref[pl.ds(start, tok_rows), :]
        scores = lax.dot_general(queries, key_block, contract_last, preferred_element_type=jnp.float32)
        return key_block, scores * score_scale

    def grad_probs_of(start):
        value_block = value_ref[pl.ds(start, tok_rows), :]
        return lax.dot_general(grads, value_block, contract_last, preferred_element_type=jnp.float32)

    def forward(block, carry, masked):
        peak, total, weighted = carry
        start = pl.multiple_of(block * tok_rows, tok_rows)
        _, scores = scores_of(start)
        if masked:
            scores = jnp.where(visible, scores, -1e30)
        grad_probs = grad_probs_of(start)
        new_peak = jnp.maximum(peak, jnp.max(scores, axis=1, keepdims=True))
        exp_terms = jnp.exp(scores - new_peak)
        if masked:
            exp_terms = jnp.where(visible, exp_terms, 0.0)
        shrink = jnp.exp(peak - new_peak)
        total = total * shrink + jnp.sum(exp_terms, axis=1, keepdims=True)
        weighted = weighted * shrink + jnp.sum(exp_terms * grad_probs, axis=1, keepdims=True)
        return new_peak, total, weighted

    start_carry = (
        jnp.full((rows, 1), -1e30, jnp.float32),
        jnp.zeros((rows, 1), jnp.float32),
        jnp.zeros((rows, 1), jnp.float32),
    )
    carry = lax.fori_loop(0, index, lambda b, c: forward(b, c, False), start_carry)
    peak, total, weighted = forward(index, carry, True)
    log_totals = peak + jnp.log(total)
    delta_rows = weighted / total
    lse_ref[...] = log_totals

    def backward(block, grad_query, masked):
        start = pl.multiple_of(block * tok_rows, tok_rows)
        key_block, scores = scores_of(start)
        probabilities = jnp.exp(scores - log_totals)
        if masked:
            probabilities = jnp.where(visible, probabilities, 0.0)
        grad_probs = grad_probs_of(start)
        grad_scores = (probabilities * (grad_probs - delta_rows)).astype(jnp.bfloat16)
        prob_bf16 = probabilities.astype(jnp.bfloat16)
        grad_query = grad_query + jnp.dot(grad_scores, key_block, preferred_element_type=jnp.float32)
        key_add = lax.dot_general(grad_scores, queries, contract_first, preferred_element_type=jnp.float32)
        value_add = lax.dot_general(prob_bf16, grads, contract_first, preferred_element_type=jnp.float32)
        dk_ref[pl.ds(start, tok_rows), :] = key_add * score_scale
        dv_ref[pl.ds(start, tok_rows), :] = value_add
        return grad_query

    grad_query = lax.fori_loop(
        0, index, lambda b, g: backward(b, g, False), jnp.zeros((rows, head_dim), jnp.float32)
    )
    grad_query = backward(index, grad_query, True) * score_scale
    for h in range(heads):
        dq_ref[:, h * head_dim:(h + 1) * head_dim] = grad_query[h * tok_rows:(h + 1) * tok_rows]

    def clear(block, unused):
        start = pl.multiple_of(block * tok_rows, tok_rows)
        dk_ref[pl.ds(start, tok_rows), :] = jnp.zeros((tok_rows, head_dim), jnp.float32)
        dv_ref[pl.ds(start, tok_rows), :] = jnp.zeros((tok_rows, head_dim), jnp.float32)
        return unused

    lax.fori_loop(index + 1, block_count, clear, 0)


def body(queries, key_rows, value_rows, cotangent, trace_ids, correct, group_size):
    tok_rows = queries.shape[0]
    row_width = queries.shape[1]
    head_dim = key_rows.shape[1]
    head_count = row_width // head_dim
    chip_count = lax.axis_size("chip")
    ctx_count = chip_count * 2
    core = lax.axis_index("core")
    my_index = lax.axis_index("chip") * 2 + core
    length = tok_rows * ctx_count
    score_scale = 1.0 / math.sqrt(head_dim)
    pass_rates = pass_rate(correct, group_size)
    traces = jnp.arange(pass_rates.shape[0], dtype=jnp.int32)
    weights = jnp.sum(
        jnp.where(trace_ids[:, None] == traces[None, :], pass_rates[None, :], 0.0), axis=1
    )
    out_grads = (weights[:, None] * cotangent.astype(jnp.float32)).astype(jnp.bfloat16)

    joined = jnp.concatenate([key_rows, value_rows], 1)
    spread = jnp.broadcast_to(joined[None], (ctx_count,) + joined.shape)
    gathered = lax.all_to_all(spread, ("chip", "core"), 0, 0, tiled=True).reshape(length, 2 * head_dim)
    key_piece = gathered[:, :head_dim]
    value_piece = gathered[:, head_dim:]

    rows = head_count * tok_rows
    vmem = pl.BlockSpec(memory_space=pltpu.MemorySpace.VMEM)
    smem = pl.BlockSpec(memory_space=pltpu.MemorySpace.SMEM)
    kernel = functools.partial(
        attention_kernel, heads=head_count, head_dim=head_dim, tok_rows=tok_rows, score_scale=score_scale
    )
    stacked_lse, query_grads, key_part, value_part = pl.pallas_call(
        kernel,
        out_shape=(
            jax.ShapeDtypeStruct((rows, 1), jnp.float32),
            jax.ShapeDtypeStruct((tok_rows, row_width), jnp.float32),
            jax.ShapeDtypeStruct((length, head_dim), jnp.float32),
            jax.ShapeDtypeStruct((length, head_dim), jnp.float32),
        ),
        in_specs=[smem, vmem, vmem, vmem, vmem],
        out_specs=(vmem, vmem, vmem, vmem),
    )(my_index.reshape(1).astype(jnp.int32), queries, out_grads, key_piece, value_piece)
    log_totals = stacked_lse.reshape(head_count, tok_rows).T

    chip_rows = 2 * tok_rows
    key_part = key_part.reshape(chip_count, chip_rows, head_dim)
    value_part = value_part.reshape(chip_count, chip_rows, head_dim)
    lead = core == 0
    swapped = lax.ppermute(jnp.where(lead, value_part, key_part), "core", [(0, 1), (1, 0)])
    own_part = jnp.where(lead, key_part, value_part) + swapped
    reduced = jnp.sum(lax.all_to_all(own_part, "chip", 0, 0, tiled=True), axis=0).astype(jnp.bfloat16)
    other = lax.ppermute(
        jnp.where(lead, reduced[tok_rows:], reduced[:tok_rows]), "core", [(0, 1), (1, 0)]
    )
    grad_keys = jnp.where(lead, reduced[:tok_rows], other)
    grad_values = jnp.where(lead, other, reduced[tok_rows:])
    return (log_totals, query_grads, grad_keys, grad_values)


def solution(mesh):
    order = [mesh.axis_names.index("ctx"), mesh.axis_names.index("head")]
    devices = mesh.devices.transpose(order)
    ctx_size, head_size = devices.shape
    chip_mesh = Mesh(devices.reshape(ctx_size // 2, 2, head_size), ("chip", "core", "head"))
    rows = P(("chip", "core"), "head")
    return jax.shard_map(
        body,
        mesh=chip_mesh,
        in_specs=(rows, rows, rows, rows, P(("chip", "core")), P(), P()),
        out_specs=(rows, rows, rows, rows),
        check_vma=False,
    )
```

time: 95.5 us -> 96.8 us (1.014)
  local copies, waits for them, and re-layouts: 10.7 us -> 4.27 us
  blocking collectives: 43.6 us -> 49.4 us
  Pallas kernels: 0 us -> 4.41 us
  matrix products: 2.9 us -> 0 us
  starting transfers between devices: 8.26 us -> 9.63 us
  waiting for transfers between devices: 24.3 us -> 23 us
  other arithmetic: 3.86 us -> 4.96 us
    all_to_all x1, blocking collectives: 43.6 us -> 49.4 us  [body(): lax.all_to_all(own_part, 'chip', 0, 0, tiled=True)]
    pallas_call x0 -> x1, Pallas kernels: none -> 4.41 us  [body(): pl.pallas_call(kernel, out_shape=(jax.ShapeDtypeStruct((rows, 1), jnp.flo...]
    dynamic_update_slice x8 -> x0, local copies, waits for them, and re-layouts: 4.12 us -> none  [backward_step(): lax.dynamic_update_slice_in_dim(partial_sums, block_sums, key_start, 0)]
    dot_general x7 -> x0, matrix products: 2.9 us -> none  [the longest x1 0.57 us: forward_block(): jnp.einsum('tqd,kd->tqk', grad_part, value_block, preferred_element_type=...]
    broadcast_in_dim x3 -> x0, local copies, waits for them, and re-layouts: 1.51 us -> none  [the longest x1 1.48 us: body(): jnp.zeros((length, 2 * head_dim), jnp.float32)]
    ppermute x1, starting transfers between devices: 0.68 us -> 2.04 us  [body(): lax.ppermute(jnp.where(lead, value_part, key_part), 'core', [(0, 1), (1,...]
    all_to_all x1, waiting for transfers between devices: 21.9 us -> 20.7 us  [body(): lax.all_to_all(spread, ('chip', 'core'), 0, 0, tiled=True)]
    slice x1, local copies, waits for them, and re-layouts: 0.07 us -> 1.06 us  [body(): value_piece = gathered[:, head_dim:]]
  transfers between devices with their start and end apart: 3 -> 3, of which waited for: 3 -> 2; matrix products, arithmetic and copies ran while one was open for 2% -> 2% of each run, Pallas kernels for 0% -> 0%
where the time goes in v2:
time: 96.8 us; the launch traced here: 96.4 us
  blocking collectives  49.4 us (51%)
  waiting for transfers between devices  23 us (24%)
  starting transfers between devices  9.63 us (10%)
  other arithmetic  4.96 us (5%)
  Pallas kernels  4.41 us (5%)
  local copies, waits for them, and re-layouts  4.27 us (4%)
    all_to_all x1, blocking collectives, body(): lax.all_to_all(own_part, 'chip', 0, 0, tiled=True)  49.4 us
    all_to_all x1, waiting for transfers between devices, body(): lax.all_to_all(spread, ('chip', 'core'), 0, 0, tiled=True)  20.7 us
    all_to_all x1, starting transfers between devices, body(): lax.all_to_all(spread, ('chip', 'core'), 0, 0, tiled=True)  7.52 us
    pallas_call x1, Pallas kernels, body(): pl.pallas_call(kernel, out_shape=(jax.ShapeDtypeStruct((rows, 1), jnp.flo...  4.41 us
    ppermute x1, waiting for transfers between devices, body(): lax.ppermute(jnp.where(lead, value_part, key_part), 'core', [(0, 1), (1,...  2.29 us
    unnamed x10, local copies, waits for them, and re-layouts  2.15 us
    ppermute x1, starting transfers between devices, body(): lax.ppermute(jnp.where(lead, value_part, key_part), 'core', [(0, 1), (1,...  2.04 us
  transfers between devices with their start and end apart: 3, of which 2 were waited for; matrix products, arithmetic and copies ran while one was open for 2% of the time, Pallas kernels for 0%

profile of v2, /device:TPU:0, one launch (start us, length us, event | category | flops | bytes accessed | tf_op | source)
XLA Modules:
  0.0 96.4 jit_solution(9499231845286058909)
XLA Ops:
  0.6 0.8 pad_maximum_fusion
  1.4 1.1 %broadcast_in_dim.24 = bf16[16,128,256]{2,1,0:T(8,128)(2,1)} broadcast(bf16[128,256]{1,0:T(8,128)(2,1)S(1)} %pad_maximum_fusion), dimensions={1,2} | broadcast | bytes 1114112 | tf_op jit(solution)/shard_map/broadcast_in_dim | solution.py:129
  2.5 0.0 copy-start.1
  2.5 7.5 %all-to-all-start = ((bf16[16,128,256]{2,1,0:T(8,128)(2,1)}), bf16[16,128,256]{2,1,0:T(8,128)(2,1)S(1)}, u32[]{:S(2)}, u32[]{:S(2)}) async-start(bf16[16,128,256]{2,1,0:T(8,128)(2,1)} %broadcast_in_dim.24), calls=%async_computation | async-start | bytes 2097152 | tf_op jit(solution)/shard_map/all_to_all | solution.py:130
  10.0 0.0 copy-start.2
  10.0 0.0 copy-start.3
  10.0 0.6 copy-done.2
  10.7 0.0 copy-done.3
  10.7 0.0 copy-start.4
  10.7 0.6 copy-done.4
  11.3 0.1 select_reduce_fusion
  11.4 0.0 copy-done.1
  11.4 0.8 multiply_convert_fusion.grad_ref
  12.2 20.7 %all-to-all-done = bf16[16,128,256]{2,1,0:T(8,128)(2,1)S(1)} async-done(((bf16[16,128,256]{2,1,0:T(8,128)(2,1)}), bf16[16,128,256]{2,1,0:T(8,128)(2,1)S(1)}, u32[]{:S(2)}, u32[]{:S(2)}) %all-to-all-start) | async-done | bytes 1048608 | tf_op jit(solution)/shard_map/all_to_all | solution.py:130
  33.0 1.1 %fusion.1 = (bf16[2048,128]{1,0:T(8,128)(2,1)}, bf16[2048,128]{1,0:T(8,128)(2,1)}) fusion(bf16[2048,256]{1,0:T(8,128)(2,1)S(1)} %bitcast.8), kind=kLoop, calls=%fused_computation.12 | loop fusion | bytes 2097152 | tf_op jit(solution)/shard_map/slice | solution.py:132
  34.0 4.4 %shard_map.102 = (f32[768,1]{1,0:T(8,128)}, f32[128,768]{1,0:T(8,128)}, f32[2048,128]{1,0:T(8,128)}, f32[2048,128]{1,0:T(8,128)}) custom-call(s32[1]{0:T(128)} %bitcast.index_ref, bf16[128,768]{1,0:T(8,128)(2,1)} %query_ref.1, bf16[128,768]{1,0:T(8,128)(2,1)} %multiply_convert_fusion.grad_ref, bf16[2048,128]{1,0:T(8,128)(2,1)} %get-tuple-element.15.key_ref, ...), custom_call_target="tpu_custom_call" | custom-call | tf_op jit(solution)/shard_map/pallas_call | solution.py:140
  38.4 1.7 %broadcast_select_fusion = (f32[2048,128]{1,0:T(8,128)S(1)}, f32[2048,128]{1,0:T(8,128)S(1)}) fusion(f32[2048,128]{1,0:T(8,128)} %get-tuple-element.11, f32[2048,128]{1,0:T(8,128)} %get-tuple-element.10, pred[]{:T(512)S(6)} %eq.19), kind=kLoop, calls=%fused_computation | loop fusion | flops 524288 | bytes 4194305 | tf_op jit(solution)/shard_map/jit(_where)/select_n | solution.py:157
  40.1 2.0 %collective-permute-start = (f32[8,256,128]{2,1,0:T(8,128)S(1)}, f32[8,256,128]{2,1,0:T(8,128)S(1)}, u32[]{:S(2)}, u32[]{:S(2)}) collective-permute-start(f32[8,256,128]{2,1,0:T(8,128)S(1)} %bitcast.9), channel_id=1, source_target_pairs={{0,2},{2,0},{1,3},{3,1},{4,6},{6,4},{5,7},{7,5},{8,10},{10,8},{9,1... | collective-permute-start | bytes 3145736 | tf_op jit(solution)/shard_map/ppermute | solution.py:157
  42.1 2.3 %collective-permute-done = f32[8,256,128]{2,1,0:T(8,128)S(1)} collective-permute-done((f32[8,256,128]{2,1,0:T(8,128)S(1)}, f32[8,256,128]{2,1,0:T(8,128)S(1)}, u32[]{:S(2)}, u32[]{:S(2)}) %collective-permute-start) | collective-permute-done | bytes 1048608 | tf_op jit(solution)/shard_map/ppermute | solution.py:157
  44.4 0.2 add.13
  44.6 49.4 %all_to_all.10 = f32[8,256,128]{2,1,0:T(8,128)S(1)} all-to-all(f32[8,256,128]{2,1,0:T(8,128)S(1)} %add.13), channel_id=1, replica_groups=mesh['chip'=8,'core'=2,'head'=2] {'chip'}, dimensions={0} | all-to-all | bytes 2097152 | tf_op jit(solution)/shard_map/all_to_all | solution.py:159
  94.0 0.0 copy-start
  94.0 0.1 reduce_sum.19
  94.0 0.1 collective-permute-start.1
  94.1 0.8 copy-done
  95.0 0.8 reduce
  95.7 0.0 collective-permute-done.1
  95.7 0.6 broadcast_select_fusion.2
  (2 shorter events, 0.0 us)
Async XLA Ops:
  2.5 9.0 %copy-start.1 = (bf16[128,768]{1,0:T(8,128)(2,1)S(1)}, bf16[128,768]{1,0:T(8,128)(2,1)}, u32[]{:S(2)}) copy-start(bf16[128,768]{1,0:T(8,128)(2,1)} %param.10) | copy-start | bytes 589828
  2.5 30.5 %all-to-all-start = ((bf16[16,128,256]{2,1,0:T(8,128)(2,1)}), bf16[16,128,256]{2,1,0:T(8,128)(2,1)S(1)}, u32[]{:S(2)}, u32[]{:S(2)}) async-start(bf16[16,128,256]{2,1,0:T(8,128)(2,1)} %broadcast_in_dim.24), calls=%async_computation | async-start | bytes 2097152 | tf_op jit(solution)/shard_map/all_to_all | solution.py:130
  10.0 0.7 copy-start.2
  10.0 0.7 copy-start.3
  10.7 0.7 copy-start.4
  40.1 4.3 %collective-permute-start = (f32[8,256,128]{2,1,0:T(8,128)S(1)}, f32[8,256,128]{2,1,0:T(8,128)S(1)}, u32[]{:S(2)}, u32[]{:S(2)}) collective-permute-start(f32[8,256,128]{2,1,0:T(8,128)S(1)} %bitcast.9), channel_id=1, source_target_pairs={{0,2},{2,0},{1,3},{3,1},{4,6},{6,4},{5,7},{7,5},{8,10},{10,8},{9,1... | collective-permute-start | bytes 3145736 | tf_op jit(solution)/shard_map/ppermute | solution.py:157
  94.0 1.0 %copy-start = (f32[768,1]{1,0:T(8,128)S(1)}, f32[768,1]{1,0:T(8,128)}, u32[]{:S(2)}) copy-start(f32[768,1]{1,0:T(8,128)} %get-tuple-element.8) | copy-start | bytes 9220
  94.0 1.7 %collective-permute-start.1 = (bf16[128,128]{1,0:T(8,128)(2,1)S(1)}, bf16[128,128]{1,0:T(8,128)(2,1)S(1)}, u32[]{:S(2)}, u32[]{:S(2)}) collective-permute-start(bf16[128,128]{1,0:T(8,128)(2,1)S(1)} %broadcast_select_fusion.4), channel_id=1, source_target_pairs={{0,2},{2,0},{1,3},{3,1},{4,6},{6,4},{5,7},{7,5},{8,10},{10,8},{9,1... | collective-permute-start | bytes 98312 | tf_op jit(solution)/shard_map/ppermute | solution.py:160

commit v3 on v2

--- a/solution.py
+++ b/solution.py
@@ -33,41 +33,39 @@
     grads = jnp.concatenate(
         [grad_ref[:, h * head_dim:(h + 1) * head_dim] for h in range(heads)], 0
     )
-    row_tok = lax.broadcasted_iota(jnp.int32, (heads, tok_rows, tok_rows), 1).reshape(rows, tok_rows)
-    col_tok = lax.broadcasted_iota(jnp.int32, (rows, tok_rows), 1)
-    visible = col_tok <= row_tok
-    contract_last = (((1,), (1,)), ((), ()))
+    queries_t = queries.astype(jnp.float32).T.astype(jnp.bfloat16)
+    grads_t = grads.astype(jnp.float32).T.astype(jnp.bfloat16)
+    key_tok = lax.broadcasted_iota(jnp.int32, (tok_rows, rows), 0)
+    row_tok = lax.rem(lax.broadcasted_iota(jnp.int32, (tok_rows, rows), 1), tok_rows)
+    visible = key_tok <= row_tok
     contract_first = (((0,), (0,)), ((), ()))
 
-    def scores_of(start):
+    def blocks_of(block):
+        start = pl.multiple_of(block * tok_rows, tok_rows)
         key_block = key_ref[pl.ds(start, tok_rows), :]
-        scores = lax.dot_general(queries, key_block, contract_last, preferred_element_type=jnp.float32)
-        return key_block, scores * score_scale
-
-    def grad_probs_of(start):
         value_block = value_ref[pl.ds(start, tok_rows), :]
-        return lax.dot_general(grads, value_block, contract_last, preferred_element_type=jnp.float32)
+        scores = jnp.dot(key_block, queries_t, preferred_element_type=jnp.float32) * score_scale
+        grad_probs = jnp.dot(value_block, grads_t, preferred_element_type=jnp.float32)
+        return start, key_block, scores, grad_probs
 
     def forward(block, carry, masked):
         peak, total, weighted = carry
-        start = pl.multiple_of(block * tok_rows, tok_rows)
-        _, scores = scores_of(start)
+        _, _, scores, grad_probs = blocks_of(block)
         if masked:
             scores = jnp.where(visible, scores, -1e30)
-        grad_probs = grad_probs_of(start)
-        new_peak = jnp.maximum(peak, jnp.max(scores, axis=1, keepdims=True))
+        new_peak = jnp.maximum(peak, jnp.max(scores, axis=0, keepdims=True))
         exp_terms = jnp.exp(scores - new_peak)
         if masked:
             exp_terms = jnp.where(visible, exp_terms, 0.0)
         shrink = jnp.exp(peak - new_peak)
-        total = total * shrink + jnp.sum(exp_terms, axis=1, keepdims=True)
-        weighted = weighted * shrink + jnp.sum(exp_terms * grad_probs, axis=1, keepdims=True)
+        total = total * shrink + jnp.sum(exp_terms, axis=0, keepdims=True)
+        weighted = weighted * shrink + jnp.sum(exp_terms * grad_probs, axis=0, keepdims=True)
         return new_peak, total, weighted
 
     start_carry = (
-        jnp.full((rows, 1), -1e30, jnp.float32),
-        jnp.zeros((rows, 1), jnp.float32),
-        jnp.zeros((rows, 1), jnp.float32),
+        jnp.full((1, rows), -1e30, jnp.float32),
+        jnp.zeros((1, rows), jnp.float32),
+        jnp.zeros((1, rows), jnp.float32),
     )
     carry = lax.fori_loop(0, index, lambda b, c: forward(b, c, False), start_carry)
     peak, total, weighted = forward(index, carry, True)
@@ -75,26 +73,26 @@
     delta_rows = weighted / total
     lse_ref[...] = log_totals
 
-    def backward(block, grad_query, masked):
-        start = pl.multiple_of(block * tok_rows, tok_rows)
-        key_block, scores = scores_of(start)
+    def backward(block, grad_query_t, masked):
+        start, key_block, scores, grad_probs = blocks_of(block)
         probabilities = jnp.exp(scores - log_totals)
         if masked:
             probabilities = jnp.where(visible, probabilities, 0.0)
-        grad_probs = grad_probs_of(start)
         grad_scores = (probabilities * (grad_probs - delta_rows)).astype(jnp.bfloat16)
         prob_bf16 = probabilities.astype(jnp.bfloat16)
-        grad_query = grad_query + jnp.dot(grad_scores, key_block, preferred_element_type=jnp.float32)
-        key_add = lax.dot_general(grad_scores, queries, contract_first, preferred_element_type=jnp.float32)
-        value_add = lax.dot_general(prob_bf16, grads, contract_first, preferred_element_type=jnp.float32)
+        grad_query_t = grad_query_t + lax.dot_general(
+            key_block, grad_scores, contract_first, preferred_element_type=jnp.float32
+        )
+        key_add = jnp.dot(grad_scores, queries, preferred_element_type=jnp.float32)
+        value_add = jnp.dot(prob_bf16, grads, preferred_element_type=jnp.float32)
         dk_ref[pl.ds(start, tok_rows), :] = key_add * score_scale
         dv_ref[pl.ds(start, tok_rows), :] = value_add
-        return grad_query
+        return grad_query_t
 
-    grad_query = lax.fori_loop(
-        0, index, lambda b, g: backward(b, g, False), jnp.zeros((rows, head_dim), jnp.float32)
+    grad_query_t = lax.fori_loop(
+        0, index, lambda b, g: backward(b, g, False), jnp.zeros((head_dim, rows), jnp.float32)
     )
-    grad_query = backward(index, grad_query, True) * score_scale
+    grad_query = (backward(index, grad_query_t, True) * score_scale).T
     for h in range(heads):
         dq_ref[:, h * head_dim:(h + 1) * head_dim] = grad_query[h * tok_rows:(h + 1) * tok_rows]
 
@@ -140,7 +138,7 @@
     stacked_lse, query_grads, key_part, value_part = pl.pallas_call(
         kernel,
         out_shape=(
-            jax.ShapeDtypeStruct((rows, 1), jnp.float32),
+            jax.ShapeDtypeStruct((1, rows), jnp.float32),
             jax.ShapeDtypeStruct((tok_rows, row_width), jnp.float32),
             jax.ShapeDtypeStruct((length, head_dim), jnp.float32),
             jax.ShapeDtypeStruct((length, head_dim), jnp.float32),

time: 96.8 us -> 91 us (0.940)
  blocking collectives: 49.4 us -> 44.7 us
    all_to_all x1, blocking collectives: 49.4 us -> 44.7 us  [body(): lax.all_to_all(own_part, 'chip', 0, 0, tiled=True)]
where the time goes in v3:
time: 91 us; the launch traced here: 90.6 us
  blocking collectives  44.7 us (49%)
  waiting for transfers between devices  23 us (25%)
  starting transfers between devices  9.17 us (10%)
  other arithmetic  4.8 us (5%)
  Pallas kernels  4.14 us (5%)
  local copies, waits for them, and re-layouts  4.01 us (4%)
    all_to_all x1, blocking collectives, body(): lax.all_to_all(own_part, 'chip', 0, 0, tiled=True)  44.7 us
    all_to_all x1, waiting for transfers between devices, body(): lax.all_to_all(spread, ('chip', 'core'), 0, 0, tiled=True)  20.7 us
    all_to_all x1, starting transfers between devices, body(): lax.all_to_all(spread, ('chip', 'core'), 0, 0, tiled=True)  7.52 us
    pallas_call x1, Pallas kernels, body(): pl.pallas_call(kernel, out_shape=(jax.ShapeDtypeStruct((1, rows), jnp.flo...  4.14 us
    ppermute x1, waiting for transfers between devices, body(): lax.ppermute(jnp.where(lead, value_part, key_part), 'core', [(0, 1), (1,...  2.29 us
    unnamed x10, local copies, waits for them, and re-layouts  1.88 us
  transfers between devices with their start and end apart: 3, of which 2 were waited for; matrix products, arithmetic and copies ran while one was open for 2% of the time, Pallas kernels for 0%

profile of v3, /device:TPU:0, one launch (start us, length us, event | category | flops | bytes accessed | tf_op | source)
XLA Modules:
  0.0 90.6 jit_solution(12677246052532747230)
XLA Ops:
  0.6 0.8 pad_maximum_fusion
  1.4 1.1 %broadcast_in_dim.24 = bf16[16,128,256]{2,1,0:T(8,128)(2,1)} broadcast(bf16[128,256]{1,0:T(8,128)(2,1)S(1)} %pad_maximum_fusion), dimensions={1,2} | broadcast | bytes 1114112 | tf_op jit(solution)/shard_map/broadcast_in_dim | solution.py:127
  2.5 0.0 copy-start
  2.5 7.5 %all-to-all-start = ((bf16[16,128,256]{2,1,0:T(8,128)(2,1)}), bf16[16,128,256]{2,1,0:T(8,128)(2,1)S(1)}, u32[]{:S(2)}, u32[]{:S(2)}) async-start(bf16[16,128,256]{2,1,0:T(8,128)(2,1)} %broadcast_in_dim.24), calls=%async_computation | async-start | bytes 2097152 | tf_op jit(solution)/shard_map/all_to_all | solution.py:128
  10.0 0.0 copy-start.2
  10.0 0.0 copy-start.3
  10.0 0.6 copy-done.2
  10.7 0.0 copy-done.3
  10.7 0.0 copy-start.4
  10.7 0.6 copy-done.4
  11.3 0.1 select_reduce_fusion
  11.4 0.0 copy-done
  11.4 0.8 multiply_convert_fusion.grad_ref
  12.2 20.7 %all-to-all-done = bf16[16,128,256]{2,1,0:T(8,128)(2,1)S(1)} async-done(((bf16[16,128,256]{2,1,0:T(8,128)(2,1)}), bf16[16,128,256]{2,1,0:T(8,128)(2,1)S(1)}, u32[]{:S(2)}, u32[]{:S(2)}) %all-to-all-start) | async-done | bytes 1048608 | tf_op jit(solution)/shard_map/all_to_all | solution.py:128
  33.0 1.1 %fusion.1 = (bf16[2048,128]{1,0:T(8,128)(2,1)}, bf16[2048,128]{1,0:T(8,128)(2,1)}) fusion(bf16[2048,256]{1,0:T(8,128)(2,1)S(1)} %bitcast.8), kind=kLoop, calls=%fused_computation.12 | loop fusion | bytes 2097152 | tf_op jit(solution)/shard_map/slice | solution.py:130
  34.0 4.1 %shard_map.102 = (f32[1,768]{1,0:T(1,128)}, f32[128,768]{1,0:T(8,128)}, f32[2048,128]{1,0:T(8,128)}, f32[2048,128]{1,0:T(8,128)}) custom-call(s32[1]{0:T(128)} %bitcast.index_ref, bf16[128,768]{1,0:T(8,128)(2,1)} %query_ref.1, bf16[128,768]{1,0:T(8,128)(2,1)} %multiply_convert_fusion.grad_ref, bf16[2048,128]{1,0:T(8,128)(2,1)} %get-tuple-element.15.key_ref, ...), custom_call_target="tpu_custom_call" | custom-call | tf_op jit(solution)/shard_map/pallas_call | solution.py:138
  38.2 1.7 %broadcast_select_fusion = (f32[2048,128]{1,0:T(8,128)S(1)}, f32[2048,128]{1,0:T(8,128)S(1)}) fusion(f32[2048,128]{1,0:T(8,128)} %get-tuple-element.11, f32[2048,128]{1,0:T(8,128)} %get-tuple-element.10, pred[]{:T(512)S(6)} %eq.19), kind=kLoop, calls=%fused_computation | loop fusion | flops 524288 | bytes 4194305 | tf_op jit(solution)/shard_map/jit(_where)/select_n | solution.py:155
  39.8 1.6 %collective-permute-start = (f32[8,256,128]{2,1,0:T(8,128)S(1)}, f32[8,256,128]{2,1,0:T(8,128)S(1)}, u32[]{:S(2)}, u32[]{:S(2)}) collective-permute-start(f32[8,256,128]{2,1,0:T(8,128)S(1)} %bitcast.9), channel_id=1, source_target_pairs={{0,2},{2,0},{1,3},{3,1},{4,6},{6,4},{5,7},{7,5},{8,10},{10,8},{9,1... | collective-permute-start | bytes 3145736 | tf_op jit(solution)/shard_map/ppermute | solution.py:155
  41.4 2.3 %collective-permute-done = f32[8,256,128]{2,1,0:T(8,128)S(1)} collective-permute-done((f32[8,256,128]{2,1,0:T(8,128)S(1)}, f32[8,256,128]{2,1,0:T(8,128)S(1)}, u32[]{:S(2)}, u32[]{:S(2)}) %collective-permute-start) | collective-permute-done | bytes 1048608 | tf_op jit(solution)/shard_map/ppermute | solution.py:155
  43.7 0.2 add.13
  43.9 44.7 %all_to_all.10 = f32[8,256,128]{2,1,0:T(8,128)S(1)} all-to-all(f32[8,256,128]{2,1,0:T(8,128)S(1)} %add.13), channel_id=1, replica_groups=mesh['chip'=8,'core'=2,'head'=2] {'chip'}, dimensions={0} | all-to-all | bytes 2097152 | tf_op jit(solution)/shard_map/all_to_all | solution.py:157
  88.6 0.1 reduce_sum.19
  88.7 0.0 copy-start.1
  88.7 0.1 collective-permute-start.1
  88.8 0.6 copy-done.1
  89.4 0.6 reduce
  90.0 0.0 collective-permute-done.1
  90.0 0.6 broadcast_select_fusion.2
  (2 shorter events, 0.0 us)
Async XLA Ops:
  2.5 9.0 %copy-start = (bf16[128,768]{1,0:T(8,128)(2,1)S(1)}, bf16[128,768]{1,0:T(8,128)(2,1)}, u32[]{:S(2)}) copy-start(bf16[128,768]{1,0:T(8,128)(2,1)} %param.10) | copy-start | bytes 589828
  2.5 30.5 %all-to-all-start = ((bf16[16,128,256]{2,1,0:T(8,128)(2,1)}), bf16[16,128,256]{2,1,0:T(8,128)(2,1)S(1)}, u32[]{:S(2)}, u32[]{:S(2)}) async-start(bf16[16,128,256]{2,1,0:T(8,128)(2,1)} %broadcast_in_dim.24), calls=%async_computation | async-start | bytes 2097152 | tf_op jit(solution)/shard_map/all_to_all | solution.py:128
  10.0 0.7 copy-start.2
  10.0 0.7 copy-start.3
  10.7 0.7 copy-start.4
  39.8 3.9 %collective-permute-start = (f32[8,256,128]{2,1,0:T(8,128)S(1)}, f32[8,256,128]{2,1,0:T(8,128)S(1)}, u32[]{:S(2)}, u32[]{:S(2)}) collective-permute-start(f32[8,256,128]{2,1,0:T(8,128)S(1)} %bitcast.9), channel_id=1, source_target_pairs={{0,2},{2,0},{1,3},{3,1},{4,6},{6,4},{5,7},{7,5},{8,10},{10,8},{9,1... | collective-permute-start | bytes 3145736 | tf_op jit(solution)/shard_map/ppermute | solution.py:155
  88.7 0.7 copy-start.1
  88.7 1.3 %collective-permute-start.1 = (bf16[128,128]{1,0:T(8,128)(2,1)S(1)}, bf16[128,128]{1,0:T(8,128)(2,1)S(1)}, u32[]{:S(2)}, u32[]{:S(2)}) collective-permute-start(bf16[128,128]{1,0:T(8,128)(2,1)S(1)} %broadcast_select_fusion.4), channel_id=1, source_target_pairs={{0,2},{2,0},{1,3},{3,1},{4,6},{6,4},{5,7},{7,5},{8,10},{10,8},{9,1... | collective-permute-start | bytes 98312 | tf_op jit(solution)/shard_map/ppermute | solution.py:158

commit v4 on v3

--- a/solution.py
+++ b/solution.py
@@ -21,11 +21,12 @@
 
 
 def attention_kernel(
-    index_ref, query_ref, grad_ref, key_ref, value_ref,
-    lse_ref, dq_ref, dk_ref, dv_ref, *, heads, head_dim, tok_rows, score_scale,
+    index_ref, query_ref, grad_ref, joined_ref,
+    lse_ref, dq_ref, keep_ref, send_ref, *, heads, head_dim, tok_rows, score_scale,
 ):
     index = index_ref[0]
-    block_count = key_ref.shape[0] // tok_rows
+    lead = index_ref[1] == 0
+    block_count = joined_ref.shape[0] // tok_rows
     rows = heads * tok_rows
     queries = jnp.concatenate(
         [query_ref[:, h * head_dim:(h + 1) * head_dim] for h in range(heads)], 0
@@ -42,8 +43,8 @@
 
     def blocks_of(block):
         start = pl.multiple_of(block * tok_rows, tok_rows)
-        key_block = key_ref[pl.ds(start, tok_rows), :]
-        value_block = value_ref[pl.ds(start, tok_rows), :]
+        key_block = joined_ref[pl.ds(start, tok_rows), :head_dim]
+        value_block = joined_ref[pl.ds(start, tok_rows), head_dim:]
         scores = jnp.dot(key_block, queries_t, preferred_element_type=jnp.float32) * score_scale
         grad_probs = jnp.dot(value_block, grads_t, preferred_element_type=jnp.float32)
         return start, key_block, scores, grad_probs
@@ -85,8 +86,18 @@
         )
         key_add = jnp.dot(grad_scores, queries, preferred_element_type=jnp.float32)
         value_add = jnp.dot(prob_bf16, grads, preferred_element_type=jnp.float32)
-        dk_ref[pl.ds(start, tok_rows), :] = key_add * score_scale
-        dv_ref[pl.ds(start, tok_rows), :] = value_add
+        key_add = key_add * score_scale
+
+        @pl.when(lead)
+        def _():
+            keep_ref[pl.ds(start, tok_rows), :] = key_add
+            send_ref[pl.ds(start, tok_rows), :] = value_add
+
+        @pl.when(jnp.logical_not(lead))
+        def _():
+            keep_ref[pl.ds(start, tok_rows), :] = value_add
+            send_ref[pl.ds(start, tok_rows), :] = key_add
+
         return grad_query_t
 
     grad_query_t = lax.fori_loop(
@@ -98,8 +109,8 @@
 
     def clear(block, unused):
         start = pl.multiple_of(block * tok_rows, tok_rows)
-        dk_ref[pl.ds(start, tok_rows), :] = jnp.zeros((tok_rows, head_dim), jnp.float32)
-        dv_ref[pl.ds(start, tok_rows), :] = jnp.zeros((tok_rows, head_dim), jnp.float32)
+        keep_ref[pl.ds(start, tok_rows), :] = jnp.zeros((tok_rows, head_dim), jnp.float32)
+        send_ref[pl.ds(start, tok_rows), :] = jnp.zeros((tok_rows, head_dim), jnp.float32)
         return unused
 
     lax.fori_loop(index + 1, block_count, clear, 0)
@@ -126,8 +137,6 @@
     joined = jnp.concatenate([key_rows, value_rows], 1)
     spread = jnp.broadcast_to(joined[None], (ctx_count,) + joined.shape)
     gathered = lax.all_to_all(spread, ("chip", "core"), 0, 0, tiled=True).reshape(length, 2 * head_dim)
-    key_piece = gathered[:, :head_dim]
-    value_piece = gathered[:, head_dim:]
 
     rows = head_count * tok_rows
     vmem = pl.BlockSpec(memory_space=pltpu.MemorySpace.VMEM)
@@ -135,7 +144,7 @@
     kernel = functools.partial(
         attention_kernel, heads=head_count, head_dim=head_dim, tok_rows=tok_rows, score_scale=score_scale
     )
-    stacked_lse, query_grads, key_part, value_part = pl.pallas_call(
+    stacked_lse, query_grads, keep_part, send_part = pl.pallas_call(
         kernel,
         out_shape=(
             jax.ShapeDtypeStruct((1, rows), jnp.float32),
@@ -143,17 +152,16 @@
             jax.ShapeDtypeStruct((length, head_dim), jnp.float32),
             jax.ShapeDtypeStruct((length, head_dim), jnp.float32),
         ),
-        in_specs=[smem, vmem, vmem, vmem, vmem],
+        in_specs=[smem, vmem, vmem, vmem],
         out_specs=(vmem, vmem, vmem, vmem),
-    )(my_index.reshape(1).astype(jnp.int32), queries, out_grads, key_piece, value_piece)
+    )(jnp.stack([my_index, core]).astype(jnp.int32), queries, out_grads, gathered)
     log_totals = stacked_lse.reshape(head_count, tok_rows).T
 
     chip_rows = 2 * tok_rows
-    key_part = key_part.reshape(chip_count, chip_rows, head_dim)
-    value_part = value_part.reshape(chip_count, chip_rows, head_dim)
+    keep_part = keep_part.reshape(chip_count, chip_rows, head_dim)
+    send_part = send_part.reshape(chip_count, chip_rows, head_dim)
     lead = core == 0
-    swapped = lax.ppermute(jnp.where(lead, value_part, key_part), "core", [(0, 1), (1, 0)])
-    own_part = jnp.where(lead, key_part, value_part) + swapped
+    own_part = keep_part + lax.ppermute(send_part, "core", [(0, 1), (1, 0)])
     reduced = jnp.sum(lax.all_to_all(own_part, "chip", 0, 0, tiled=True), axis=0).astype(jnp.bfloat16)
     other = lax.ppermute(
         jnp.where(lead, reduced[tok_rows:], reduced[:tok_rows]), "core", [(0, 1), (1, 0)]

time: 91 us -> 92.5 us (1.016)
  blocking collectives: 44.7 us -> 0 us
  waiting for transfers between devices: 23 us -> 49.5 us
  starting transfers between devices: 9.17 us -> 28.2 us
  other arithmetic: 4.8 us -> 5.9 us
    all_to_all x1 -> x0, blocking collectives: 44.7 us -> none  [body(): lax.all_to_all(own_part, 'chip', 0, 0, tiled=True)]
    all_to_all x0 -> x1, waiting for transfers between devices: none -> 26.3 us  [body(): lax.all_to_all(own_part, 'chip', 0, 0, tiled=True)]
    all_to_all x0 -> x1, starting transfers between devices: none -> 19 us  [body(): lax.all_to_all(own_part, 'chip', 0, 0, tiled=True)]
    add x1, other arithmetic: 0.16 us -> 2.35 us  [body(): own_part = keep_part + lax.ppermute(send_part, 'core', [(0, 1), (1, 0)])]
    select_n x1 -> x0, other arithmetic: 1.68 us -> none  [body(): jnp.where(lead, value_part, key_part)]
    slice x1 -> x0, local copies, waits for them, and re-layouts: 1.06 us -> none  [body(): value_piece = gathered[:, head_dim:]]
    unnamed x10 -> x12, local copies, waits for them, and re-layouts: 1.88 us -> 2.32 us
  transfers between devices with their start and end apart: 3 -> 4, of which waited for: 2 -> 3; matrix products, arithmetic and copies ran while one was open for 2% -> 2% of each run, Pallas kernels for 0% -> 0%
where the time goes in v4:
time: 92.5 us; the launch traced here: 92 us
  waiting for transfers between devices  49.5 us (54%)
  starting transfers between devices  28.2 us (30%)
  other arithmetic  5.9 us (6%)
  Pallas kernels  4.33 us (5%)
  local copies, waits for them, and re-layouts  3.4 us (4%)
    all_to_all x1, waiting for transfers between devices, body(): lax.all_to_all(own_part, 'chip', 0, 0, tiled=True)  26.3 us
    all_to_all x1, waiting for transfers between devices, body(): lax.all_to_all(spread, ('chip', 'core'), 0, 0, tiled=True)  20.7 us
    all_to_all x1, starting transfers between devices, body(): lax.all_to_all(own_part, 'chip', 0, 0, tiled=True)  19 us
    all_to_all x1, starting transfers between devices, body(): lax.all_to_all(spread, ('chip', 'core'), 0, 0, tiled=True)  7.52 us
    pallas_call x1, Pallas kernels, body(): pl.pallas_call(kernel, out_shape=(jax.ShapeDtypeStruct((1, rows), jnp.flo...  4.33 us
    ppermute x1, waiting for transfers between devices, body(): own_part = keep_part + lax.ppermute(send_part, 'core', [(0, 1), (1, 0)])  2.5 us
    add x1, other arithmetic, body(): own_part = keep_part + lax.ppermute(send_part, 'core', [(0, 1), (1, 0)])  2.35 us
    unnamed x12, local copies, waits for them, and re-layouts  2.32 us
  transfers between devices with their start and end apart: 4, of which 3 were waited for; matrix products, arithmetic and copies ran while one was open for 2% of the time, Pallas kernels for 0%

profile of v4, /device:TPU:0, one launch (start us, length us, event | category | flops | bytes accessed | tf_op | source)
XLA Modules:
  0.0 92.0 jit_solution(880051521596873344)
XLA Ops:
  0.6 0.8 pad_maximum_fusion
  1.4 1.1 %broadcast_in_dim.24 = bf16[16,128,256]{2,1,0:T(8,128)(2,1)} broadcast(bf16[128,256]{1,0:T(8,128)(2,1)S(1)} %pad_maximum_fusion), dimensions={1,2} | broadcast | bytes 1114112 | tf_op jit(solution)/shard_map/broadcast_in_dim | solution.py:138
  2.5 0.0 copy-start.1
  2.5 7.5 %all-to-all-start = ((bf16[16,128,256]{2,1,0:T(8,128)(2,1)}), bf16[16,128,256]{2,1,0:T(8,128)(2,1)S(1)}, u32[]{:S(2)}, u32[]{:S(2)}) async-start(bf16[16,128,256]{2,1,0:T(8,128)(2,1)} %broadcast_in_dim.24), calls=%async_computation | async-start | bytes 2097152 | tf_op jit(solution)/shard_map/all_to_all | solution.py:139
  10.0 0.0 copy-start.3
  10.0 0.0 copy-start.4
  10.1 0.6 pad_add_fusion.index_ref
  10.6 0.0 copy-done.3
  10.7 0.0 copy-done.4
  10.7 0.0 copy-start.5
  10.7 0.6 copy-done.5
  11.4 0.1 select_reduce_fusion
  11.4 0.0 copy-done.1
  11.4 0.8 multiply_convert_fusion.grad_ref
  12.2 20.7 %all-to-all-done = bf16[16,128,256]{2,1,0:T(8,128)(2,1)S(1)} async-done(((bf16[16,128,256]{2,1,0:T(8,128)(2,1)}), bf16[16,128,256]{2,1,0:T(8,128)(2,1)S(1)}, u32[]{:S(2)}, u32[]{:S(2)}) %all-to-all-start) | async-done | bytes 1048608 | tf_op jit(solution)/shard_map/all_to_all | solution.py:139
  33.0 0.0 copy-start
  33.0 1.0 %copy-done = bf16[16,128,256]{2,1,0:T(8,128)(2,1)} copy-done((bf16[16,128,256]{2,1,0:T(8,128)(2,1)}, bf16[16,128,256]{2,1,0:T(8,128)(2,1)S(1)}, u32[]{:S(2)}) %copy-start) | copy-done | bytes 1048600
  34.0 4.3 %shard_map.102 = (f32[1,768]{1,0:T(1,128)}, f32[128,768]{1,0:T(8,128)}, f32[2048,128]{1,0:T(8,128)}, f32[2048,128]{1,0:T(8,128)}) custom-call(s32[2]{0:T(128)} %pad_add_fusion.index_ref, bf16[128,768]{1,0:T(8,128)(2,1)} %query_ref.1, bf16[128,768]{1,0:T(8,128)(2,1)} %multiply_convert_fusion.grad_ref, bf16[2048,256]{1,0:T(8,128)(2,1)} %bitcast.8), custom_call_target="tpu_custom_call" | custom-call | tf_op jit(solution)/shard_map/pallas_call | solution.py:147
  38.3 1.5 %collective-permute-start = (f32[8,256,128]{2,1,0:T(8,128)}, f32[8,256,128]{2,1,0:T(8,128)S(1)}, u32[]{:S(2)}, u32[]{:S(2)}) collective-permute-start(f32[8,256,128]{2,1,0:T(8,128)} %bitcast.11), channel_id=1, source_target_pairs={{0,2},{2,0},{1,3},{3,1},{4,6},{6,4},{5,7},{7,5},{8,10},{10,8},{9,1... | collective-permute-start | bytes 3145736 | tf_op jit(solution)/shard_map/ppermute | solution.py:164
  39.9 2.5 %collective-permute-done = f32[8,256,128]{2,1,0:T(8,128)S(1)} collective-permute-done((f32[8,256,128]{2,1,0:T(8,128)}, f32[8,256,128]{2,1,0:T(8,128)S(1)}, u32[]{:S(2)}, u32[]{:S(2)}) %collective-permute-start) | collective-permute-done | bytes 1048608 | tf_op jit(solution)/shard_map/ppermute | solution.py:164
  42.4 2.4 %add.13 = f32[8,256,128]{2,1,0:T(8,128)} add(f32[8,256,128]{2,1,0:T(8,128)} %bitcast.9, f32[8,256,128]{2,1,0:T(8,128)S(1)} %collective-permute-done) | non-fusion elementwise | flops 262144 | bytes 3145728 | tf_op jit(solution)/shard_map/add | solution.py:164
  44.7 19.0 %all-to-all-start.1 = ((f32[8,256,128]{2,1,0:T(8,128)}), f32[8,256,128]{2,1,0:T(8,128)S(1)}, u32[]{:S(2)}, u32[]{:S(2)}) async-start(f32[8,256,128]{2,1,0:T(8,128)} %add.13), calls=%async_computation.1 | async-start | bytes 2097152 | tf_op jit(solution)/shard_map/all_to_all | solution.py:165
  63.8 26.3 %all-to-all-done.1 = f32[8,256,128]{2,1,0:T(8,128)S(1)} async-done(((f32[8,256,128]{2,1,0:T(8,128)}), f32[8,256,128]{2,1,0:T(8,128)S(1)}, u32[]{:S(2)}, u32[]{:S(2)}) %all-to-all-start.1) | async-done | bytes 1048608 | tf_op jit(solution)/shard_map/all_to_all | solution.py:165
  90.0 0.1 reduce_sum.19
  90.1 0.0 copy-start.2
  90.1 0.1 collective-permute-start.1
  90.2 0.6 copy-done.2
  90.8 0.6 reduce
  91.4 0.0 collective-permute-done.1
  91.4 0.6 broadcast_select_fusion
  (2 shorter events, 0.0 us)
Async XLA Ops:
  2.5 9.0 %copy-start.1 = (bf16[128,768]{1,0:T(8,128)(2,1)S(1)}, bf16[128,768]{1,0:T(8,128)(2,1)}, u32[]{:S(2)}) copy-start(bf16[128,768]{1,0:T(8,128)(2,1)} %param.10) | copy-start | bytes 589828
  2.5 30.5 %all-to-all-start = ((bf16[16,128,256]{2,1,0:T(8,128)(2,1)}), bf16[16,128,256]{2,1,0:T(8,128)(2,1)S(1)}, u32[]{:S(2)}, u32[]{:S(2)}) async-start(bf16[16,128,256]{2,1,0:T(8,128)(2,1)} %broadcast_in_dim.24), calls=%async_computation | async-start | bytes 2097152 | tf_op jit(solution)/shard_map/all_to_all | solution.py:139
  10.0 0.7 copy-start.3
  10.0 0.7 copy-start.4
  10.7 0.7 copy-start.5
  33.0 1.0 %copy-start = (bf16[16,128,256]{2,1,0:T(8,128)(2,1)}, bf16[16,128,256]{2,1,0:T(8,128)(2,1)S(1)}, u32[]{:S(2)}) copy-start(bf16[16,128,256]{2,1,0:T(8,128)(2,1)S(1)} %all-to-all-done) | copy-start | bytes 3145732
  38.3 4.0 %collective-permute-start = (f32[8,256,128]{2,1,0:T(8,128)}, f32[8,256,128]{2,1,0:T(8,128)S(1)}, u32[]{:S(2)}, u32[]{:S(2)}) collective-permute-start(f32[8,256,128]{2,1,0:T(8,128)} %bitcast.11), channel_id=1, source_target_pairs={{0,2},{2,0},{1,3},{3,1},{4,6},{6,4},{5,7},{7,5},{8,10},{10,8},{9,1... | collective-permute-start | bytes 3145736 | tf_op jit(solution)/shard_map/ppermute | solution.py:164
  44.7 45.3 %all-to-all-start.1 = ((f32[8,256,128]{2,1,0:T(8,128)}), f32[8,256,128]{2,1,0:T(8,128)S(1)}, u32[]{:S(2)}, u32[]{:S(2)}) async-start(f32[8,256,128]{2,1,0:T(8,128)} %add.13), calls=%async_computation.1 | async-start | bytes 2097152 | tf_op jit(solution)/shard_map/all_to_all | solution.py:165
  90.1 0.7 copy-start.2
  90.1 1.3 %collective-permute-start.1 = (bf16[128,128]{1,0:T(8,128)(2,1)S(1)}, bf16[128,128]{1,0:T(8,128)(2,1)S(1)}, u32[]{:S(2)}, u32[]{:S(2)}) collective-permute-start(bf16[128,128]{1,0:T(8,128)(2,1)S(1)} %broadcast_select_fusion.2), channel_id=1, source_target_pairs={{0,2},{2,0},{1,3},{3,1},{4,6},{6,4},{5,7},{7,5},{8,10},{10,8},{9,1... | collective-permute-start | bytes 98312 | tf_op jit(solution)/shard_map/ppermute | solution.py:166

commit v5 on v3

--- a/solution.py
+++ b/solution.py
@@ -21,11 +21,12 @@
 
 
 def attention_kernel(
-    index_ref, query_ref, grad_ref, key_ref, value_ref,
+    index_ref, query_ref, grad_ref, mine_ref, other_ref,
     lse_ref, dq_ref, dk_ref, dv_ref, *, heads, head_dim, tok_rows, score_scale,
 ):
     index = index_ref[0]
-    block_count = key_ref.shape[0] // tok_rows
+    core = index_ref[1]
+    block_count = 2 * mine_ref.shape[0] // tok_rows
     rows = heads * tok_rows
     queries = jnp.concatenate(
         [query_ref[:, h * head_dim:(h + 1) * head_dim] for h in range(heads)], 0
@@ -42,8 +43,14 @@
 
     def blocks_of(block):
         start = pl.multiple_of(block * tok_rows, tok_rows)
-        key_block = key_ref[pl.ds(start, tok_rows), :]
-        value_block = value_ref[pl.ds(start, tok_rows), :]
+        source = pl.multiple_of((block // 2) * tok_rows, tok_rows)
+        joined_block = jnp.where(
+            block % 2 == core,
+            mine_ref[pl.ds(source, tok_rows), :],
+            other_ref[pl.ds(source, tok_rows), :],
+        )
+        key_block = joined_block[:, :head_dim]
+        value_block = joined_block[:, head_dim:]
         scores = jnp.dot(key_block, queries_t, preferred_element_type=jnp.float32) * score_scale
         grad_probs = jnp.dot(value_block, grads_t, preferred_element_type=jnp.float32)
         return start, key_block, scores, grad_probs
@@ -124,10 +131,11 @@
     out_grads = (weights[:, None] * cotangent.astype(jnp.float32)).astype(jnp.bfloat16)
 
     joined = jnp.concatenate([key_rows, value_rows], 1)
-    spread = jnp.broadcast_to(joined[None], (ctx_count,) + joined.shape)
-    gathered = lax.all_to_all(spread, ("chip", "core"), 0, 0, tiled=True).reshape(length, 2 * head_dim)
-    key_piece = gathered[:, :head_dim]
-    value_piece = gathered[:, head_dim:]
+    spread = jnp.broadcast_to(joined[None], (chip_count,) + joined.shape)
+    mine = lax.all_to_all(spread, "chip", 0, 0, tiled=True)
+    other = lax.ppermute(mine, "core", [(0, 1), (1, 0)])
+    mine = mine.reshape(chip_count * tok_rows, 2 * head_dim)
+    other = other.reshape(chip_count * tok_rows, 2 * head_dim)
 
     rows = head_count * tok_rows
     vmem = pl.BlockSpec(memory_space=pltpu.MemorySpace.VMEM)
@@ -145,7 +153,7 @@
         ),
         in_specs=[smem, vmem, vmem, vmem, vmem],
         out_specs=(vmem, vmem, vmem, vmem),
-    )(my_index.reshape(1).astype(jnp.int32), queries, out_grads, key_piece, value_piece)
+    )(jnp.stack([my_index, core]).astype(jnp.int32), queries, out_grads, mine, other)
     log_totals = stacked_lse.reshape(head_count, tok_rows).T
 
     chip_rows = 2 * tok_rows

time: 91 us -> 80.5 us (0.88)
  waiting for transfers between devices: 23 us -> 17.2 us
  blocking collectives: 44.7 us -> 41.8 us
  local copies, waits for them, and re-layouts: 4.01 us -> 2.24 us
    all_to_all x1, waiting for transfers between devices: 20.7 us -> 13.9 us  [body(): mine = lax.all_to_all(spread, 'chip', 0, 0, tiled=True)]
    all_to_all x1, blocking collectives: 44.7 us -> 41.8 us  [body(): lax.all_to_all(own_part, 'chip', 0, 0, tiled=True)]
    slice x1 -> x0, local copies, waits for them, and re-layouts: 1.06 us -> none  [body(): value_piece = gathered[:, head_dim:]]
    ppermute x0 -> x1, waiting for transfers between devices: none -> 1 us  [body(): other = lax.ppermute(mine, 'core', [(0, 1), (1, 0)])]
    unnamed x10 -> x14, local copies, waits for them, and re-layouts: 1.88 us -> 1.41 us
  transfers between devices with their start and end apart: 3 -> 4, of which waited for: 2 -> 3; matrix products, arithmetic and copies ran while one was open for 2% -> 3% of each run, Pallas kernels for 0% -> 0%
where the time goes in v5:
time: 80.5 us; the launch traced here: 80.1 us
  blocking collectives  41.8 us (52%)
  waiting for transfers between devices  17.2 us (21%)
  starting transfers between devices  8.59 us (11%)
  other arithmetic  5.39 us (7%)
  Pallas kernels  4.18 us (5%)
  local copies, waits for them, and re-layouts  2.24 us (3%)
    all_to_all x1, blocking collectives, body(): lax.all_to_all(own_part, 'chip', 0, 0, tiled=True)  41.8 us
    all_to_all x1, waiting for transfers between devices, body(): mine = lax.all_to_all(spread, 'chip', 0, 0, tiled=True)  13.9 us
    all_to_all x1, starting transfers between devices, body(): mine = lax.all_to_all(spread, 'chip', 0, 0, tiled=True)  7.41 us
    pallas_call x1, Pallas kernels, body(): pl.pallas_call(kernel, out_shape=(jax.ShapeDtypeStruct((1, rows), jnp.flo...  4.18 us
    ppermute x1, waiting for transfers between devices, body(): lax.ppermute(jnp.where(lead, value_part, key_part), 'core', [(0, 1), (1,...  2.29 us
    select_n x1, other arithmetic, body(): jnp.where(lead, value_part, key_part)  1.68 us
  transfers between devices with their start and end apart: 4, of which 3 were waited for; matrix products, arithmetic and copies ran while one was open for 3% of the time, Pallas kernels for 0%

profile of v5, /device:TPU:0, one launch (start us, length us, event | category | flops | bytes accessed | tf_op | source)
XLA Modules:
  0.0 80.1 jit_solution(5687436851021725318)
XLA Ops:
  0.6 0.8 pad_maximum_fusion
  1.4 0.8 %broadcast_in_dim.24 = bf16[8,128,256]{2,1,0:T(8,128)(2,1)} broadcast(bf16[128,256]{1,0:T(8,128)(2,1)S(1)} %pad_maximum_fusion), dimensions={1,2} | broadcast | bytes 589824 | tf_op jit(solution)/shard_map/broadcast_in_dim | solution.py:134
  2.2 0.0 copy-start.2
  2.2 7.4 %all-to-all-start = ((bf16[8,128,256]{2,1,0:T(8,128)(2,1)}), bf16[8,128,256]{2,1,0:T(8,128)(2,1)S(1)}, u32[]{:S(2)}, u32[]{:S(2)}) async-start(bf16[8,128,256]{2,1,0:T(8,128)(2,1)} %broadcast_in_dim.24), calls=%async_computation | async-start | bytes 1048576 | tf_op jit(solution)/shard_map/all_to_all | solution.py:135
  9.7 0.0 copy-start.4
  9.7 0.0 copy-start.5
  9.7 0.6 pad_add_fusion.index_ref
  10.3 0.0 copy-start.6
  10.3 13.9 %all-to-all-done = bf16[8,128,256]{2,1,0:T(8,128)(2,1)S(1)} async-done(((bf16[8,128,256]{2,1,0:T(8,128)(2,1)}), bf16[8,128,256]{2,1,0:T(8,128)(2,1)S(1)}, u32[]{:S(2)}, u32[]{:S(2)}) %all-to-all-start) | async-done | bytes 524320 | tf_op jit(solution)/shard_map/all_to_all | solution.py:135
  24.1 0.0 collective-permute-start
  24.1 0.0 copy-done.4
  24.2 0.0 copy-done.5
  24.2 0.0 copy-done.6
  24.2 0.1 select_reduce_fusion
  24.3 0.0 copy-done.2
  24.3 0.8 multiply_convert_fusion.grad_ref
  25.1 1.0 %collective-permute-done = bf16[8,128,256]{2,1,0:T(8,128)(2,1)S(1)} collective-permute-done((bf16[8,128,256]{2,1,0:T(8,128)(2,1)S(1)}, bf16[8,128,256]{2,1,0:T(8,128)(2,1)S(1)}, u32[]{:S(2)}, u32[]{:S(2)}) %collective-permute-start) | collective-permute-done | bytes 524320 | tf_op jit(solution)/shard_map/ppermute | solution.py:136
  26.1 0.0 copy-done
  26.1 0.8 %copy-done.1 = bf16[8,128,256]{2,1,0:T(8,128)(2,1)} copy-done((bf16[8,128,256]{2,1,0:T(8,128)(2,1)}, bf16[8,128,256]{2,1,0:T(8,128)(2,1)S(1)}, u32[]{:S(2)}) %copy-start.1) | copy-done | bytes 524312
  26.9 4.2 %shard_map.102 = (f32[1,768]{1,0:T(1,128)}, f32[128,768]{1,0:T(8,128)}, f32[2048,128]{1,0:T(8,128)}, f32[2048,128]{1,0:T(8,128)}) custom-call(s32[2]{0:T(128)} %pad_add_fusion.index_ref, bf16[128,768]{1,0:T(8,128)(2,1)} %query_ref.1, bf16[128,768]{1,0:T(8,128)(2,1)} %multiply_convert_fusion.grad_ref, bf16[1024,256]{1,0:T(8,128)(2,1)} %bitcast.10, ...), custom_call_target="tpu_custom_call" | custom-call | tf_op jit(solution)/shard_map/pallas_call | solution.py:146
  31.1 1.7 %broadcast_select_fusion = (f32[2048,128]{1,0:T(8,128)S(1)}, f32[2048,128]{1,0:T(8,128)S(1)}) fusion(f32[2048,128]{1,0:T(8,128)} %get-tuple-element.11, f32[2048,128]{1,0:T(8,128)} %get-tuple-element.10, pred[]{:T(512)S(6)} %eq.19), kind=kLoop, calls=%fused_computation | loop fusion | flops 524288 | bytes 4194305 | tf_op jit(solution)/shard_map/jit(_where)/select_n | solution.py:163
  32.7 1.1 %collective-permute-start.1 = (f32[8,256,128]{2,1,0:T(8,128)S(1)}, f32[8,256,128]{2,1,0:T(8,128)S(1)}, u32[]{:S(2)}, u32[]{:S(2)}) collective-permute-start(f32[8,256,128]{2,1,0:T(8,128)S(1)} %bitcast.11), channel_id=1, source_target_pairs={{0,2},{2,0},{1,3},{3,1},{4,6},{6,4},{5,7},{7,5},{8,10},{10,8},{9,1... | collective-permute-start | bytes 3145736 | tf_op jit(solution)/shard_map/ppermute | solution.py:163
  33.8 2.3 %collective-permute-done.1 = f32[8,256,128]{2,1,0:T(8,128)S(1)} collective-permute-done((f32[8,256,128]{2,1,0:T(8,128)S(1)}, f32[8,256,128]{2,1,0:T(8,128)S(1)}, u32[]{:S(2)}, u32[]{:S(2)}) %collective-permute-start.1) | collective-permute-done | bytes 1048608 | tf_op jit(solution)/shard_map/ppermute | solution.py:163
  36.1 0.2 add.13
  36.3 41.8 %all_to_all.10 = f32[8,256,128]{2,1,0:T(8,128)S(1)} all-to-all(f32[8,256,128]{2,1,0:T(8,128)S(1)} %add.13), channel_id=1, replica_groups=mesh['chip'=8,'core'=2,'head'=2] {'chip'}, dimensions={0} | all-to-all | bytes 2097152 | tf_op jit(solution)/shard_map/all_to_all | solution.py:165
  78.1 0.1 reduce_sum.19
  78.2 0.0 copy-start.3
  78.2 0.1 collective-permute-start.2
  78.3 0.6 copy-done.3
  78.9 0.6 reduce
  79.5 0.0 collective-permute-done.2
  79.5 0.6 broadcast_select_fusion.2
  (4 shorter events, 0.0 us)
Async XLA Ops:
  2.2 22.0 %copy-start.2 = (bf16[128,768]{1,0:T(8,128)(2,1)S(1)}, bf16[128,768]{1,0:T(8,128)(2,1)}, u32[]{:S(2)}) copy-start(bf16[128,768]{1,0:T(8,128)(2,1)} %param.10) | copy-start | bytes 589828
  2.2 21.9 %all-to-all-start = ((bf16[8,128,256]{2,1,0:T(8,128)(2,1)}), bf16[8,128,256]{2,1,0:T(8,128)(2,1)S(1)}, u32[]{:S(2)}, u32[]{:S(2)}) async-start(bf16[8,128,256]{2,1,0:T(8,128)(2,1)} %broadcast_in_dim.24), calls=%async_computation | async-start | bytes 1048576 | tf_op jit(solution)/shard_map/all_to_all | solution.py:135
  9.7 14.5 %copy-start.4 = (s32[16]{0:T(128)S(1)}, s32[16]{0:T(128)}, u32[]{:S(2)}) copy-start(s32[16]{0:T(128)} %param.12) | copy-start | bytes 196
  9.7 14.5 %copy-start.5 = (s32[16]{0:T(128)S(1)}, s32[16]{0:T(128)}, u32[]{:S(2)}) copy-start(s32[16]{0:T(128)} %param.13) | copy-start | bytes 196
  10.3 13.9 %copy-start.6 = (s32[128]{0:T(128)S(1)}, s32[128]{0:T(128)}, u32[]{:S(2)}) copy-start(s32[128]{0:T(128)} %param.11) | copy-start | bytes 1540
  24.1 1.9 %copy-start = (bf16[8,128,256]{2,1,0:T(8,128)(2,1)}, bf16[8,128,256]{2,1,0:T(8,128)(2,1)S(1)}, u32[]{:S(2)}) copy-start(bf16[8,128,256]{2,1,0:T(8,128)(2,1)S(1)} %all-to-all-done) | copy-start | bytes 1572868
  24.1 1.9 %collective-permute-start = (bf16[8,128,256]{2,1,0:T(8,128)(2,1)S(1)}, bf16[8,128,256]{2,1,0:T(8,128)(2,1)S(1)}, u32[]{:S(2)}, u32[]{:S(2)}) collective-permute-start(bf16[8,128,256]{2,1,0:T(8,128)(2,1)S(1)} %all-to-all-done), channel_id=1, source_target_pairs={{0,2},{2,0},{1,3},{3,1},{4,6},{6,4},{5,7},{7,5},{8,10},{10,8},{9,1... | collective-permute-start | bytes 1572872 | tf_op jit(solution)/shard_map/ppermute | solution.py:136
  26.1 0.8 %copy-start.1 = (bf16[8,128,256]{2,1,0:T(8,128)(2,1)}, bf16[8,128,256]{2,1,0:T(8,128)(2,1)S(1)}, u32[]{:S(2)}) copy-start(bf16[8,128,256]{2,1,0:T(8,128)(2,1)S(1)} %collective-permute-done) | copy-start | bytes 1572868
  32.7 3.4 %collective-permute-start.1 = (f32[8,256,128]{2,1,0:T(8,128)S(1)}, f32[8,256,128]{2,1,0:T(8,128)S(1)}, u32[]{:S(2)}, u32[]{:S(2)}) collective-permute-start(f32[8,256,128]{2,1,0:T(8,128)S(1)} %bitcast.11), channel_id=1, source_target_pairs={{0,2},{2,0},{1,3},{3,1},{4,6},{6,4},{5,7},{7,5},{8,10},{10,8},{9,1... | collective-permute-start | bytes 3145736 | tf_op jit(solution)/shard_map/ppermute | solution.py:163
  78.2 0.7 copy-start.3
  78.2 1.3 %collective-permute-start.2 = (bf16[128,128]{1,0:T(8,128)(2,1)S(1)}, bf16[128,128]{1,0:T(8,128)(2,1)S(1)}, u32[]{:S(2)}, u32[]{:S(2)}) collective-permute-start(bf16[128,128]{1,0:T(8,128)(2,1)S(1)} %broadcast_select_fusion.4), channel_id=1, source_target_pairs={{0,2},{2,0},{1,3},{3,1},{4,6},{6,4},{5,7},{7,5},{8,10},{10,8},{9,1... | collective-permute-start | bytes 98312 | tf_op jit(solution)/shard_map/ppermute | solution.py:166

commit v6 on v5

--- a/solution.py
+++ b/solution.py
@@ -22,11 +22,13 @@
 
 def attention_kernel(
     index_ref, query_ref, grad_ref, mine_ref, other_ref,
-    lse_ref, dq_ref, dk_ref, dv_ref, *, heads, head_dim, tok_rows, score_scale,
+    lse_ref, dq_ref, dk_ref, dv_ref, *, heads, head_dim, tok_rows, score_scale, tile_blocks,
 ):
     index = index_ref[0]
     core = index_ref[1]
-    block_count = 2 * mine_ref.shape[0] // tok_rows
+    pair_rows = tile_blocks * tok_rows
+    pair_count = mine_ref.shape[0] * 2 // pair_rows
+    last = index // tile_blocks
     rows = heads * tok_rows
     queries = jnp.concatenate(
         [query_ref[:, h * head_dim:(h + 1) * head_dim] for h in range(heads)], 0
@@ -36,28 +38,29 @@
     )
     queries_t = queries.astype(jnp.float32).T.astype(jnp.bfloat16)
     grads_t = grads.astype(jnp.float32).T.astype(jnp.bfloat16)
-    key_tok = lax.broadcasted_iota(jnp.int32, (tok_rows, rows), 0)
-    row_tok = lax.rem(lax.broadcasted_iota(jnp.int32, (tok_rows, rows), 1), tok_rows)
-    visible = key_tok <= row_tok
+    key_tok = lax.broadcasted_iota(jnp.int32, (pair_rows, rows), 0)
+    row_tok = lax.rem(lax.broadcasted_iota(jnp.int32, (pair_rows, rows), 1), tok_rows)
+    visible = key_tok <= row_tok + (index - tile_blocks * last) * tok_rows
     contract_first = (((0,), (0,)), ((), ()))
+    lead = core == 0
 
-    def blocks_of(block):
-        start = pl.multiple_of(block * tok_rows, tok_rows)
-        source = pl.multiple_of((block // 2) * tok_rows, tok_rows)
-        joined_block = jnp.where(
-            block % 2 == core,
-            mine_ref[pl.ds(source, tok_rows), :],
-            other_ref[pl.ds(source, tok_rows), :],
-        )
-        key_block = joined_block[:, :head_dim]
-        value_block = joined_block[:, head_dim:]
+    def blocks_of(pair):
+        parts = []
+        for chip in range(tile_blocks // 2):
+            source = pl.multiple_of((pair * (tile_blocks // 2) + chip) * tok_rows, tok_rows)
+            own = mine_ref[pl.ds(source, tok_rows), :]
+            partner = other_ref[pl.ds(source, tok_rows), :]
+            parts += [jnp.where(lead, own, partner), jnp.where(lead, partner, own)]
+        joined = jnp.concatenate(parts, 0)
+        key_block = joined[:, :head_dim]
+        value_block = joined[:, head_dim:]
         scores = jnp.dot(key_block, queries_t, preferred_element_type=jnp.float32) * score_scale
         grad_probs = jnp.dot(value_block, grads_t, preferred_element_type=jnp.float32)
-        return start, key_block, scores, grad_probs
+        return pl.multiple_of(pair * pair_rows, pair_rows), key_block, scores, grad_probs
 
-    def forward(block, carry, masked):
+    def forward(pair, carry, masked):
         peak, total, weighted = carry
-        _, _, scores, grad_probs = blocks_of(block)
+        _, _, scores, grad_probs = blocks_of(pair)
         if masked:
             scores = jnp.where(visible, scores, -1e30)
         new_peak = jnp.maximum(peak, jnp.max(scores, axis=0, keepdims=True))
@@ -74,14 +77,14 @@
         jnp.zeros((1, rows), jnp.float32),
         jnp.zeros((1, rows), jnp.float32),
     )
-    carry = lax.fori_loop(0, index, lambda b, c: forward(b, c, False), start_carry)
-    peak, total, weighted = forward(index, carry, True)
+    carry = lax.fori_loop(0, last, lambda b, c: forward(b, c, False), start_carry)
+    peak, total, weighted = forward(last, carry, True)
     log_totals = peak + jnp.log(total)
     delta_rows = weighted / total
     lse_ref[...] = log_totals
 
-    def backward(block, grad_query_t, masked):
-        start, key_block, scores, grad_probs = blocks_of(block)
+    def backward(pair, grad_query_t, masked):
+        start, key_block, scores, grad_probs = blocks_of(pair)
         probabilities = jnp.exp(scores - log_totals)
         if masked:
             probabilities = jnp.where(visible, probabilities, 0.0)
@@ -92,24 +95,24 @@
         )
         key_add = jnp.dot(grad_scores, queries, preferred_element_type=jnp.float32)
         value_add = jnp.dot(prob_bf16, grads, preferred_element_type=jnp.float32)
-        dk_ref[pl.ds(start, tok_rows), :] = key_add * score_scale
-        dv_ref[pl.ds(start, tok_rows), :] = value_add
+        dk_ref[pl.ds(start, pair_rows), :] = key_add * score_scale
+        dv_ref[pl.ds(start, pair_rows), :] = value_add
         return grad_query_t
 
     grad_query_t = lax.fori_loop(
-        0, index, lambda b, g: backward(b, g, False), jnp.zeros((head_dim, rows), jnp.float32)
+        0, last, lambda b, g: backward(b, g, False), jnp.zeros((head_dim, rows), jnp.float32)
     )
-    grad_query = (backward(index, grad_query_t, True) * score_scale).T
+    grad_query = (backward(last, grad_query_t, True) * score_scale).T
     for h in range(heads):
         dq_ref[:, h * head_dim:(h + 1) * head_dim] = grad_query[h * tok_rows:(h + 1) * tok_rows]
 
-    def clear(block, unused):
-        start = pl.multiple_of(block * tok_rows, tok_rows)
-        dk_ref[pl.ds(start, tok_rows), :] = jnp.zeros((tok_rows, head_dim), jnp.float32)
-        dv_ref[pl.ds(start, tok_rows), :] = jnp.zeros((tok_rows, head_dim), jnp.float32)
+    def clear(pair, unused):
+        start = pl.multiple_of(pair * pair_rows, pair_rows)
+        dk_ref[pl.ds(start, pair_rows), :] = jnp.zeros((pair_rows, head_dim), jnp.float32)
+        dv_ref[pl.ds(start, pair_rows), :] = jnp.zeros((pair_rows, head_dim), jnp.float32)
         return unused
 
-    lax.fori_loop(index + 1, block_count, clear, 0)
+    lax.fori_loop(last + 1, pair_count, clear, 0)
 
 
 def body(queries, key_rows, value_rows, cotangent, trace_ids, correct, group_size):
@@ -141,7 +144,8 @@
     vmem = pl.BlockSpec(memory_space=pltpu.MemorySpace.VMEM)
     smem = pl.BlockSpec(memory_space=pltpu.MemorySpace.SMEM)
     kernel = functools.partial(
-        attention_kernel, heads=head_count, head_dim=head_dim, tok_rows=tok_rows, score_scale=score_scale
+        attention_kernel, heads=head_count, head_dim=head_dim, tok_rows=tok_rows,
+        score_scale=score_scale, tile_blocks=math.gcd(ctx_count, 4),
     )
     stacked_lse, query_grads, key_part, value_part = pl.pallas_call(
         kernel,

time: 80.5 us -> 74.5 us (0.925)
  blocking collectives: 41.8 us -> 35.2 us
  Pallas kernels: 4.18 us -> 5.49 us
  starting transfers between devices: 8.59 us -> 7.67 us
    all_to_all x1, blocking collectives: 41.8 us -> 35.2 us  [body(): lax.all_to_all(own_part, 'chip', 0, 0, tiled=True)]
    pallas_call x1, Pallas kernels: 4.18 us -> 5.49 us  [body(): pl.pallas_call(kernel, out_shape=(jax.ShapeDtypeStruct((1, rows), jnp.flo...]
    ppermute x1, starting transfers between devices: 1.11 us -> 0.19 us  [body(): lax.ppermute(jnp.where(lead, value_part, key_part), 'core', [(0, 1), (1,...]
where the time goes in v6:
time: 74.5 us; the launch traced here: 74.1 us
  blocking collectives  35.2 us (47%)
  waiting for transfers between devices  17.4 us (23%)
  starting transfers between devices  7.67 us (10%)
  Pallas kernels  5.49 us (7%)
  other arithmetic  5.39 us (7%)
  local copies, waits for them, and re-layouts  2.24 us (3%)
    all_to_all x1, blocking collectives, body(): lax.all_to_all(own_part, 'chip', 0, 0, tiled=True)  35.2 us
    all_to_all x1, waiting for transfers between devices, body(): mine = lax.all_to_all(spread, 'chip', 0, 0, tiled=True)  13.9 us
    all_to_all x1, starting transfers between devices, body(): mine = lax.all_to_all(spread, 'chip', 0, 0, tiled=True)  7.41 us
    pallas_call x1, Pallas kernels, body(): pl.pallas_call(kernel, out_shape=(jax.ShapeDtypeStruct((1, rows), jnp.flo...  5.49 us
    ppermute x1, waiting for transfers between devices, body(): lax.ppermute(jnp.where(lead, value_part, key_part), 'core', [(0, 1), (1,...  2.54 us
    select_n x1, other arithmetic, body(): jnp.where(lead, value_part, key_part)  1.68 us
  transfers between devices with their start and end apart: 4, of which 3 were waited for; matrix products, arithmetic and copies ran while one was open for 3% of the time, Pallas kernels for 0%

profile of v6, /device:TPU:0, one launch (start us, length us, event | category | flops | bytes accessed | tf_op | source)
XLA Modules:
  0.0 74.1 jit_solution(5443716218590415672)
XLA Ops:
  0.6 0.8 %pad_maximum_fusion = bf16[128,256]{1,0:T(8,128)(2,1)S(1)} fusion(bf16[128,128]{1,0:T(8,128)(2,1)} %param.9, bf16[128,128]{1,0:T(8,128)(2,1)} %param.8), kind=kLoop, calls=%fused_computation.3 | loop fusion | flops 131072 | bytes 131072 | tf_op jit(solution)/shard_map/concatenate | solution.py:136
  1.4 0.8 %broadcast_in_dim.24 = bf16[8,128,256]{2,1,0:T(8,128)(2,1)} broadcast(bf16[128,256]{1,0:T(8,128)(2,1)S(1)} %pad_maximum_fusion), dimensions={1,2} | broadcast | bytes 589824 | tf_op jit(solution)/shard_map/broadcast_in_dim | solution.py:137
  2.2 0.0 copy-start.2
  2.2 7.4 %all-to-all-start = ((bf16[8,128,256]{2,1,0:T(8,128)(2,1)}), bf16[8,128,256]{2,1,0:T(8,128)(2,1)S(1)}, u32[]{:S(2)}, u32[]{:S(2)}) async-start(bf16[8,128,256]{2,1,0:T(8,128)(2,1)} %broadcast_in_dim.24), calls=%async_computation | async-start | bytes 1048576 | tf_op jit(solution)/shard_map/all_to_all | solution.py:138
  9.7 0.0 copy-start.4
  9.7 0.0 copy-start.5
  9.7 0.6 pad_add_fusion.index_ref
  10.3 0.0 copy-start.6
  10.3 13.9 %all-to-all-done = bf16[8,128,256]{2,1,0:T(8,128)(2,1)S(1)} async-done(((bf16[8,128,256]{2,1,0:T(8,128)(2,1)}), bf16[8,128,256]{2,1,0:T(8,128)(2,1)S(1)}, u32[]{:S(2)}, u32[]{:S(2)}) %all-to-all-start) | async-done | bytes 524320 | tf_op jit(solution)/shard_map/all_to_all | solution.py:138
  24.1 0.0 collective-permute-start
  24.1 0.0 copy-done.4
  24.2 0.0 copy-done.5
  24.2 0.0 copy-done.6
  24.2 0.1 select_reduce_fusion
  24.3 0.0 copy-done.2
  24.3 0.8 %multiply_convert_fusion.grad_ref = bf16[128,768]{1,0:T(8,128)(2,1)} fusion(bf16[128,768]{1,0:T(8,128)(2,1)S(1)} %copy-done.2, f32[128]{0:T(128)S(1)} %select_reduce_fusion), kind=kLoop, calls=%fused_computation.2 | loop fusion | flops 294912 | bytes 393728 | tf_op jit(solution)/shard_map/convert_element_type | solution.py:134
  25.1 1.0 %collective-permute-done = bf16[8,128,256]{2,1,0:T(8,128)(2,1)S(1)} collective-permute-done((bf16[8,128,256]{2,1,0:T(8,128)(2,1)S(1)}, bf16[8,128,256]{2,1,0:T(8,128)(2,1)S(1)}, u32[]{:S(2)}, u32[]{:S(2)}) %collective-permute-start) | collective-permute-done | bytes 524320 | tf_op jit(solution)/shard_map/ppermute | solution.py:139
  26.1 0.0 copy-done
  26.1 0.8 %copy-done.1 = bf16[8,128,256]{2,1,0:T(8,128)(2,1)} copy-done((bf16[8,128,256]{2,1,0:T(8,128)(2,1)}, bf16[8,128,256]{2,1,0:T(8,128)(2,1)S(1)}, u32[]{:S(2)}) %copy-start.1) | copy-done | bytes 524312
  26.9 5.5 %shard_map.102 = (f32[1,768]{1,0:T(1,128)}, f32[128,768]{1,0:T(8,128)}, f32[2048,128]{1,0:T(8,128)}, f32[2048,128]{1,0:T(8,128)}) custom-call(s32[2]{0:T(128)} %pad_add_fusion.index_ref, bf16[128,768]{1,0:T(8,128)(2,1)} %query_ref.1, bf16[128,768]{1,0:T(8,128)(2,1)} %multiply_convert_fusion.grad_ref, bf16[1024,256]{1,0:T(8,128)(2,1)} %bitcast.10, ...), custom_call_target="tpu_custom_call" | custom-call | tf_op jit(solution)/shard_map/pallas_call | solution.py:150
  32.4 1.7 %broadcast_select_fusion = (f32[2048,128]{1,0:T(8,128)S(1)}, f32[2048,128]{1,0:T(8,128)S(1)}) fusion(f32[2048,128]{1,0:T(8,128)} %get-tuple-element.11, f32[2048,128]{1,0:T(8,128)} %get-tuple-element.10, pred[]{:T(512)S(6)} %eq.19), kind=kLoop, calls=%fused_computation | loop fusion | flops 524288 | bytes 4194305 | tf_op jit(solution)/shard_map/jit(_where)/select_n | solution.py:167
  34.0 0.2 collective-permute-start.1
  34.2 2.5 %collective-permute-done.1 = f32[8,256,128]{2,1,0:T(8,128)S(1)} collective-permute-done((f32[8,256,128]{2,1,0:T(8,128)S(1)}, f32[8,256,128]{2,1,0:T(8,128)S(1)}, u32[]{:S(2)}, u32[]{:S(2)}) %collective-permute-start.1) | collective-permute-done | bytes 1048608 | tf_op jit(solution)/shard_map/ppermute | solution.py:167
  36.8 0.2 add.13
  36.9 35.2 %all_to_all.10 = f32[8,256,128]{2,1,0:T(8,128)S(1)} all-to-all(f32[8,256,128]{2,1,0:T(8,128)S(1)} %add.13), channel_id=1, replica_groups=mesh['chip'=8,'core'=2,'head'=2] {'chip'}, dimensions={0} | all-to-all | bytes 2097152 | tf_op jit(solution)/shard_map/all_to_all | solution.py:169
  72.1 0.1 reduce_sum.19
  72.2 0.0 copy-start.3
  72.2 0.1 collective-permute-start.2
  72.3 0.6 copy-done.3
  72.9 0.6 reduce
  73.5 0.0 collective-permute-done.2
  73.5 0.6 broadcast_select_fusion.2
  (4 shorter events, 0.0 us)
Async XLA Ops:
  2.2 22.0 %copy-start.2 = (bf16[128,768]{1,0:T(8,128)(2,1)S(1)}, bf16[128,768]{1,0:T(8,128)(2,1)}, u32[]{:S(2)}) copy-start(bf16[128,768]{1,0:T(8,128)(2,1)} %param.10) | copy-start | bytes 589828
  2.2 21.9 %all-to-all-start = ((bf16[8,128,256]{2,1,0:T(8,128)(2,1)}), bf16[8,128,256]{2,1,0:T(8,128)(2,1)S(1)}, u32[]{:S(2)}, u32[]{:S(2)}) async-start(bf16[8,128,256]{2,1,0:T(8,128)(2,1)} %broadcast_in_dim.24), calls=%async_computation | async-start | bytes 1048576 | tf_op jit(solution)/shard_map/all_to_all | solution.py:138
  9.7 14.5 %copy-start.4 = (s32[16]{0:T(128)S(1)}, s32[16]{0:T(128)}, u32[]{:S(2)}) copy-start(s32[16]{0:T(128)} %param.12) | copy-start | bytes 196
  9.7 14.5 %copy-start.5 = (s32[16]{0:T(128)S(1)}, s32[16]{0:T(128)}, u32[]{:S(2)}) copy-start(s32[16]{0:T(128)} %param.13) | copy-start | bytes 196
  10.3 13.9 %copy-start.6 = (s32[128]{0:T(128)S(1)}, s32[128]{0:T(128)}, u32[]{:S(2)}) copy-start(s32[128]{0:T(128)} %param.11) | copy-start | bytes 1540
  24.1 1.9 %copy-start = (bf16[8,128,256]{2,1,0:T(8,128)(2,1)}, bf16[8,128,256]{2,1,0:T(8,128)(2,1)S(1)}, u32[]{:S(2)}) copy-start(bf16[8,128,256]{2,1,0:T(8,128)(2,1)S(1)} %all-to-all-done) | copy-start | bytes 1572868
  24.1 1.9 %collective-permute-start = (bf16[8,128,256]{2,1,0:T(8,128)(2,1)S(1)}, bf16[8,128,256]{2,1,0:T(8,128)(2,1)S(1)}, u32[]{:S(2)}, u32[]{:S(2)}) collective-permute-start(bf16[8,128,256]{2,1,0:T(8,128)(2,1)S(1)} %all-to-all-done), channel_id=1, source_target_pairs={{0,2},{2,0},{1,3},{3,1},{4,6},{6,4},{5,7},{7,5},{8,10},{10,8},{9,1... | collective-permute-start | bytes 1572872 | tf_op jit(solution)/shard_map/ppermute | solution.py:139
  26.1 0.8 %copy-start.1 = (bf16[8,128,256]{2,1,0:T(8,128)(2,1)}, bf16[8,128,256]{2,1,0:T(8,128)(2,1)S(1)}, u32[]{:S(2)}) copy-start(bf16[8,128,256]{2,1,0:T(8,128)(2,1)S(1)} %collective-permute-done) | copy-start | bytes 1572868
  34.0 2.7 %collective-permute-start.1 = (f32[8,256,128]{2,1,0:T(8,128)S(1)}, f32[8,256,128]{2,1,0:T(8,128)S(1)}, u32[]{:S(2)}, u32[]{:S(2)}) collective-permute-start(f32[8,256,128]{2,1,0:T(8,128)S(1)} %bitcast.11), channel_id=1, source_target_pairs={{0,2},{2,0},{1,3},{3,1},{4,6},{6,4},{5,7},{7,5},{8,10},{10,8},{9,1... | collective-permute-start | bytes 3145736 | tf_op jit(solution)/shard_map/ppermute | solution.py:167
  72.2 0.7 copy-start.3
  72.2 1.3 %collective-permute-start.2 = (bf16[128,128]{1,0:T(8,128)(2,1)S(1)}, bf16[128,128]{1,0:T(8,128)(2,1)S(1)}, u32[]{:S(2)}, u32[]{:S(2)}) collective-permute-start(bf16[128,128]{1,0:T(8,128)(2,1)S(1)} %broadcast_select_fusion.4), channel_id=1, source_target_pairs={{0,2},{2,0},{1,3},{3,1},{4,6},{6,4},{5,7},{7,5},{8,10},{10,8},{9,1... | collective-permute-start | bytes 98312 | tf_op jit(solution)/shard_map/ppermute | solution.py:170

commit v7 on v6

--- a/solution.py
+++ b/solution.py
@@ -145,7 +145,7 @@
     smem = pl.BlockSpec(memory_space=pltpu.MemorySpace.SMEM)
     kernel = functools.partial(
         attention_kernel, heads=head_count, head_dim=head_dim, tok_rows=tok_rows,
-        score_scale=score_scale, tile_blocks=math.gcd(ctx_count, 4),
+        score_scale=score_scale, tile_blocks=math.gcd(ctx_count, 8),
     )
     stacked_lse, query_grads, key_part, value_part = pl.pallas_call(
         kernel,

time: 74.5 us -> 73.9 us (level)
  blocking collectives: 35.2 us -> 32.8 us
  Pallas kernels: 5.49 us -> 7.33 us
    all_to_all x1, blocking collectives: 35.2 us -> 32.8 us  [body(): lax.all_to_all(own_part, 'chip', 0, 0, tiled=True)]
    pallas_call x1, Pallas kernels: 5.49 us -> 7.33 us  [body(): pl.pallas_call(kernel, out_shape=(jax.ShapeDtypeStruct((1, rows), jnp.flo...]
where the time goes in v7:
time: 73.9 us; the launch traced here: 73.5 us
  blocking collectives  32.8 us (44%)
  waiting for transfers between devices  17.4 us (24%)
  starting transfers between devices  7.69 us (10%)
  Pallas kernels  7.33 us (10%)
  other arithmetic  5.39 us (7%)
  local copies, waits for them, and re-layouts  2.24 us (3%)
    all_to_all x1, blocking collectives, body(): lax.all_to_all(own_part, 'chip', 0, 0, tiled=True)  32.8 us
    all_to_all x1, waiting for transfers between devices, body(): mine = lax.all_to_all(spread, 'chip', 0, 0, tiled=True)  13.9 us
    all_to_all x1, starting transfers between devices, body(): mine = lax.all_to_all(spread, 'chip', 0, 0, tiled=True)  7.41 us
    pallas_call x1, Pallas kernels, body(): pl.pallas_call(kernel, out_shape=(jax.ShapeDtypeStruct((1, rows), jnp.flo...  7.33 us
    ppermute x1, waiting for transfers between devices, body(): lax.ppermute(jnp.where(lead, value_part, key_part), 'core', [(0, 1), (1,...  2.52 us
    select_n x1, other arithmetic, body(): jnp.where(lead, value_part, key_part)  1.68 us
  transfers between devices with their start and end apart: 4, of which 3 were waited for; matrix products, arithmetic and copies ran while one was open for 3% of the time, Pallas kernels for 0%

profile of v7, /device:TPU:0, one launch (start us, length us, event | category | flops | bytes accessed | tf_op | source)
XLA Modules:
  0.0 73.5 jit_solution(10246063305769725817)
XLA Ops:
  0.6 0.8 %pad_maximum_fusion = bf16[128,256]{1,0:T(8,128)(2,1)S(1)} fusion(bf16[128,128]{1,0:T(8,128)(2,1)} %param.9, bf16[128,128]{1,0:T(8,128)(2,1)} %param.8), kind=kLoop, calls=%fused_computation.3 | loop fusion | flops 131072 | bytes 131072 | tf_op jit(solution)/shard_map/concatenate | solution.py:136
  1.4 0.8 %broadcast_in_dim.24 = bf16[8,128,256]{2,1,0:T(8,128)(2,1)} broadcast(bf16[128,256]{1,0:T(8,128)(2,1)S(1)} %pad_maximum_fusion), dimensions={1,2} | broadcast | bytes 589824 | tf_op jit(solution)/shard_map/broadcast_in_dim | solution.py:137
  2.2 0.0 copy-start.2
  2.2 7.4 %all-to-all-start = ((bf16[8,128,256]{2,1,0:T(8,128)(2,1)}), bf16[8,128,256]{2,1,0:T(8,128)(2,1)S(1)}, u32[]{:S(2)}, u32[]{:S(2)}) async-start(bf16[8,128,256]{2,1,0:T(8,128)(2,1)} %broadcast_in_dim.24), calls=%async_computation | async-start | bytes 1048576 | tf_op jit(solution)/shard_map/all_to_all | solution.py:138
  9.7 0.0 copy-start.4
  9.7 0.0 copy-start.5
  9.7 0.6 pad_add_fusion.index_ref
  10.3 0.0 copy-start.6
  10.3 13.9 %all-to-all-done = bf16[8,128,256]{2,1,0:T(8,128)(2,1)S(1)} async-done(((bf16[8,128,256]{2,1,0:T(8,128)(2,1)}), bf16[8,128,256]{2,1,0:T(8,128)(2,1)S(1)}, u32[]{:S(2)}, u32[]{:S(2)}) %all-to-all-start) | async-done | bytes 524320 | tf_op jit(solution)/shard_map/all_to_all | solution.py:138
  24.1 0.0 collective-permute-start
  24.1 0.0 copy-done.4
  24.2 0.0 copy-done.5
  24.2 0.0 copy-done.6
  24.2 0.1 select_reduce_fusion
  24.3 0.0 copy-done.2
  24.3 0.8 %multiply_convert_fusion.grad_ref = bf16[128,768]{1,0:T(8,128)(2,1)} fusion(bf16[128,768]{1,0:T(8,128)(2,1)S(1)} %copy-done.2, f32[128]{0:T(128)S(1)} %select_reduce_fusion), kind=kLoop, calls=%fused_computation.2 | loop fusion | flops 294912 | bytes 393728 | tf_op jit(solution)/shard_map/convert_element_type | solution.py:134
  25.1 1.0 %collective-permute-done = bf16[8,128,256]{2,1,0:T(8,128)(2,1)S(1)} collective-permute-done((bf16[8,128,256]{2,1,0:T(8,128)(2,1)S(1)}, bf16[8,128,256]{2,1,0:T(8,128)(2,1)S(1)}, u32[]{:S(2)}, u32[]{:S(2)}) %collective-permute-start) | collective-permute-done | bytes 524320 | tf_op jit(solution)/shard_map/ppermute | solution.py:139
  26.1 0.0 copy-done
  26.1 0.8 %copy-done.1 = bf16[8,128,256]{2,1,0:T(8,128)(2,1)} copy-done((bf16[8,128,256]{2,1,0:T(8,128)(2,1)}, bf16[8,128,256]{2,1,0:T(8,128)(2,1)S(1)}, u32[]{:S(2)}) %copy-start.1) | copy-done | bytes 524312
  26.9 7.3 %shard_map.102 = (f32[1,768]{1,0:T(1,128)}, f32[128,768]{1,0:T(8,128)}, f32[2048,128]{1,0:T(8,128)}, f32[2048,128]{1,0:T(8,128)}) custom-call(s32[2]{0:T(128)} %pad_add_fusion.index_ref, bf16[128,768]{1,0:T(8,128)(2,1)} %query_ref.1, bf16[128,768]{1,0:T(8,128)(2,1)} %multiply_convert_fusion.grad_ref, bf16[1024,256]{1,0:T(8,128)(2,1)} %bitcast.10, ...), custom_call_target="tpu_custom_call" | custom-call | tf_op jit(solution)/shard_map/pallas_call | solution.py:150
  34.2 1.7 %broadcast_select_fusion = (f32[2048,128]{1,0:T(8,128)S(1)}, f32[2048,128]{1,0:T(8,128)S(1)}) fusion(f32[2048,128]{1,0:T(8,128)} %get-tuple-element.11, f32[2048,128]{1,0:T(8,128)} %get-tuple-element.10, pred[]{:T(512)S(6)} %eq.19), kind=kLoop, calls=%fused_computation | loop fusion | flops 524288 | bytes 4194305 | tf_op jit(solution)/shard_map/jit(_where)/select_n | solution.py:167
  35.9 0.2 collective-permute-start.1
  36.1 2.5 %collective-permute-done.1 = f32[8,256,128]{2,1,0:T(8,128)S(1)} collective-permute-done((f32[8,256,128]{2,1,0:T(8,128)S(1)}, f32[8,256,128]{2,1,0:T(8,128)S(1)}, u32[]{:S(2)}, u32[]{:S(2)}) %collective-permute-start.1) | collective-permute-done | bytes 1048608 | tf_op jit(solution)/shard_map/ppermute | solution.py:167
  38.6 0.2 add.13
  38.8 32.8 %all_to_all.10 = f32[8,256,128]{2,1,0:T(8,128)S(1)} all-to-all(f32[8,256,128]{2,1,0:T(8,128)S(1)} %add.13), channel_id=1, replica_groups=mesh['chip'=8,'core'=2,'head'=2] {'chip'}, dimensions={0} | all-to-all | bytes 2097152 | tf_op jit(solution)/shard_map/all_to_all | solution.py:169
  71.5 0.1 reduce_sum.19
  71.6 0.0 copy-start.3
  71.6 0.1 collective-permute-start.2
  71.7 0.6 copy-done.3
  72.3 0.6 reduce
  72.9 0.0 collective-permute-done.2
  72.9 0.6 broadcast_select_fusion.2
  (4 shorter events, 0.0 us)
Async XLA Ops:
  2.2 22.0 %copy-start.2 = (bf16[128,768]{1,0:T(8,128)(2,1)S(1)}, bf16[128,768]{1,0:T(8,128)(2,1)}, u32[]{:S(2)}) copy-start(bf16[128,768]{1,0:T(8,128)(2,1)} %param.10) | copy-start | bytes 589828
  2.2 21.9 %all-to-all-start = ((bf16[8,128,256]{2,1,0:T(8,128)(2,1)}), bf16[8,128,256]{2,1,0:T(8,128)(2,1)S(1)}, u32[]{:S(2)}, u32[]{:S(2)}) async-start(bf16[8,128,256]{2,1,0:T(8,128)(2,1)} %broadcast_in_dim.24), calls=%async_computation | async-start | bytes 1048576 | tf_op jit(solution)/shard_map/all_to_all | solution.py:138
  9.7 14.5 %copy-start.4 = (s32[16]{0:T(128)S(1)}, s32[16]{0:T(128)}, u32[]{:S(2)}) copy-start(s32[16]{0:T(128)} %param.12) | copy-start | bytes 196
  9.7 14.5 %copy-start.5 = (s32[16]{0:T(128)S(1)}, s32[16]{0:T(128)}, u32[]{:S(2)}) copy-start(s32[16]{0:T(128)} %param.13) | copy-start | bytes 196
  10.3 13.9 %copy-start.6 = (s32[128]{0:T(128)S(1)}, s32[128]{0:T(128)}, u32[]{:S(2)}) copy-start(s32[128]{0:T(128)} %param.11) | copy-start | bytes 1540
  24.1 1.9 %copy-start = (bf16[8,128,256]{2,1,0:T(8,128)(2,1)}, bf16[8,128,256]{2,1,0:T(8,128)(2,1)S(1)}, u32[]{:S(2)}) copy-start(bf16[8,128,256]{2,1,0:T(8,128)(2,1)S(1)} %all-to-all-done) | copy-start | bytes 1572868
  24.1 1.9 %collective-permute-start = (bf16[8,128,256]{2,1,0:T(8,128)(2,1)S(1)}, bf16[8,128,256]{2,1,0:T(8,128)(2,1)S(1)}, u32[]{:S(2)}, u32[]{:S(2)}) collective-permute-start(bf16[8,128,256]{2,1,0:T(8,128)(2,1)S(1)} %all-to-all-done), channel_id=1, source_target_pairs={{0,2},{2,0},{1,3},{3,1},{4,6},{6,4},{5,7},{7,5},{8,10},{10,8},{9,1... | collective-permute-start | bytes 1572872 | tf_op jit(solution)/shard_map/ppermute | solution.py:139
  26.1 0.8 %copy-start.1 = (bf16[8,128,256]{2,1,0:T(8,128)(2,1)}, bf16[8,128,256]{2,1,0:T(8,128)(2,1)S(1)}, u32[]{:S(2)}) copy-start(bf16[8,128,256]{2,1,0:T(8,128)(2,1)S(1)} %collective-permute-done) | copy-start | bytes 1572868
  35.9 2.7 %collective-permute-start.1 = (f32[8,256,128]{2,1,0:T(8,128)S(1)}, f32[8,256,128]{2,1,0:T(8,128)S(1)}, u32[]{:S(2)}, u32[]{:S(2)}) collective-permute-start(f32[8,256,128]{2,1,0:T(8,128)S(1)} %bitcast.11), channel_id=1, source_target_pairs={{0,2},{2,0},{1,3},{3,1},{4,6},{6,4},{5,7},{7,5},{8,10},{10,8},{9,1... | collective-permute-start | bytes 3145736 | tf_op jit(solution)/shard_map/ppermute | solution.py:167
  71.6 0.7 copy-start.3
  71.6 1.3 %collective-permute-start.2 = (bf16[128,128]{1,0:T(8,128)(2,1)S(1)}, bf16[128,128]{1,0:T(8,128)(2,1)S(1)}, u32[]{:S(2)}, u32[]{:S(2)}) collective-permute-start(bf16[128,128]{1,0:T(8,128)(2,1)S(1)} %broadcast_select_fusion.4), channel_id=1, source_target_pairs={{0,2},{2,0},{1,3},{3,1},{4,6},{6,4},{5,7},{7,5},{8,10},{10,8},{9,1... | collective-permute-start | bytes 98312 | tf_op jit(solution)/shard_map/ppermute | solution.py:170

commit v8 on v7

--- a/solution.py
+++ b/solution.py
@@ -22,7 +22,7 @@
 
 def attention_kernel(
     index_ref, query_ref, grad_ref, mine_ref, other_ref,
-    lse_ref, dq_ref, dk_ref, dv_ref, *, heads, head_dim, tok_rows, score_scale, tile_blocks,
+    lse_ref, dq_ref, keep_ref, send_ref, *, heads, head_dim, tok_rows, score_scale, tile_blocks,
 ):
     index = index_ref[0]
     core = index_ref[1]
@@ -95,8 +95,22 @@
         )
         key_add = jnp.dot(grad_scores, queries, preferred_element_type=jnp.float32)
         value_add = jnp.dot(prob_bf16, grads, preferred_element_type=jnp.float32)
-        dk_ref[pl.ds(start, pair_rows), :] = key_add * score_scale
-        dv_ref[pl.ds(start, pair_rows), :] = value_add
+        key_add = key_add * score_scale
+        for block in range(tile_blocks):
+            row = pl.multiple_of((pair * (tile_blocks // 2) + block // 2) * tok_rows, tok_rows)
+            part = slice(block * tok_rows, (block + 1) * tok_rows)
+            own_first = block % 2 == 0
+
+            @pl.when(lead == own_first)
+            def _():
+                keep_ref[pl.ds(row, tok_rows), :head_dim] = key_add[part]
+                keep_ref[pl.ds(row, tok_rows), head_dim:] = value_add[part]
+
+            @pl.when(lead != own_first)
+            def _():
+                send_ref[pl.ds(row, tok_rows), :head_dim] = key_add[part]
+                send_ref[pl.ds(row, tok_rows), head_dim:] = value_add[part]
+
         return grad_query_t
 
     grad_query_t = lax.fori_loop(
@@ -107,9 +121,10 @@
         dq_ref[:, h * head_dim:(h + 1) * head_dim] = grad_query[h * tok_rows:(h + 1) * tok_rows]
 
     def clear(pair, unused):
-        start = pl.multiple_of(pair * pair_rows, pair_rows)
-        dk_ref[pl.ds(start, pair_rows), :] = jnp.zeros((pair_rows, head_dim), jnp.float32)
-        dv_ref[pl.ds(start, pair_rows), :] = jnp.zeros((pair_rows, head_dim), jnp.float32)
+        half_rows = pair_rows // 2
+        start = pl.multiple_of(pair * half_rows, half_rows)
+        keep_ref[pl.ds(start, half_rows), :] = jnp.zeros((half_rows, 2 * head_dim), jnp.float32)
+        send_ref[pl.ds(start, half_rows), :] = jnp.zeros((half_rows, 2 * head_dim), jnp.float32)
         return unused
 
     lax.fori_loop(last + 1, pair_count, clear, 0)
@@ -147,31 +162,26 @@
         attention_kernel, heads=head_count, head_dim=head_dim, tok_rows=tok_rows,
         score_scale=score_scale, tile_blocks=math.gcd(ctx_count, 8),
     )
-    stacked_lse, query_grads, key_part, value_part = pl.pallas_call(
+    stacked_lse, query_grads, keep_part, send_part = pl.pallas_call(
         kernel,
         out_shape=(
             jax.ShapeDtypeStruct((1, rows), jnp.float32),
             jax.ShapeDtypeStruct((tok_rows, row_width), jnp.float32),
-            jax.ShapeDtypeStruct((length, head_dim), jnp.float32),
-            jax.ShapeDtypeStruct((length, head_dim), jnp.float32),
+            jax.ShapeDtypeStruct((chip_count * tok_rows, 2 * head_dim), jnp.float32),
+            jax.ShapeDtypeStruct((chip_count * tok_rows, 2 * head_dim), jnp.float32),
         ),
         in_specs=[smem, vmem, vmem, vmem, vmem],
         out_specs=(vmem, vmem, vmem, vmem),
     )(jnp.stack([my_index, core]).astype(jnp.int32), queries, out_grads, mine, other)
     log_totals = stacked_lse.reshape(head_count, tok_rows).T
 
-    chip_rows = 2 * tok_rows
-    key_part = key_part.reshape(chip_count, chip_rows, head_dim)
-    value_part = value_part.reshape(chip_count, chip_rows, head_dim)
-    lead = core == 0
-    swapped = lax.ppermute(jnp.where(lead, value_part, key_part), "core", [(0, 1), (1, 0)])
-    own_part = jnp.where(lead, key_part, value_part) + swapped
-    reduced = jnp.sum(lax.all_to_all(own_part, "chip", 0, 0, tiled=True), axis=0).astype(jnp.bfloat16)
-    other = lax.ppermute(
-        jnp.where(lead, reduced[tok_rows:], reduced[:tok_rows]), "core", [(0, 1), (1, 0)]
-    )
-    grad_keys = jnp.where(lead, reduced[:tok_rows], other)
-    grad_values = jnp.where(lead, other, reduced[tok_rows:])
+    own_part = keep_part + lax.ppermute(send_part, "core", [(0, 1), (1, 0)])
+    reduced = jnp.sum(
+        lax.all_to_all(own_part.reshape(chip_count, tok_rows, 2 * head_dim), "chip", 0, 0, tiled=True),
+        axis=0,
+    )
+    grad_keys = reduced[:, :head_dim].astype(jnp.bfloat16)
+    grad_values = reduced[:, head_dim:].astype(jnp.bfloat16)
     return (log_totals, query_grads, grad_keys, grad_values)
 
 

time: 73.9 us -> 74.1 us (level)
  blocking collectives: 32.8 us -> 0 us
  waiting for transfers between devices: 17.4 us -> 43.1 us
  starting transfers between devices: 7.69 us -> 14.8 us
    all_to_all x1 -> x0, blocking collectives: 32.8 us -> none  [body(): lax.all_to_all(own_part, 'chip', 0, 0, tiled=True)]
    all_to_all x0 -> x1, waiting for transfers between devices: none -> 25.5 us  [body(): lax.all_to_all(own_part.reshape(chip_count, tok_rows, 2 * head_dim), 'chi...]
    all_to_all x0 -> x1, starting transfers between devices: none -> 7.19 us  [body(): lax.all_to_all(own_part.reshape(chip_count, tok_rows, 2 * head_dim), 'chi...]
    select_n x3 -> x0, other arithmetic: 2.32 us -> none  [the longest x1 1.68 us: body(): jnp.where(lead, value_part, key_part)]
    add x1, other arithmetic: 0.16 us -> 2.4 us  [body(): own_part = keep_part + lax.ppermute(send_part, 'core', [(0, 1), (1, 0)])]
    ppermute x2 -> x1, waiting for transfers between devices: 2.53 us -> 2.73 us  [body(): own_part = keep_part + lax.ppermute(send_part, 'core', [(0, 1), (1, 0)])]
  transfers between devices with their start and end apart: 4 -> 4, of which waited for: 3 -> 4; matrix products, arithmetic and copies ran while one was open for 3% -> 3% of each run, Pallas kernels for 0% -> 0%
where the time goes in v8:
time: 74.1 us; the launch traced here: 73.7 us
  waiting for transfers between devices  43.1 us (58%)
  starting transfers between devices  14.8 us (20%)
  Pallas kernels  7.58 us (10%)
  other arithmetic  5.32 us (7%)
  local copies, waits for them, and re-layouts  2.29 us (3%)
    all_to_all x1, waiting for transfers between devices, body(): lax.all_to_all(own_part.reshape(chip_count, tok_rows, 2 * head_dim), 'chi...  25.5 us
    all_to_all x1, waiting for transfers between devices, body(): mine = lax.all_to_all(spread, 'chip', 0, 0, tiled=True)  13.9 us
    pallas_call x1, Pallas kernels, body(): pl.pallas_call(kernel, out_shape=(jax.ShapeDtypeStruct((1, rows), jnp.flo...  7.58 us
    all_to_all x1, starting transfers between devices, body(): mine = lax.all_to_all(spread, 'chip', 0, 0, tiled=True)  7.41 us
    all_to_all x1, starting transfers between devices, body(): lax.all_to_all(own_part.reshape(chip_count, tok_rows, 2 * head_dim), 'chi...  7.19 us
    ppermute x1, waiting for transfers between devices, body(): own_part = keep_part + lax.ppermute(send_part, 'core', [(0, 1), (1, 0)])  2.73 us
    add x1, other arithmetic, body(): own_part = keep_part + lax.ppermute(send_part, 'core', [(0, 1), (1, 0)])  2.4 us
  transfers between devices with their start and end apart: 4, of which 4 were waited for; matrix products, arithmetic and copies ran while one was open for 3% of the time, Pallas kernels for 0%

profile of v8, /device:TPU:0, one launch (start us, length us, event | category | flops | bytes accessed | tf_op | source)
XLA Modules:
  0.0 73.7 jit_solution(3888914395104704586)
XLA Ops:
  0.6 0.8 %pad_maximum_fusion = bf16[128,256]{1,0:T(8,128)(2,1)S(1)} fusion(bf16[128,128]{1,0:T(8,128)(2,1)} %param.9, bf16[128,128]{1,0:T(8,128)(2,1)} %param.8), kind=kLoop, calls=%fused_computation.1 | loop fusion | flops 131072 | bytes 131072 | tf_op jit(solution)/shard_map/concatenate | solution.py:151
  1.4 0.8 %broadcast_in_dim.24 = bf16[8,128,256]{2,1,0:T(8,128)(2,1)} broadcast(bf16[128,256]{1,0:T(8,128)(2,1)S(1)} %pad_maximum_fusion), dimensions={1,2} | broadcast | bytes 589824 | tf_op jit(solution)/shard_map/broadcast_in_dim | solution.py:152
  2.2 0.0 copy-start.2
  2.2 7.4 %all-to-all-start = ((bf16[8,128,256]{2,1,0:T(8,128)(2,1)}), bf16[8,128,256]{2,1,0:T(8,128)(2,1)S(1)}, u32[]{:S(2)}, u32[]{:S(2)}) async-start(bf16[8,128,256]{2,1,0:T(8,128)(2,1)} %broadcast_in_dim.24), calls=%async_computation | async-start | bytes 1048576 | tf_op jit(solution)/shard_map/all_to_all | solution.py:153
  9.7 0.0 copy-start.4
  9.7 0.0 copy-start.5
  9.7 0.6 pad_add_fusion.index_ref
  10.3 0.0 copy-start.6
  10.3 13.9 %all-to-all-done = bf16[8,128,256]{2,1,0:T(8,128)(2,1)S(1)} async-done(((bf16[8,128,256]{2,1,0:T(8,128)(2,1)}), bf16[8,128,256]{2,1,0:T(8,128)(2,1)S(1)}, u32[]{:S(2)}, u32[]{:S(2)}) %all-to-all-start) | async-done | bytes 524320 | tf_op jit(solution)/shard_map/all_to_all | solution.py:153
  24.1 0.0 copy-start
  24.1 0.0 collective-permute-start
  24.1 0.0 copy-done.4
  24.2 0.0 copy-done.5
  24.2 0.0 copy-done.6
  24.2 0.1 select_reduce_fusion
  24.3 0.0 copy-done.2
  24.3 0.8 %multiply_convert_fusion.grad_ref = bf16[128,768]{1,0:T(8,128)(2,1)} fusion(bf16[128,768]{1,0:T(8,128)(2,1)S(1)} %copy-done.2, f32[128]{0:T(128)S(1)} %select_reduce_fusion), kind=kLoop, calls=%fused_computation | loop fusion | flops 294912 | bytes 393728 | tf_op jit(solution)/shard_map/convert_element_type | solution.py:149
  25.1 1.0 %collective-permute-done = bf16[8,128,256]{2,1,0:T(8,128)(2,1)S(1)} collective-permute-done((bf16[8,128,256]{2,1,0:T(8,128)(2,1)S(1)}, bf16[8,128,256]{2,1,0:T(8,128)(2,1)S(1)}, u32[]{:S(2)}, u32[]{:S(2)}) %collective-permute-start) | collective-permute-done | bytes 524320 | tf_op jit(solution)/shard_map/ppermute | solution.py:154
  26.1 0.0 copy-start.1
  26.1 0.0 copy-done
  26.1 0.8 %copy-done.1 = bf16[8,128,256]{2,1,0:T(8,128)(2,1)} copy-done((bf16[8,128,256]{2,1,0:T(8,128)(2,1)}, bf16[8,128,256]{2,1,0:T(8,128)(2,1)S(1)}, u32[]{:S(2)}) %copy-start.1) | copy-done | bytes 524312
  26.9 7.6 %shard_map.102 = (f32[1,768]{1,0:T(1,128)}, f32[128,768]{1,0:T(8,128)}, f32[1024,256]{1,0:T(8,128)}, f32[1024,256]{1,0:T(8,128)}) custom-call(s32[2]{0:T(128)} %pad_add_fusion.index_ref, bf16[128,768]{1,0:T(8,128)(2,1)} %query_ref.1, bf16[128,768]{1,0:T(8,128)(2,1)} %multiply_convert_fusion.grad_ref, bf16[1024,256]{1,0:T(8,128)(2,1)} %bitcast.8, ...), custom_call_target="tpu_custom_call" | custom-call | tf_op jit(solution)/shard_map/pallas_call | solution.py:165
  34.5 0.1 collective-permute-start.1
  34.6 2.7 %collective-permute-done.1 = f32[1024,256]{1,0:T(8,128)S(1)} collective-permute-done((f32[1024,256]{1,0:T(8,128)}, f32[1024,256]{1,0:T(8,128)S(1)}, u32[]{:S(2)}, u32[]{:S(2)}) %collective-permute-start.1) | collective-permute-done | bytes 1048608 | tf_op jit(solution)/shard_map/ppermute | solution.py:178
  37.3 2.4 %add.13 = f32[1024,256]{1,0:T(8,128)} add(f32[1024,256]{1,0:T(8,128)} %get-tuple-element.10, f32[1024,256]{1,0:T(8,128)S(1)} %collective-permute-done.1) | non-fusion elementwise | flops 262144 | bytes 3145728 | tf_op jit(solution)/shard_map/add | solution.py:178
  39.7 0.0 copy-start.3
  39.7 7.2 %all-to-all-start.1 = ((f32[8,128,256]{2,1,0:T(8,128)}), f32[8,128,256]{2,1,0:T(8,128)S(1)}, u32[]{:S(2)}, u32[]{:S(2)}) async-start(f32[8,128,256]{2,1,0:T(8,128)} %bitcast.5), calls=%async_computation.1 | async-start | bytes 2097152 | tf_op jit(solution)/shard_map/all_to_all | solution.py:180
  46.9 0.0 copy-done.3
  46.9 0.6 reduce
  47.5 25.5 %all-to-all-done.1 = f32[8,128,256]{2,1,0:T(8,128)S(1)} async-done(((f32[8,128,256]{2,1,0:T(8,128)}), f32[8,128,256]{2,1,0:T(8,128)S(1)}, u32[]{:S(2)}, u32[]{:S(2)}) %all-to-all-start.1) | async-done | bytes 1048608 | tf_op jit(solution)/shard_map/all_to_all | solution.py:180
  73.0 0.1 reduce_sum.19
  73.1 0.6 fusion.1
  (1 shorter events, 0.0 us)
Async XLA Ops:
  2.2 22.0 %copy-start.2 = (bf16[128,768]{1,0:T(8,128)(2,1)S(1)}, bf16[128,768]{1,0:T(8,128)(2,1)}, u32[]{:S(2)}) copy-start(bf16[128,768]{1,0:T(8,128)(2,1)} %param.10) | copy-start | bytes 589828
  2.2 21.9 %all-to-all-start = ((bf16[8,128,256]{2,1,0:T(8,128)(2,1)}), bf16[8,128,256]{2,1,0:T(8,128)(2,1)S(1)}, u32[]{:S(2)}, u32[]{:S(2)}) async-start(bf16[8,128,256]{2,1,0:T(8,128)(2,1)} %broadcast_in_dim.24), calls=%async_computation | async-start | bytes 1048576 | tf_op jit(solution)/shard_map/all_to_all | solution.py:153
  9.7 14.5 %copy-start.4 = (s32[16]{0:T(128)S(1)}, s32[16]{0:T(128)}, u32[]{:S(2)}) copy-start(s32[16]{0:T(128)} %param.12) | copy-start | bytes 196
  9.7 14.5 %copy-start.5 = (s32[16]{0:T(128)S(1)}, s32[16]{0:T(128)}, u32[]{:S(2)}) copy-start(s32[16]{0:T(128)} %param.13) | copy-start | bytes 196
  10.3 13.9 %copy-start.6 = (s32[128]{0:T(128)S(1)}, s32[128]{0:T(128)}, u32[]{:S(2)}) copy-start(s32[128]{0:T(128)} %param.11) | copy-start | bytes 1540
  24.1 1.9 %copy-start = (bf16[8,128,256]{2,1,0:T(8,128)(2,1)}, bf16[8,128,256]{2,1,0:T(8,128)(2,1)S(1)}, u32[]{:S(2)}) copy-start(bf16[8,128,256]{2,1,0:T(8,128)(2,1)S(1)} %all-to-all-done) | copy-start | bytes 1572868
  24.1 1.9 %collective-permute-start = (bf16[8,128,256]{2,1,0:T(8,128)(2,1)S(1)}, bf16[8,128,256]{2,1,0:T(8,128)(2,1)S(1)}, u32[]{:S(2)}, u32[]{:S(2)}) collective-permute-start(bf16[8,128,256]{2,1,0:T(8,128)(2,1)S(1)} %all-to-all-done), channel_id=1, source_target_pairs={{0,2},{2,0},{1,3},{3,1},{4,6},{6,4},{5,7},{7,5},{8,10},{10,8},{9,1... | collective-permute-start | bytes 1572872 | tf_op jit(solution)/shard_map/ppermute | solution.py:154
  26.1 0.8 %copy-start.1 = (bf16[8,128,256]{2,1,0:T(8,128)(2,1)}, bf16[8,128,256]{2,1,0:T(8,128)(2,1)S(1)}, u32[]{:S(2)}) copy-start(bf16[8,128,256]{2,1,0:T(8,128)(2,1)S(1)} %collective-permute-done) | copy-start | bytes 1572868
  34.5 2.9 %collective-permute-start.1 = (f32[1024,256]{1,0:T(8,128)}, f32[1024,256]{1,0:T(8,128)S(1)}, u32[]{:S(2)}, u32[]{:S(2)}) collective-permute-start(f32[1024,256]{1,0:T(8,128)} %get-tuple-element.11), channel_id=1, source_target_pairs={{0,2},{2,0},{1,3},{3,1},{4,6},{6,4},{5,7},{7,5},{8,10},{10,8},{9,1... | collective-permute-start | bytes 3145736 | tf_op jit(solution)/shard_map/ppermute | solution.py:178
  39.7 7.2 %copy-start.3 = (f32[1,768]{1,0:T(1,128)S(1)}, f32[1,768]{1,0:T(1,128)}, u32[]{:S(2)}) copy-start(f32[1,768]{1,0:T(1,128)} %get-tuple-element.8) | copy-start | bytes 9220
  39.7 33.3 %all-to-all-start.1 = ((f32[8,128,256]{2,1,0:T(8,128)}), f32[8,128,256]{2,1,0:T(8,128)S(1)}, u32[]{:S(2)}, u32[]{:S(2)}) async-start(f32[8,128,256]{2,1,0:T(8,128)} %bitcast.5), calls=%async_computation.1 | async-start | bytes 2097152 | tf_op jit(solution)/shard_map/all_to_all | solution.py:180

commit v9 on v8

--- a/solution.py
+++ b/solution.py
@@ -21,7 +21,7 @@
 
 
 def attention_kernel(
-    index_ref, query_ref, grad_ref, mine_ref, other_ref,
+    index_ref, query_ref, weight_ref, cotangent_ref, mine_ref, other_ref,
     lse_ref, dq_ref, keep_ref, send_ref, *, heads, head_dim, tok_rows, score_scale, tile_blocks,
 ):
     index = index_ref[0]
@@ -33,8 +33,13 @@
     queries = jnp.concatenate(
         [query_ref[:, h * head_dim:(h + 1) * head_dim] for h in range(heads)], 0
     )
+    weights = weight_ref[...]
     grads = jnp.concatenate(
-        [grad_ref[:, h * head_dim:(h + 1) * head_dim] for h in range(heads)], 0
+        [
+            (weights * cotangent_ref[:, h * head_dim:(h + 1) * head_dim].astype(jnp.float32)).astype(jnp.bfloat16)
+            for h in range(heads)
+        ],
+        0,
     )
     queries_t = queries.astype(jnp.float32).T.astype(jnp.bfloat16)
     grads_t = grads.astype(jnp.float32).T.astype(jnp.bfloat16)
@@ -130,6 +135,10 @@
     lax.fori_loop(last + 1, pair_count, clear, 0)
 
 
+def add_kernel(first_ref, second_ref, out_ref):
+    out_ref[...] = first_ref[...] + second_ref[...]
+
+
 def body(queries, key_rows, value_rows, cotangent, trace_ids, correct, group_size):
     tok_rows = queries.shape[0]
     row_width = queries.shape[1]
@@ -146,7 +155,6 @@
     weights = jnp.sum(
         jnp.where(trace_ids[:, None] == traces[None, :], pass_rates[None, :], 0.0), axis=1
     )
-    out_grads = (weights[:, None] * cotangent.astype(jnp.float32)).astype(jnp.bfloat16)
 
     joined = jnp.concatenate([key_rows, value_rows], 1)
     spread = jnp.broadcast_to(joined[None], (chip_count,) + joined.shape)
@@ -170,12 +178,18 @@
             jax.ShapeDtypeStruct((chip_count * tok_rows, 2 * head_dim), jnp.float32),
             jax.ShapeDtypeStruct((chip_count * tok_rows, 2 * head_dim), jnp.float32),
         ),
-        in_specs=[smem, vmem, vmem, vmem, vmem],
+        in_specs=[smem, vmem, vmem, vmem, vmem, vmem],
         out_specs=(vmem, vmem, vmem, vmem),
-    )(jnp.stack([my_index, core]).astype(jnp.int32), queries, out_grads, mine, other)
+    )(jnp.stack([my_index, core]).astype(jnp.int32), queries, weights[:, None], cotangent, mine, other)
     log_totals = stacked_lse.reshape(head_count, tok_rows).T
 
-    own_part = keep_part + lax.ppermute(send_part, "core", [(0, 1), (1, 0)])
+    swapped = lax.ppermute(send_part, "core", [(0, 1), (1, 0)])
+    own_part = pl.pallas_call(
+        add_kernel,
+        out_shape=jax.ShapeDtypeStruct(keep_part.shape, jnp.float32),
+        in_specs=[vmem, vmem],
+        out_specs=vmem,
+    )(keep_part, swapped)
     reduced = jnp.sum(
         lax.all_to_all(own_part.reshape(chip_count, tok_rows, 2 * head_dim), "chip", 0, 0, tiled=True),
         axis=0,

time: 74.1 us -> 75.4 us (1.018)
  blocking collectives: 0 us -> 21.6 us
  waiting for transfers between devices: 43.1 us -> 28.2 us
  starting transfers between devices: 14.8 us -> 7.63 us
  other arithmetic: 5.32 us -> 2.15 us
  Pallas kernels: 7.58 us -> 10.2 us
  local copies, waits for them, and re-layouts: 2.29 us -> 4.58 us
    all_to_all x0 -> x1, blocking collectives: none -> 21.6 us  [body(): mine = lax.all_to_all(spread, 'chip', 0, 0, tiled=True)]
    all_to_all x1 -> x0, waiting for transfers between devices: 13.9 us -> none  [body(): mine = lax.all_to_all(spread, 'chip', 0, 0, tiled=True)]
    all_to_all x1 -> x0, starting transfers between devices: 7.41 us -> none  [body(): mine = lax.all_to_all(spread, 'chip', 0, 0, tiled=True)]
    pallas_call x0 -> x1, Pallas kernels: none -> 2.64 us  [body(): pl.pallas_call(add_kernel, out_shape=jax.ShapeDtypeStruct(keep_part.shape...]
    add x1 -> x0, other arithmetic: 2.4 us -> none  [body(): own_part = keep_part + lax.ppermute(send_part, 'core', [(0, 1), (1, 0)])]
    unnamed x14, local copies, waits for them, and re-layouts: 0.83 us -> 3.17 us
    ppermute x1, waiting for transfers between devices: 1 us -> 0.01 us  [body(): other = lax.ppermute(mine, 'core', [(0, 1), (1, 0)])]
    broadcast_in_dim x1, local copies, waits for them, and re-layouts: 0.83 us -> 0.03 us  [body(): spread = jnp.broadcast_to(joined[None], (chip_count,) + joined.shape)]
  transfers between devices with their start and end apart: 4 -> 3, of which waited for: 4 -> 2; matrix products, arithmetic and copies ran while one was open for 3% -> 3% of each run, Pallas kernels for 0% -> 0%
where the time goes in v9:
time: 75.4 us; the launch traced here: 75 us
  waiting for transfers between devices  28.2 us (37%)
  blocking collectives  21.6 us (29%)
  Pallas kernels  10.2 us (14%)
  starting transfers between devices  7.63 us (10%)
  local copies, waits for them, and re-layouts  4.58 us (6%)
  other arithmetic  2.15 us (3%)
    all_to_all x1, waiting for transfers between devices, body(): lax.all_to_all(own_part.reshape(chip_count, tok_rows, 2 * head_dim), 'chi...  25.7 us
    all_to_all x1, blocking collectives, body(): mine = lax.all_to_all(spread, 'chip', 0, 0, tiled=True)  21.6 us
    pallas_call x1, Pallas kernels, body(): pl.pallas_call(kernel, out_shape=(jax.ShapeDtypeStruct((1, rows), jnp.flo...  7.57 us
    all_to_all x1, starting transfers between devices, body(): lax.all_to_all(own_part.reshape(chip_count, tok_rows, 2 * head_dim), 'chi...  7.16 us
    unnamed x14, local copies, waits for them, and re-layouts  3.17 us
    pallas_call x1, Pallas kernels, body(): pl.pallas_call(add_kernel, out_shape=jax.ShapeDtypeStruct(keep_part.shape...  2.64 us
    ppermute x1, waiting for transfers between devices, body(): swapped = lax.ppermute(send_part, 'core', [(0, 1), (1, 0)])  2.5 us
  transfers between devices with their start and end apart: 3, of which 2 were waited for; matrix products, arithmetic and copies ran while one was open for 3% of the time, Pallas kernels for 0%

profile of v9, /device:TPU:0, one launch (start us, length us, event | category | flops | bytes accessed | tf_op | source)
XLA Modules:
  0.0 75.0 jit_solution(3497670491024343464)
XLA Ops:
  0.6 0.8 %pad_maximum_fusion = bf16[128,256]{1,0:T(8,128)(2,1)S(1)} fusion(bf16[128,128]{1,0:T(8,128)(2,1)} %param.9, bf16[128,128]{1,0:T(8,128)(2,1)} %param.8), kind=kLoop, calls=%fused_computation | loop fusion | flops 131072 | bytes 131072 | tf_op jit(solution)/shard_map/concatenate | solution.py:159
  1.5 21.6 %all_to_all.10 = bf16[8,128,256]{2,1,0:T(8,128)(2,1)S(1)} all-to-all(bf16[8,128,256]{2,1,0:T(8,128)(2,1)S(1)} %broadcast_in_dim.27), channel_id=1, replica_groups=mesh['chip'=8,'core'=2,'head'=2] {'chip'}, dimensions={0} | all-to-all | bytes 1048576 | tf_op jit(solution)/shard_map/all_to_all | solution.py:161
  23.1 0.0 copy-start
  23.1 0.0 collective-permute-start
  23.1 0.0 copy-start.4
  23.1 0.0 copy-start.5
  23.1 0.6 copy-done.4
  23.7 0.1 copy-done.5
  23.8 0.0 copy-start.6
  23.8 0.6 copy-done.6
  24.4 0.1 select_reduce_fusion
  24.5 0.7 copy.12.weight_ref
  25.3 0.6 pad_add_fusion.index_ref
  25.9 0.0 collective-permute-done
  25.9 0.0 copy-start.2
  25.9 0.0 copy-done
  25.9 0.8 %copy-done.2 = bf16[8,128,256]{2,1,0:T(8,128)(2,1)} copy-done((bf16[8,128,256]{2,1,0:T(8,128)(2,1)}, bf16[8,128,256]{2,1,0:T(8,128)(2,1)S(1)}, u32[]{:S(2)}) %copy-start.2) | copy-done | bytes 524312
  26.7 7.6 %shard_map.102 = (f32[1,768]{1,0:T(1,128)}, f32[128,768]{1,0:T(8,128)}, f32[1024,256]{1,0:T(8,128)}, f32[1024,256]{1,0:T(8,128)}) custom-call(s32[2]{0:T(128)} %pad_add_fusion.index_ref, bf16[128,768]{1,0:T(8,128)(2,1)} %query_ref.1, f32[128,1]{1,0:T(8,128)} %copy.12.weight_ref, bf16[128,768]{1,0:T(8,128)(2,1)} %cotangent_ref.1, bf16[1024,256]{1,0:T(8,128)(2,1)} %bitcast.10, ...), custom_call_target="tpu_custom_call" | custom-call | tf_op jit(solution)/shard_map/pallas_call | solution.py:173
  34.2 0.5 collective-permute-start.1
  34.7 2.5 %collective-permute-done.1.second_ref = f32[1024,256]{1,0:T(8,128)S(1)} collective-permute-done((f32[1024,256]{1,0:T(8,128)}, f32[1024,256]{1,0:T(8,128)S(1)}, u32[]{:S(2)}, u32[]{:S(2)}) %collective-permute-start.1) | collective-permute-done | bytes 1048608 | tf_op jit(solution)/shard_map/ppermute | solution.py:186
  37.2 0.0 copy-start.1
  37.2 1.0 %copy-done.1 = f32[1024,256]{1,0:T(8,128)} copy-done((f32[1024,256]{1,0:T(8,128)}, f32[1024,256]{1,0:T(8,128)S(1)}, u32[]{:S(2)}) %copy-start.1) | copy-done | bytes 1048600
  38.2 2.6 %shard_map.103 = f32[1024,256]{1,0:T(8,128)} custom-call(f32[1024,256]{1,0:T(8,128)} %get-tuple-element.10.first_ref, f32[1024,256]{1,0:T(8,128)} %copy-done.1), custom_call_target="tpu_custom_call" | custom-call | tf_op jit(solution)/shard_map/pallas_call | solution.py:187
  40.9 0.0 copy-start.3
  40.9 7.2 %all-to-all-start.1 = ((f32[8,128,256]{2,1,0:T(8,128)}), f32[8,128,256]{2,1,0:T(8,128)S(1)}, u32[]{:S(2)}, u32[]{:S(2)}) async-start(f32[8,128,256]{2,1,0:T(8,128)} %bitcast.9), calls=%async_computation.1 | async-start | bytes 2097152 | tf_op jit(solution)/shard_map/all_to_all | solution.py:194
  48.0 0.0 copy-done.3
  48.0 0.6 reduce
  48.6 25.7 %all-to-all-done.1 = f32[8,128,256]{2,1,0:T(8,128)S(1)} async-done(((f32[8,128,256]{2,1,0:T(8,128)}), f32[8,128,256]{2,1,0:T(8,128)S(1)}, u32[]{:S(2)}, u32[]{:S(2)}) %all-to-all-start.1) | async-done | bytes 1048608 | tf_op jit(solution)/shard_map/all_to_all | solution.py:194
  74.3 0.1 reduce_sum.19
  74.4 0.6 fusion.1
  (2 shorter events, 0.0 us)
Async XLA Ops:
  23.1 2.8 %copy-start = (bf16[8,128,256]{2,1,0:T(8,128)(2,1)}, bf16[8,128,256]{2,1,0:T(8,128)(2,1)S(1)}, u32[]{:S(2)}) copy-start(bf16[8,128,256]{2,1,0:T(8,128)(2,1)S(1)} %all_to_all.10) | copy-start | bytes 1572868
  23.1 2.8 %collective-permute-start = (bf16[8,128,256]{2,1,0:T(8,128)(2,1)S(1)}, bf16[8,128,256]{2,1,0:T(8,128)(2,1)S(1)}, u32[]{:S(2)}, u32[]{:S(2)}) collective-permute-start(bf16[8,128,256]{2,1,0:T(8,128)(2,1)S(1)} %all_to_all.10), channel_id=1, source_target_pairs={{0,2},{2,0},{1,3},{3,1},{4,6},{6,4},{5,7},{7,5},{8,10},{10,8},{9,1... | collective-permute-start | bytes 1572872 | tf_op jit(solution)/shard_map/ppermute | solution.py:162
  23.1 0.7 copy-start.4
  23.1 0.7 copy-start.5
  23.8 0.7 copy-start.6
  25.9 0.8 %copy-start.2 = (bf16[8,128,256]{2,1,0:T(8,128)(2,1)}, bf16[8,128,256]{2,1,0:T(8,128)(2,1)S(1)}, u32[]{:S(2)}) copy-start(bf16[8,128,256]{2,1,0:T(8,128)(2,1)S(1)} %collective-permute-done) | copy-start | bytes 1572868
  34.2 3.0 %collective-permute-start.1 = (f32[1024,256]{1,0:T(8,128)}, f32[1024,256]{1,0:T(8,128)S(1)}, u32[]{:S(2)}, u32[]{:S(2)}) collective-permute-start(f32[1024,256]{1,0:T(8,128)} %get-tuple-element.11), channel_id=1, source_target_pairs={{0,2},{2,0},{1,3},{3,1},{4,6},{6,4},{5,7},{7,5},{8,10},{10,8},{9,1... | collective-permute-start | bytes 3145736 | tf_op jit(solution)/shard_map/ppermute | solution.py:186
  37.2 1.0 %copy-start.1 = (f32[1024,256]{1,0:T(8,128)}, f32[1024,256]{1,0:T(8,128)S(1)}, u32[]{:S(2)}) copy-start(f32[1024,256]{1,0:T(8,128)S(1)} %collective-permute-done.1.second_ref) | copy-start | bytes 3145732
  40.9 7.2 %copy-start.3 = (f32[1,768]{1,0:T(1,128)S(1)}, f32[1,768]{1,0:T(1,128)}, u32[]{:S(2)}) copy-start(f32[1,768]{1,0:T(1,128)} %get-tuple-element.8) | copy-start | bytes 9220
  40.9 33.5 %all-to-all-start.1 = ((f32[8,128,256]{2,1,0:T(8,128)}), f32[8,128,256]{2,1,0:T(8,128)S(1)}, u32[]{:S(2)}, u32[]{:S(2)}) async-start(f32[8,128,256]{2,1,0:T(8,128)} %bitcast.9), calls=%async_computation.1 | async-start | bytes 2097152 | tf_op jit(solution)/shard_map/all_to_all | solution.py:194

commit v10 on v7

--- a/solution.py
+++ b/solution.py
@@ -9,6 +9,8 @@
 from jax.sharding import Mesh, PartitionSpec as P
 
 PASSK = 4
+LOG2_E = 1.4426950408889634
+LN_2 = 0.6931471805599453
 
 
 def pass_rate(correct, group_size):
@@ -54,7 +56,7 @@
         joined = jnp.concatenate(parts, 0)
         key_block = joined[:, :head_dim]
         value_block = joined[:, head_dim:]
-        scores = jnp.dot(key_block, queries_t, preferred_element_type=jnp.float32) * score_scale
+        scores = jnp.dot(key_block, queries_t, preferred_element_type=jnp.float32) * (score_scale * LOG2_E)
         grad_probs = jnp.dot(value_block, grads_t, preferred_element_type=jnp.float32)
         return pl.multiple_of(pair * pair_rows, pair_rows), key_block, scores, grad_probs
 
@@ -64,10 +66,10 @@
         if masked:
             scores = jnp.where(visible, scores, -1e30)
         new_peak = jnp.maximum(peak, jnp.max(scores, axis=0, keepdims=True))
-        exp_terms = jnp.exp(scores - new_peak)
+        exp_terms = jnp.exp2(scores - new_peak)
         if masked:
             exp_terms = jnp.where(visible, exp_terms, 0.0)
-        shrink = jnp.exp(peak - new_peak)
+        shrink = jnp.exp2(peak - new_peak)
         total = total * shrink + jnp.sum(exp_terms, axis=0, keepdims=True)
         weighted = weighted * shrink + jnp.sum(exp_terms * grad_probs, axis=0, keepdims=True)
         return new_peak, total, weighted
@@ -79,13 +81,13 @@
     )
     carry = lax.fori_loop(0, last, lambda b, c: forward(b, c, False), start_carry)
     peak, total, weighted = forward(last, carry, True)
-    log_totals = peak + jnp.log(total)
+    log_totals = peak + jnp.log2(total)
     delta_rows = weighted / total
-    lse_ref[...] = log_totals
+    lse_ref[...] = log_totals * LN_2
 
     def backward(pair, grad_query_t, masked):
         start, key_block, scores, grad_probs = blocks_of(pair)
-        probabilities = jnp.exp(scores - log_totals)
+        probabilities = jnp.exp2(scores - log_totals)
         if masked:
             probabilities = jnp.where(visible, probabilities, 0.0)
         grad_scores = (probabilities * (grad_probs - delta_rows)).astype(jnp.bfloat16)

time: 73.9 us -> 73.7 us (level)
  no operation moved by 1% of the time
where the time goes in v10:
time: 73.7 us; the launch traced here: 73.3 us
  blocking collectives  32.6 us (44%)
  waiting for transfers between devices  17.4 us (24%)
  starting transfers between devices  7.68 us (10%)
  Pallas kernels  7.24 us (10%)
  other arithmetic  5.39 us (7%)
  local copies, waits for them, and re-layouts  2.24 us (3%)
    all_to_all x1, blocking collectives, body(): lax.all_to_all(own_part, 'chip', 0, 0, tiled=True)  32.6 us
    all_to_all x1, waiting for transfers between devices, body(): mine = lax.all_to_all(spread, 'chip', 0, 0, tiled=True)  13.9 us
    all_to_all x1, starting transfers between devices, body(): mine = lax.all_to_all(spread, 'chip', 0, 0, tiled=True)  7.41 us
    pallas_call x1, Pallas kernels, body(): pl.pallas_call(kernel, out_shape=(jax.ShapeDtypeStruct((1, rows), jnp.flo...  7.24 us
    ppermute x1, waiting for transfers between devices, body(): lax.ppermute(jnp.where(lead, value_part, key_part), 'core', [(0, 1), (1,...  2.53 us
    select_n x1, other arithmetic, body(): jnp.where(lead, value_part, key_part)  1.68 us
  transfers between devices with their start and end apart: 4, of which 3 were waited for; matrix products, arithmetic and copies ran while one was open for 3% of the time, Pallas kernels for 0%

profile of v10, /device:TPU:0, one launch (start us, length us, event | category | flops | bytes accessed | tf_op | source)
XLA Modules:
  0.0 73.3 jit_solution(895379158804514543)
XLA Ops:
  0.6 0.8 %pad_maximum_fusion = bf16[128,256]{1,0:T(8,128)(2,1)S(1)} fusion(bf16[128,128]{1,0:T(8,128)(2,1)} %param.9, bf16[128,128]{1,0:T(8,128)(2,1)} %param.8), kind=kLoop, calls=%fused_computation.3 | loop fusion | flops 131072 | bytes 131072 | tf_op jit(solution)/shard_map/concatenate | solution.py:138
  1.4 0.8 %broadcast_in_dim.24 = bf16[8,128,256]{2,1,0:T(8,128)(2,1)} broadcast(bf16[128,256]{1,0:T(8,128)(2,1)S(1)} %pad_maximum_fusion), dimensions={1,2} | broadcast | bytes 589824 | tf_op jit(solution)/shard_map/broadcast_in_dim | solution.py:139
  2.2 0.0 copy-start.2
  2.2 7.4 %all-to-all-start = ((bf16[8,128,256]{2,1,0:T(8,128)(2,1)}), bf16[8,128,256]{2,1,0:T(8,128)(2,1)S(1)}, u32[]{:S(2)}, u32[]{:S(2)}) async-start(bf16[8,128,256]{2,1,0:T(8,128)(2,1)} %broadcast_in_dim.24), calls=%async_computation | async-start | bytes 1048576 | tf_op jit(solution)/shard_map/all_to_all | solution.py:140
  9.7 0.0 copy-start.4
  9.7 0.0 copy-start.5
  9.7 0.6 pad_add_fusion.index_ref
  10.3 0.0 copy-start.6
  10.3 13.9 %all-to-all-done = bf16[8,128,256]{2,1,0:T(8,128)(2,1)S(1)} async-done(((bf16[8,128,256]{2,1,0:T(8,128)(2,1)}), bf16[8,128,256]{2,1,0:T(8,128)(2,1)S(1)}, u32[]{:S(2)}, u32[]{:S(2)}) %all-to-all-start) | async-done | bytes 524320 | tf_op jit(solution)/shard_map/all_to_all | solution.py:140
  24.1 0.0 collective-permute-start
  24.1 0.0 copy-done.4
  24.2 0.0 copy-done.5
  24.2 0.0 copy-done.6
  24.2 0.1 select_reduce_fusion
  24.3 0.0 copy-done.2
  24.3 0.8 %multiply_convert_fusion.grad_ref = bf16[128,768]{1,0:T(8,128)(2,1)} fusion(bf16[128,768]{1,0:T(8,128)(2,1)S(1)} %copy-done.2, f32[128]{0:T(128)S(1)} %select_reduce_fusion), kind=kLoop, calls=%fused_computation.2 | loop fusion | flops 294912 | bytes 393728 | tf_op jit(solution)/shard_map/convert_element_type | solution.py:136
  25.1 1.0 %collective-permute-done = bf16[8,128,256]{2,1,0:T(8,128)(2,1)S(1)} collective-permute-done((bf16[8,128,256]{2,1,0:T(8,128)(2,1)S(1)}, bf16[8,128,256]{2,1,0:T(8,128)(2,1)S(1)}, u32[]{:S(2)}, u32[]{:S(2)}) %collective-permute-start) | collective-permute-done | bytes 524320 | tf_op jit(solution)/shard_map/ppermute | solution.py:141
  26.1 0.0 copy-done
  26.1 0.8 %copy-done.1 = bf16[8,128,256]{2,1,0:T(8,128)(2,1)} copy-done((bf16[8,128,256]{2,1,0:T(8,128)(2,1)}, bf16[8,128,256]{2,1,0:T(8,128)(2,1)S(1)}, u32[]{:S(2)}) %copy-start.1) | copy-done | bytes 524312
  26.9 7.2 %shard_map.102 = (f32[1,768]{1,0:T(1,128)}, f32[128,768]{1,0:T(8,128)}, f32[2048,128]{1,0:T(8,128)}, f32[2048,128]{1,0:T(8,128)}) custom-call(s32[2]{0:T(128)} %pad_add_fusion.index_ref, bf16[128,768]{1,0:T(8,128)(2,1)} %query_ref.1, bf16[128,768]{1,0:T(8,128)(2,1)} %multiply_convert_fusion.grad_ref, bf16[1024,256]{1,0:T(8,128)(2,1)} %bitcast.10, ...), custom_call_target="tpu_custom_call" | custom-call | tf_op jit(solution)/shard_map/pallas_call | solution.py:152
  34.1 1.7 %broadcast_select_fusion = (f32[2048,128]{1,0:T(8,128)S(1)}, f32[2048,128]{1,0:T(8,128)S(1)}) fusion(f32[2048,128]{1,0:T(8,128)} %get-tuple-element.11, f32[2048,128]{1,0:T(8,128)} %get-tuple-element.10, pred[]{:T(512)S(6)} %eq.19), kind=kLoop, calls=%fused_computation | loop fusion | flops 524288 | bytes 4194305 | tf_op jit(solution)/shard_map/jit(_where)/select_n | solution.py:169
  35.8 0.2 collective-permute-start.1
  36.0 2.5 %collective-permute-done.1 = f32[8,256,128]{2,1,0:T(8,128)S(1)} collective-permute-done((f32[8,256,128]{2,1,0:T(8,128)S(1)}, f32[8,256,128]{2,1,0:T(8,128)S(1)}, u32[]{:S(2)}, u32[]{:S(2)}) %collective-permute-start.1) | collective-permute-done | bytes 1048608 | tf_op jit(solution)/shard_map/ppermute | solution.py:169
  38.5 0.2 add.13
  38.7 32.6 %all_to_all.10 = f32[8,256,128]{2,1,0:T(8,128)S(1)} all-to-all(f32[8,256,128]{2,1,0:T(8,128)S(1)} %add.13), channel_id=1, replica_groups=mesh['chip'=8,'core'=2,'head'=2] {'chip'}, dimensions={0} | all-to-all | bytes 2097152 | tf_op jit(solution)/shard_map/all_to_all | solution.py:171
  71.3 0.1 reduce_sum.19
  71.3 0.0 copy-start.3
  71.3 0.1 collective-permute-start.2
  71.4 0.6 copy-done.3
  72.0 0.6 reduce
  72.6 0.0 collective-permute-done.2
  72.6 0.6 broadcast_select_fusion.2
  (4 shorter events, 0.0 us)
Async XLA Ops:
  2.2 22.0 %copy-start.2 = (bf16[128,768]{1,0:T(8,128)(2,1)S(1)}, bf16[128,768]{1,0:T(8,128)(2,1)}, u32[]{:S(2)}) copy-start(bf16[128,768]{1,0:T(8,128)(2,1)} %param.10) | copy-start | bytes 589828
  2.2 21.9 %all-to-all-start = ((bf16[8,128,256]{2,1,0:T(8,128)(2,1)}), bf16[8,128,256]{2,1,0:T(8,128)(2,1)S(1)}, u32[]{:S(2)}, u32[]{:S(2)}) async-start(bf16[8,128,256]{2,1,0:T(8,128)(2,1)} %broadcast_in_dim.24), calls=%async_computation | async-start | bytes 1048576 | tf_op jit(solution)/shard_map/all_to_all | solution.py:140
  9.7 14.5 %copy-start.4 = (s32[16]{0:T(128)S(1)}, s32[16]{0:T(128)}, u32[]{:S(2)}) copy-start(s32[16]{0:T(128)} %param.12) | copy-start | bytes 196
  9.7 14.5 %copy-start.5 = (s32[16]{0:T(128)S(1)}, s32[16]{0:T(128)}, u32[]{:S(2)}) copy-start(s32[16]{0:T(128)} %param.13) | copy-start | bytes 196
  10.3 13.9 %copy-start.6 = (s32[128]{0:T(128)S(1)}, s32[128]{0:T(128)}, u32[]{:S(2)}) copy-start(s32[128]{0:T(128)} %param.11) | copy-start | bytes 1540
  24.1 1.9 %copy-start = (bf16[8,128,256]{2,1,0:T(8,128)(2,1)}, bf16[8,128,256]{2,1,0:T(8,128)(2,1)S(1)}, u32[]{:S(2)}) copy-start(bf16[8,128,256]{2,1,0:T(8,128)(2,1)S(1)} %all-to-all-done) | copy-start | bytes 1572868
  24.1 1.9 %collective-permute-start = (bf16[8,128,256]{2,1,0:T(8,128)(2,1)S(1)}, bf16[8,128,256]{2,1,0:T(8,128)(2,1)S(1)}, u32[]{:S(2)}, u32[]{:S(2)}) collective-permute-start(bf16[8,128,256]{2,1,0:T(8,128)(2,1)S(1)} %all-to-all-done), channel_id=1, source_target_pairs={{0,2},{2,0},{1,3},{3,1},{4,6},{6,4},{5,7},{7,5},{8,10},{10,8},{9,1... | collective-permute-start | bytes 1572872 | tf_op jit(solution)/shard_map/ppermute | solution.py:141
  26.1 0.8 %copy-start.1 = (bf16[8,128,256]{2,1,0:T(8,128)(2,1)}, bf16[8,128,256]{2,1,0:T(8,128)(2,1)S(1)}, u32[]{:S(2)}) copy-start(bf16[8,128,256]{2,1,0:T(8,128)(2,1)S(1)} %collective-permute-done) | copy-start | bytes 1572868
  35.8 2.7 %collective-permute-start.1 = (f32[8,256,128]{2,1,0:T(8,128)S(1)}, f32[8,256,128]{2,1,0:T(8,128)S(1)}, u32[]{:S(2)}, u32[]{:S(2)}) collective-permute-start(f32[8,256,128]{2,1,0:T(8,128)S(1)} %bitcast.11), channel_id=1, source_target_pairs={{0,2},{2,0},{1,3},{3,1},{4,6},{6,4},{5,7},{7,5},{8,10},{10,8},{9,1... | collective-permute-start | bytes 3145736 | tf_op jit(solution)/shard_map/ppermute | solution.py:169
  71.3 0.7 copy-start.3
  71.3 1.3 %collective-permute-start.2 = (bf16[128,128]{1,0:T(8,128)(2,1)S(1)}, bf16[128,128]{1,0:T(8,128)(2,1)S(1)}, u32[]{:S(2)}, u32[]{:S(2)}) collective-permute-start(bf16[128,128]{1,0:T(8,128)(2,1)S(1)} %broadcast_select_fusion.4), channel_id=1, source_target_pairs={{0,2},{2,0},{1,3},{3,1},{4,6},{6,4},{5,7},{7,5},{8,10},{10,8},{9,1... | collective-permute-start | bytes 98312 | tf_op jit(solution)/shard_map/ppermute | solution.py:172

commit v11 on v10

--- a/solution.py
+++ b/solution.py
@@ -40,9 +40,16 @@
     )
     queries_t = queries.astype(jnp.float32).T.astype(jnp.bfloat16)
     grads_t = grads.astype(jnp.float32).T.astype(jnp.bfloat16)
-    key_tok = lax.broadcasted_iota(jnp.int32, (pair_rows, rows), 0)
-    row_tok = lax.rem(lax.broadcasted_iota(jnp.int32, (pair_rows, rows), 1), tok_rows)
-    visible = key_tok <= row_tok + (index - tile_blocks * last) * tok_rows
+    shift = (index - tile_blocks * last) * tok_rows
+
+    def visible():
+        key_tok = lax.broadcasted_iota(jnp.int32, (pair_rows, rows), 0)
+        lane = lax.broadcasted_iota(jnp.int32, (pair_rows, rows), 1)
+        if tok_rows & (tok_rows - 1) == 0:
+            row_tok = jnp.bitwise_and(lane, tok_rows - 1)
+        else:
+            row_tok = lax.rem(lane, tok_rows)
+        return key_tok <= row_tok + shift
     contract_first = (((0,), (0,)), ((), ()))
     lead = core == 0
 
@@ -64,11 +71,12 @@
         peak, total, weighted = carry
         _, _, scores, grad_probs = blocks_of(pair)
         if masked:
-            scores = jnp.where(visible, scores, -1e30)
+            mask = visible()
+            scores = jnp.where(mask, scores, -1e30)
         new_peak = jnp.maximum(peak, jnp.max(scores, axis=0, keepdims=True))
         exp_terms = jnp.exp2(scores - new_peak)
         if masked:
-            exp_terms = jnp.where(visible, exp_terms, 0.0)
+            exp_terms = jnp.where(mask, exp_terms, 0.0)
         shrink = jnp.exp2(peak - new_peak)
         total = total * shrink + jnp.sum(exp_terms, axis=0, keepdims=True)
         weighted = weighted * shrink + jnp.sum(exp_terms * grad_probs, axis=0, keepdims=True)
@@ -89,7 +97,7 @@
         start, key_block, scores, grad_probs = blocks_of(pair)
         probabilities = jnp.exp2(scores - log_totals)
         if masked:
-            probabilities = jnp.where(visible, probabilities, 0.0)
+            probabilities = jnp.where(visible(), probabilities, 0.0)
         grad_scores = (probabilities * (grad_probs - delta_rows)).astype(jnp.bfloat16)
         prob_bf16 = probabilities.astype(jnp.bfloat16)
         grad_query_t = grad_query_t + lax.dot_general(

time: 73.7 us -> 73.7 us (level)
  no operation moved by 1% of the time
where the time goes in v11:
time: 73.7 us; the launch traced here: 73.3 us
  blocking collectives  32.6 us (44%)
  waiting for transfers between devices  17.4 us (24%)
  starting transfers between devices  7.69 us (10%)
  Pallas kernels  7.23 us (10%)
  other arithmetic  5.39 us (7%)
  local copies, waits for them, and re-layouts  2.24 us (3%)
    all_to_all x1, blocking collectives, body(): lax.all_to_all(own_part, 'chip', 0, 0, tiled=True)  32.6 us
    all_to_all x1, waiting for transfers between devices, body(): mine = lax.all_to_all(spread, 'chip', 0, 0, tiled=True)  13.9 us
    all_to_all x1, starting transfers between devices, body(): mine = lax.all_to_all(spread, 'chip', 0, 0, tiled=True)  7.41 us
    pallas_call x1, Pallas kernels, body(): pl.pallas_call(kernel, out_shape=(jax.ShapeDtypeStruct((1, rows), jnp.flo...  7.23 us
    ppermute x1, waiting for transfers between devices, body(): lax.ppermute(jnp.where(lead, value_part, key_part), 'core', [(0, 1), (1,...  2.52 us
    select_n x1, other arithmetic, body(): jnp.where(lead, value_part, key_part)  1.68 us
  transfers between devices with their start and end apart: 4, of which 3 were waited for; matrix products, arithmetic and copies ran while one was open for 3% of the time, Pallas kernels for 0%

profile of v11, /device:TPU:0, one launch (start us, length us, event | category | flops | bytes accessed | tf_op | source)
XLA Modules:
  0.0 73.3 jit_solution(14037618198055525412)
XLA Ops:
  0.6 0.8 %pad_maximum_fusion = bf16[128,256]{1,0:T(8,128)(2,1)S(1)} fusion(bf16[128,128]{1,0:T(8,128)(2,1)} %param.9, bf16[128,128]{1,0:T(8,128)(2,1)} %param.8), kind=kLoop, calls=%fused_computation.3 | loop fusion | flops 131072 | bytes 131072 | tf_op jit(solution)/shard_map/concatenate | solution.py:146
  1.4 0.8 %broadcast_in_dim.24 = bf16[8,128,256]{2,1,0:T(8,128)(2,1)} broadcast(bf16[128,256]{1,0:T(8,128)(2,1)S(1)} %pad_maximum_fusion), dimensions={1,2} | broadcast | bytes 589824 | tf_op jit(solution)/shard_map/broadcast_in_dim | solution.py:147
  2.2 0.0 copy-start.2
  2.2 7.4 %all-to-all-start = ((bf16[8,128,256]{2,1,0:T(8,128)(2,1)}), bf16[8,128,256]{2,1,0:T(8,128)(2,1)S(1)}, u32[]{:S(2)}, u32[]{:S(2)}) async-start(bf16[8,128,256]{2,1,0:T(8,128)(2,1)} %broadcast_in_dim.24), calls=%async_computation | async-start | bytes 1048576 | tf_op jit(solution)/shard_map/all_to_all | solution.py:148
  9.7 0.0 copy-start.4
  9.7 0.0 copy-start.5
  9.7 0.6 pad_add_fusion.index_ref
  10.3 0.0 copy-start.6
  10.3 13.9 %all-to-all-done = bf16[8,128,256]{2,1,0:T(8,128)(2,1)S(1)} async-done(((bf16[8,128,256]{2,1,0:T(8,128)(2,1)}), bf16[8,128,256]{2,1,0:T(8,128)(2,1)S(1)}, u32[]{:S(2)}, u32[]{:S(2)}) %all-to-all-start) | async-done | bytes 524320 | tf_op jit(solution)/shard_map/all_to_all | solution.py:148
  24.1 0.0 collective-permute-start
  24.1 0.0 copy-done.4
  24.2 0.0 copy-done.5
  24.2 0.0 copy-done.6
  24.2 0.1 select_reduce_fusion
  24.3 0.0 copy-done.2
  24.3 0.8 %multiply_convert_fusion.grad_ref = bf16[128,768]{1,0:T(8,128)(2,1)} fusion(bf16[128,768]{1,0:T(8,128)(2,1)S(1)} %copy-done.2, f32[128]{0:T(128)S(1)} %select_reduce_fusion), kind=kLoop, calls=%fused_computation.2 | loop fusion | flops 294912 | bytes 393728 | tf_op jit(solution)/shard_map/convert_element_type | solution.py:144
  25.1 1.0 %collective-permute-done = bf16[8,128,256]{2,1,0:T(8,128)(2,1)S(1)} collective-permute-done((bf16[8,128,256]{2,1,0:T(8,128)(2,1)S(1)}, bf16[8,128,256]{2,1,0:T(8,128)(2,1)S(1)}, u32[]{:S(2)}, u32[]{:S(2)}) %collective-permute-start) | collective-permute-done | bytes 524320 | tf_op jit(solution)/shard_map/ppermute | solution.py:149
  26.1 0.0 copy-done
  26.1 0.8 %copy-done.1 = bf16[8,128,256]{2,1,0:T(8,128)(2,1)} copy-done((bf16[8,128,256]{2,1,0:T(8,128)(2,1)}, bf16[8,128,256]{2,1,0:T(8,128)(2,1)S(1)}, u32[]{:S(2)}) %copy-start.1) | copy-done | bytes 524312
  26.9 7.2 %shard_map.102 = (f32[1,768]{1,0:T(1,128)}, f32[128,768]{1,0:T(8,128)}, f32[2048,128]{1,0:T(8,128)}, f32[2048,128]{1,0:T(8,128)}) custom-call(s32[2]{0:T(128)} %pad_add_fusion.index_ref, bf16[128,768]{1,0:T(8,128)(2,1)} %query_ref.1, bf16[128,768]{1,0:T(8,128)(2,1)} %multiply_convert_fusion.grad_ref, bf16[1024,256]{1,0:T(8,128)(2,1)} %bitcast.10, ...), custom_call_target="tpu_custom_call" | custom-call | tf_op jit(solution)/shard_map/pallas_call | solution.py:160
  34.1 1.7 %broadcast_select_fusion = (f32[2048,128]{1,0:T(8,128)S(1)}, f32[2048,128]{1,0:T(8,128)S(1)}) fusion(f32[2048,128]{1,0:T(8,128)} %get-tuple-element.11, f32[2048,128]{1,0:T(8,128)} %get-tuple-element.10, pred[]{:T(512)S(6)} %eq.19), kind=kLoop, calls=%fused_computation | loop fusion | flops 524288 | bytes 4194305 | tf_op jit(solution)/shard_map/jit(_where)/select_n | solution.py:177
  35.8 0.2 collective-permute-start.1
  36.0 2.5 %collective-permute-done.1 = f32[8,256,128]{2,1,0:T(8,128)S(1)} collective-permute-done((f32[8,256,128]{2,1,0:T(8,128)S(1)}, f32[8,256,128]{2,1,0:T(8,128)S(1)}, u32[]{:S(2)}, u32[]{:S(2)}) %collective-permute-start.1) | collective-permute-done | bytes 1048608 | tf_op jit(solution)/shard_map/ppermute | solution.py:177
  38.5 0.2 add.13
  38.7 32.6 %all_to_all.10 = f32[8,256,128]{2,1,0:T(8,128)S(1)} all-to-all(f32[8,256,128]{2,1,0:T(8,128)S(1)} %add.13), channel_id=1, replica_groups=mesh['chip'=8,'core'=2,'head'=2] {'chip'}, dimensions={0} | all-to-all | bytes 2097152 | tf_op jit(solution)/shard_map/all_to_all | solution.py:179
  71.3 0.1 reduce_sum.19
  71.3 0.0 copy-start.3
  71.4 0.1 collective-permute-start.2
  71.4 0.6 copy-done.3
  72.0 0.6 reduce
  72.6 0.0 collective-permute-done.2
  72.6 0.6 broadcast_select_fusion.2
  (4 shorter events, 0.0 us)
Async XLA Ops:
  2.2 22.0 %copy-start.2 = (bf16[128,768]{1,0:T(8,128)(2,1)S(1)}, bf16[128,768]{1,0:T(8,128)(2,1)}, u32[]{:S(2)}) copy-start(bf16[128,768]{1,0:T(8,128)(2,1)} %param.10) | copy-start | bytes 589828
  2.2 21.9 %all-to-all-start = ((bf16[8,128,256]{2,1,0:T(8,128)(2,1)}), bf16[8,128,256]{2,1,0:T(8,128)(2,1)S(1)}, u32[]{:S(2)}, u32[]{:S(2)}) async-start(bf16[8,128,256]{2,1,0:T(8,128)(2,1)} %broadcast_in_dim.24), calls=%async_computation | async-start | bytes 1048576 | tf_op jit(solution)/shard_map/all_to_all | solution.py:148
  9.7 14.5 %copy-start.4 = (s32[16]{0:T(128)S(1)}, s32[16]{0:T(128)}, u32[]{:S(2)}) copy-start(s32[16]{0:T(128)} %param.12) | copy-start | bytes 196
  9.7 14.5 %copy-start.5 = (s32[16]{0:T(128)S(1)}, s32[16]{0:T(128)}, u32[]{:S(2)}) copy-start(s32[16]{0:T(128)} %param.13) | copy-start | bytes 196
  10.3 13.9 %copy-start.6 = (s32[128]{0:T(128)S(1)}, s32[128]{0:T(128)}, u32[]{:S(2)}) copy-start(s32[128]{0:T(128)} %param.11) | copy-start | bytes 1540
  24.1 1.9 %copy-start = (bf16[8,128,256]{2,1,0:T(8,128)(2,1)}, bf16[8,128,256]{2,1,0:T(8,128)(2,1)S(1)}, u32[]{:S(2)}) copy-start(bf16[8,128,256]{2,1,0:T(8,128)(2,1)S(1)} %all-to-all-done) | copy-start | bytes 1572868
  24.1 1.9 %collective-permute-start = (bf16[8,128,256]{2,1,0:T(8,128)(2,1)S(1)}, bf16[8,128,256]{2,1,0:T(8,128)(2,1)S(1)}, u32[]{:S(2)}, u32[]{:S(2)}) collective-permute-start(bf16[8,128,256]{2,1,0:T(8,128)(2,1)S(1)} %all-to-all-done), channel_id=1, source_target_pairs={{0,2},{2,0},{1,3},{3,1},{4,6},{6,4},{5,7},{7,5},{8,10},{10,8},{9,1... | collective-permute-start | bytes 1572872 | tf_op jit(solution)/shard_map/ppermute | solution.py:149
  26.1 0.8 %copy-start.1 = (bf16[8,128,256]{2,1,0:T(8,128)(2,1)}, bf16[8,128,256]{2,1,0:T(8,128)(2,1)S(1)}, u32[]{:S(2)}) copy-start(bf16[8,128,256]{2,1,0:T(8,128)(2,1)S(1)} %collective-permute-done) | copy-start | bytes 1572868
  35.8 2.7 %collective-permute-start.1 = (f32[8,256,128]{2,1,0:T(8,128)S(1)}, f32[8,256,128]{2,1,0:T(8,128)S(1)}, u32[]{:S(2)}, u32[]{:S(2)}) collective-permute-start(f32[8,256,128]{2,1,0:T(8,128)S(1)} %bitcast.11), channel_id=1, source_target_pairs={{0,2},{2,0},{1,3},{3,1},{4,6},{6,4},{5,7},{7,5},{8,10},{10,8},{9,1... | collective-permute-start | bytes 3145736 | tf_op jit(solution)/shard_map/ppermute | solution.py:177
  71.3 0.7 copy-start.3
  71.4 1.3 %collective-permute-start.2 = (bf16[128,128]{1,0:T(8,128)(2,1)S(1)}, bf16[128,128]{1,0:T(8,128)(2,1)S(1)}, u32[]{:S(2)}, u32[]{:S(2)}) collective-permute-start(bf16[128,128]{1,0:T(8,128)(2,1)S(1)} %broadcast_select_fusion.4), channel_id=1, source_target_pairs={{0,2},{2,0},{1,3},{3,1},{4,6},{6,4},{5,7},{7,5},{8,10},{10,8},{9,1... | collective-permute-start | bytes 98312 | tf_op jit(solution)/shard_map/ppermute | solution.py:180

commit v12 on v10

v12 whole, which is shorter than its diff:
```python
import functools
import math

import jax
import jax.numpy as jnp
from jax import lax
from jax.experimental import pallas as pl
from jax.experimental.pallas import tpu as pltpu
from jax.sharding import Mesh, PartitionSpec as P

PASSK = 4
LOG2_E = 1.4426950408889634
LN_2 = 0.6931471805599453


def pass_rate(correct, group_size):
    counts = group_size.astype(jnp.float32)
    hit_counts = correct.astype(jnp.float32)
    product = jnp.ones_like(counts)
    for offset in range(PASSK):
        product = product * (counts - hit_counts - offset) / (counts - offset)
    return 1.0 - product


def stacked_rows(index_ref, own_ref, partner_ref, heads, head_dim, column):
    lead = index_ref[1] == 0
    first = jnp.where(lead, own_ref[...], partner_ref[...])
    second = jnp.where(lead, partner_ref[...], own_ref[...])
    base = column * heads * head_dim
    return jnp.concatenate(
        [
            block[:, base + h * head_dim:base + (h + 1) * head_dim]
            for block in (first, second)
            for h in range(heads)
        ],
        0,
    )


def tile_parts(index_ref, mine_ref, tile, tile_chips, tok_rows, heads, head_dim, score_scale, queries_t, grads_t):
    source = pl.multiple_of(tile * tile_chips * tok_rows, tok_rows)
    joined = mine_ref[pl.ds(source, tile_chips * tok_rows), :]
    key_block = joined[:, :head_dim]
    value_block = joined[:, head_dim:]
    scores = jnp.dot(key_block, queries_t, preferred_element_type=jnp.float32) * (score_scale * LOG2_E)
    grad_probs = jnp.dot(value_block, grads_t, preferred_element_type=jnp.float32)
    return key_block, scores, grad_probs


def visible_of(index_ref, tile, tile_chips, tok_rows, heads):
    chip = index_ref[0]
    core = index_ref[1]
    rows = 2 * heads * tok_rows
    key_row = lax.broadcasted_iota(jnp.int32, (tile_chips * tok_rows, 1), 0)
    lane = lax.broadcasted_iota(jnp.int32, (1, rows), 1)
    key_chip = tile * tile_chips + key_row // tok_rows
    key_pos = (2 * key_chip + core) * tok_rows + key_row % tok_rows
    query_block = (lane >= heads * tok_rows).astype(jnp.int32)
    query_pos = (2 * chip + query_block) * tok_rows + lane % tok_rows
    return key_pos <= query_pos


def forward_kernel(index_ref, own_ref, partner_ref, mine_ref, stats_ref, *, heads, head_dim, tok_rows, score_scale, tile_chips):
    chip = index_ref[0]
    last = chip // tile_chips
    rows = 2 * heads * tok_rows
    queries_t = stacked_rows(index_ref, own_ref, partner_ref, heads, head_dim, 0).astype(jnp.float32).T.astype(jnp.bfloat16)
    grads_t = stacked_rows(index_ref, own_ref, partner_ref, heads, head_dim, 1).astype(jnp.float32).T.astype(jnp.bfloat16)

    def forward(tile, carry, masked):
        peak, total, weighted = carry
        _, scores, grad_probs = tile_parts(
            index_ref, mine_ref, tile, tile_chips, tok_rows, heads, head_dim, score_scale, queries_t, grads_t
        )
        if masked:
            mask = visible_of(index_ref, tile, tile_chips, tok_rows, heads)
            scores = jnp.where(mask, scores, -1e30)
        new_peak = jnp.maximum(peak, jnp.max(scores, axis=0, keepdims=True))
        exp_terms = jnp.exp2(scores - new_peak)
        if masked:
            exp_terms = jnp.where(mask, exp_terms, 0.0)
        shrink = jnp.exp2(peak - new_peak)
        total = total * shrink + jnp.sum(exp_terms, axis=0, keepdims=True)
        weighted = weighted * shrink + jnp.sum(exp_terms * grad_probs, axis=0, keepdims=True)
        return new_peak, total, weighted

    start_carry = (
        jnp.full((1, rows), -1e30, jnp.float32),
        jnp.zeros((1, rows), jnp.float32),
        jnp.zeros((1, rows), jnp.float32),
    )
    carry = lax.fori_loop(0, last, lambda b, c: forward(b, c, False), start_carry)
    peak, total, weighted = forward(last, carry, True)
    stats_ref[0:1, :] = peak
    stats_ref[1:2, :] = total
    stats_ref[2:3, :] = weighted


def backward_kernel(
    index_ref, own_ref, partner_ref, mine_ref, stats_ref, partner_stats_ref, lse_ref, dq_ref, part_ref,
    *, heads, head_dim, tok_rows, score_scale, tile_chips,
):
    chip = index_ref[0]
    last = chip // tile_chips
    tile_count = mine_ref.shape[0] // (tile_chips * tok_rows)
    rows = 2 * heads * tok_rows
    queries = stacked_rows(index_ref, own_ref, partner_ref, heads, head_dim, 0)
    grads = stacked_rows(index_ref, own_ref, partner_ref, heads, head_dim, 1)
    queries_t = queries.astype(jnp.float32).T.astype(jnp.bfloat16)
    grads_t = grads.astype(jnp.float32).T.astype(jnp.bfloat16)
    peak = jnp.maximum(stats_ref[0:1, :], partner_stats_ref[0:1, :])
    own_shrink = jnp.exp2(stats_ref[0:1, :] - peak)
    partner_shrink = jnp.exp2(partner_stats_ref[0:1, :] - peak)
    total = stats_ref[1:2, :] * own_shrink + partner_stats_ref[1:2, :] * partner_shrink
    weighted = stats_ref[2:3, :] * own_shrink + partner_stats_ref[2:3, :] * partner_shrink
    log_totals = peak + jnp.log2(total)
    delta_rows = weighted / total
    lse_ref[...] = log_totals
    contract_first = (((0,), (0,)), ((), ()))
    tile_rows = tile_chips * tok_rows

    def backward(tile, grad_query_t, masked):
        key_block, scores, grad_probs = tile_parts(
            index_ref, mine_ref, tile, tile_chips, tok_rows, heads, head_dim, score_scale, queries_t, grads_t
        )
        probabilities = jnp.exp2(scores - log_totals)
        if masked:
            probabilities = jnp.where(visible_of(index_ref, tile, tile_chips, tok_rows, heads), probabilities, 0.0)
        grad_scores = (probabilities * (grad_probs - delta_rows)).astype(jnp.bfloat16)
        prob_bf16 = probabilities.astype(jnp.bfloat16)
        grad_query_t = grad_query_t + lax.dot_general(
            key_block, grad_scores, contract_first, preferred_element_type=jnp.float32
        )
        key_add = jnp.dot(grad_scores, queries, preferred_element_type=jnp.float32)
        value_add = jnp.dot(prob_bf16, grads, preferred_element_type=jnp.float32)
        start = pl.multiple_of(tile * tile_rows, tile_rows)
        part_ref[pl.ds(start, tile_rows), :head_dim] = key_add * score_scale
        part_ref[pl.ds(start, tile_rows), head_dim:] = value_add
        return grad_query_t

    grad_query_t = lax.fori_loop(
        0, last, lambda b, g: backward(b, g, False), jnp.zeros((head_dim, rows), jnp.float32)
    )
    grad_query = (backward(last, grad_query_t, True) * score_scale).T
    for block in range(2):
        for h in range(heads):
            row = (block * heads + h) * tok_rows
            dq_ref[block * tok_rows:(block + 1) * tok_rows, h * head_dim:(h + 1) * head_dim] = (
                grad_query[row:row + tok_rows]
            )

    def clear(tile, unused):
        start = pl.multiple_of(tile * tile_rows, tile_rows)
        part_ref[pl.ds(start, tile_rows), :] = jnp.zeros((tile_rows, 2 * head_dim), jnp.float32)
        return unused

    lax.fori_loop(last + 1, tile_count, clear, 0)


def body(queries, key_rows, value_rows, cotangent, trace_ids, correct, group_size):
    tok_rows = queries.shape[0]
    row_width = queries.shape[1]
    head_dim = key_rows.shape[1]
    head_count = row_width // head_dim
    chip_count = lax.axis_size("chip")
    chip = lax.axis_index("chip")
    core = lax.axis_index("core")
    lead = core == 0
    score_scale = 1.0 / math.sqrt(head_dim)
    pass_rates = pass_rate(correct, group_size)
    traces = jnp.arange(pass_rates.shape[0], dtype=jnp.int32)
    weights = jnp.sum(
        jnp.where(trace_ids[:, None] == traces[None, :], pass_rates[None, :], 0.0), axis=1
    )
    out_grads = (weights[:, None] * cotangent.astype(jnp.float32)).astype(jnp.bfloat16)

    joined = jnp.concatenate([key_rows, value_rows], 1)
    spread = jnp.broadcast_to(joined[None], (chip_count,) + joined.shape)
    mine = lax.all_to_all(spread, "chip", 0, 0, tiled=True).reshape(chip_count * tok_rows, 2 * head_dim)
    own = jnp.concatenate([queries, out_grads], 1)
    partner = lax.ppermute(own, "core", [(0, 1), (1, 0)])

    rows = 2 * head_count * tok_rows
    vmem = pl.BlockSpec(memory_space=pltpu.MemorySpace.VMEM)
    smem = pl.BlockSpec(memory_space=pltpu.MemorySpace.SMEM)
    settings = dict(
        heads=head_count, head_dim=head_dim, tok_rows=tok_rows, score_scale=score_scale,
        tile_chips=math.gcd(chip_count, 4),
    )
    index = jnp.stack([chip, core]).astype(jnp.int32)
    stats = pl.pallas_call(
        functools.partial(forward_kernel, **settings),
        out_shape=jax.ShapeDtypeStruct((8, rows), jnp.float32),
        in_specs=[smem, vmem, vmem, vmem],
        out_specs=vmem,
    )(index, own, partner, mine)
    partner_stats = lax.ppermute(stats, "core", [(0, 1), (1, 0)])
    log_totals, query_grads, own_part = pl.pallas_call(
        functools.partial(backward_kernel, **settings),
        out_shape=(
            jax.ShapeDtypeStruct((1, rows), jnp.float32),
            jax.ShapeDtypeStruct((2 * tok_rows, row_width), jnp.float32),
            jax.ShapeDtypeStruct((chip_count * tok_rows, 2 * head_dim), jnp.float32),
        ),
        in_specs=[smem, vmem, vmem, vmem, vmem, vmem],
        out_specs=(vmem, vmem, vmem),
    )(index, own, partner, mine, stats, partner_stats)

    reduced = jnp.sum(
        lax.all_to_all(own_part.reshape(chip_count, tok_rows, 2 * head_dim), "chip", 0, 0, tiled=True),
        axis=0,
    )
    grad_keys = reduced[:, :head_dim].astype(jnp.bfloat16)
    grad_values = reduced[:, head_dim:].astype(jnp.bfloat16)
    mine_dq = jnp.where(lead, query_grads[:tok_rows], query_grads[tok_rows:])
    other_dq = jnp.where(lead, query_grads[tok_rows:], query_grads[:tok_rows])
    query_grads = mine_dq + lax.ppermute(other_dq, "core", [(0, 1), (1, 0)])
    half = head_count * tok_rows
    own_totals = jnp.where(lead, log_totals[:, :half], log_totals[:, half:]) * LN_2
    log_totals = own_totals.reshape(head_count, tok_rows).T
    return (log_totals, query_grads, grad_keys, grad_values)


def solution(mesh):
    order = [mesh.axis_names.index("ctx"), mesh.axis_names.index("head")]
    devices = mesh.devices.transpose(order)
    ctx_size, head_size = devices.shape
    chip_mesh = Mesh(devices.reshape(ctx_size // 2, 2, head_size), ("chip", "core", "head"))
    rows = P(("chip", "core"), "head")
    return jax.shard_map(
        body,
        mesh=chip_mesh,
        in_specs=(rows, rows, rows, rows, P(("chip", "core")), P(), P()),
        out_specs=(rows, rows, rows, rows),
        check_vma=False,
    )
```

time: 73.7 us -> 70.4 us (0.955)
  blocking collectives: 32.6 us -> 0 us
  waiting for transfers between devices: 17.4 us -> 37.5 us
  starting transfers between devices: 7.68 us -> 14.6 us
  local copies, waits for them, and re-layouts: 2.24 us -> 4.88 us
  other arithmetic: 5.39 us -> 3.14 us
  Pallas kernels: 7.24 us -> 9.08 us
    all_to_all x1 -> x0, blocking collectives: 32.6 us -> none  [body(): lax.all_to_all(own_part, 'chip', 0, 0, tiled=True)]
    all_to_all x1 -> x2, waiting for transfers between devices: 13.9 us -> 34.4 us  [the longest x1 23.4 us: body(): lax.all_to_all(own_part.reshape(chip_count, tok_rows, 2 * head_dim), 'chi...]
    all_to_all x1 -> x2, starting transfers between devices: 7.41 us -> 14.5 us  [the longest x1 7.41 us: body(): lax.all_to_all(spread, 'chip', 0, 0, tiled=True)]
    select_n x3 -> x1, other arithmetic: 2.32 us -> 0.04 us  [body(): other_dq = jnp.where(lead, query_grads[tok_rows:], query_grads[:tok_rows])]
    unnamed x14 -> x22, local copies, waits for them, and re-layouts: 1.41 us -> 3.43 us
    pallas_call x1 -> x2, Pallas kernels: 7.24 us -> 9.08 us  [the longest x1 5.23 us: body(): pl.pallas_call(functools.partial(backward_kernel, **settings), out_shape=...]
  transfers between devices with their start and end apart: 4 -> 5, of which waited for: 3 -> 5; matrix products, arithmetic and copies ran while one was open for 3% -> 3% of each run, Pallas kernels for 0% -> 0%
where the time goes in v12:
time: 70.4 us; the launch traced here: 69.9 us
  waiting for transfers between devices  37.5 us (53%)
  starting transfers between devices  14.6 us (21%)
  Pallas kernels  9.08 us (13%)
  local copies, waits for them, and re-layouts  4.88 us (7%)
  other arithmetic  3.14 us (4%)
  between operations  0.73 us (1%)
    all_to_all x1, waiting for transfers between devices, body(): lax.all_to_all(own_part.reshape(chip_count, tok_rows, 2 * head_dim), 'chi...  23.4 us
    all_to_all x1, waiting for transfers between devices, body(): lax.all_to_all(spread, 'chip', 0, 0, tiled=True)  11 us
    all_to_all x1, starting transfers between devices, body(): lax.all_to_all(spread, 'chip', 0, 0, tiled=True)  7.41 us
    all_to_all x1, starting transfers between devices, body(): lax.all_to_all(own_part.reshape(chip_count, tok_rows, 2 * head_dim), 'chi...  7.06 us
    pallas_call x1, Pallas kernels, body(): pl.pallas_call(functools.partial(backward_kernel, **settings), out_shape=...  5.23 us
    pallas_call x1, Pallas kernels, body(): pl.pallas_call(functools.partial(forward_kernel, **settings), out_shape=j...  3.85 us
    unnamed x22, local copies, waits for them, and re-layouts  3.43 us
    ppermute x1, waiting for transfers between devices, body(): partner_stats = lax.ppermute(stats, 'core', [(0, 1), (1, 0)])  1.44 us
  transfers between devices with their start and end apart: 5, of which 5 were waited for; matrix products, arithmetic and copies ran while one was open for 3% of the time, Pallas kernels for 0%

profile of v12, /device:TPU:0, one launch (start us, length us, event | category | flops | bytes accessed | tf_op | source)
XLA Modules:
  0.0 69.9 jit_solution(17128368374536292226)
XLA Ops:
  0.6 0.8 %pad_maximum_fusion.1 = bf16[128,256]{1,0:T(8,128)(2,1)S(1)} fusion(bf16[128,128]{1,0:T(8,128)(2,1)} %param.9, bf16[128,128]{1,0:T(8,128)(2,1)} %param.8), kind=kLoop, calls=%fused_computation.4 | loop fusion | flops 131072 | bytes 131072 | tf_op jit(solution)/shard_map/concatenate | solution.py:177
  1.4 0.8 %broadcast_in_dim.24 = bf16[8,128,256]{2,1,0:T(8,128)(2,1)} broadcast(bf16[128,256]{1,0:T(8,128)(2,1)S(1)} %pad_maximum_fusion.1), dimensions={1,2} | broadcast | bytes 589824 | tf_op jit(solution)/shard_map/broadcast_in_dim | solution.py:178
  2.2 7.4 %all-to-all-start = ((bf16[8,128,256]{2,1,0:T(8,128)(2,1)}), bf16[8,128,256]{2,1,0:T(8,128)(2,1)S(1)}, u32[]{:S(2)}, u32[]{:S(2)}) async-start(bf16[8,128,256]{2,1,0:T(8,128)(2,1)} %broadcast_in_dim.24), calls=%async_computation | async-start | bytes 1048576 | tf_op jit(solution)/shard_map/all_to_all | solution.py:179
  9.7 0.0 copy-done.8
  9.7 0.0 copy-done.9
  9.7 0.0 copy-start.10
  9.7 0.6 copy-done.10
  10.3 0.1 select_reduce_fusion
  10.4 0.1 multiply_convert_fusion
  10.5 0.8 %copy-done.5 = bf16[128,768]{1,0:T(8,128)(2,1)S(1)} copy-done((bf16[128,768]{1,0:T(8,128)(2,1)S(1)}, bf16[128,768]{1,0:T(8,128)(2,1)}, u32[]{:S(2)}) %copy-start.5) | copy-done | bytes 196632
  11.4 0.0 copy-start.1
  11.4 0.1 collective-permute-start
  11.5 0.6 pad_add_fusion.index_ref
  12.1 1.1 %collective-permute-done.partner_ref = bf16[128,1536]{1,0:T(8,128)(2,1)S(1)} collective-permute-done((bf16[128,1536]{1,0:T(8,128)(2,1)S(1)}, bf16[128,1536]{1,0:T(8,128)(2,1)S(1)}, u32[]{:S(2)}, u32[]{:S(2)}) %collective-permute-start) | collective-permute-done | bytes 393248 | tf_op jit(solution)/shard_map/ppermute | solution.py:181
  13.2 11.0 %all-to-all-done = bf16[8,128,256]{2,1,0:T(8,128)(2,1)S(1)} async-done(((bf16[8,128,256]{2,1,0:T(8,128)(2,1)}), bf16[8,128,256]{2,1,0:T(8,128)(2,1)S(1)}, u32[]{:S(2)}, u32[]{:S(2)}) %all-to-all-start) | async-done | bytes 524320 | tf_op jit(solution)/shard_map/all_to_all | solution.py:179
  24.1 0.0 copy-done.3
  24.2 0.8 %copy-done = bf16[8,128,256]{2,1,0:T(8,128)(2,1)} copy-done((bf16[8,128,256]{2,1,0:T(8,128)(2,1)}, bf16[8,128,256]{2,1,0:T(8,128)(2,1)S(1)}, u32[]{:S(2)}) %copy-start) | copy-done | bytes 524312
  24.9 3.8 %shard_map.102.stats_ref = f32[8,1536]{1,0:T(8,128)} custom-call(s32[2]{0:T(128)} %pad_add_fusion.index_ref, bf16[128,1536]{1,0:T(8,128)(2,1)} %copy-done.1, bf16[128,1536]{1,0:T(8,128)(2,1)} %copy-done.3, bf16[1024,256]{1,0:T(8,128)(2,1)} %bitcast.7), custom_call_target="tpu_custom_call" | custom-call | tf_op jit(solution)/shard_map/pallas_call | solution.py:191
  28.8 0.0 collective-permute-start.1
  28.8 1.4 %collective-permute-done.1.partner_stats_ref = f32[8,1536]{1,0:T(8,128)S(1)} collective-permute-done((f32[8,1536]{1,0:T(8,128)}, f32[8,1536]{1,0:T(8,128)S(1)}, u32[]{:S(2)}, u32[]{:S(2)}) %collective-permute-start.1) | collective-permute-done | bytes 49184 | tf_op jit(solution)/shard_map/ppermute | solution.py:197
  30.2 0.6 copy-done.6
  30.8 5.2 %shard_map.103 = (f32[1,1536]{1,0:T(1,128)}, f32[256,768]{1,0:T(8,128)}, f32[1024,256]{1,0:T(8,128)}) custom-call(s32[2]{0:T(128)} %pad_add_fusion.index_ref, bf16[128,1536]{1,0:T(8,128)(2,1)} %copy-done.1, bf16[128,1536]{1,0:T(8,128)(2,1)} %copy-done.3, bf16[1024,256]{1,0:T(8,128)(2,1)} %bitcast.8, f32[8,1536]{1,0:T(8,128)} %shard_map.102.stats_ref, ...), custom_call_target="tpu_custom_call" | custom-call | tf_op jit(solution)/shard_map/pallas_call | solution.py:198
  36.1 7.1 %all-to-all-start.1 = ((f32[8,128,256]{2,1,0:T(8,128)}), f32[8,128,256]{2,1,0:T(8,128)S(1)}, u32[]{:S(2)}, u32[]{:S(2)}) async-start(f32[8,128,256]{2,1,0:T(8,128)} %bitcast.9), calls=%async_computation.1 | async-start | bytes 2097152 | tf_op jit(solution)/shard_map/all_to_all | solution.py:210
  43.1 0.0 copy-start.7
  43.2 0.1 collective-permute-start.2
  43.3 0.6 copy-done.7
  43.8 0.6 fusion.1
  44.4 0.6 collective-permute-done.2
  45.0 0.8 %select_add_fusion = f32[128,768]{1,0:T(8,128)} fusion(f32[128,768]{1,0:T(8,128)S(1)} %collective-permute-done.2, f32[256,768]{1,0:T(8,128)S(1)} %copy-done.2, pred[]{:T(512)S(6)} %eq.16), kind=kLoop, calls=%fused_computation.1 | loop fusion | flops 196608 | bytes 1572865 | tf_op jit(solution)/shard_map/add | solution.py:217
  45.8 23.4 %all-to-all-done.1 = f32[8,128,256]{2,1,0:T(8,128)S(1)} async-done(((f32[8,128,256]{2,1,0:T(8,128)}), f32[8,128,256]{2,1,0:T(8,128)S(1)}, u32[]{:S(2)}, u32[]{:S(2)}) %all-to-all-start.1) | async-done | bytes 1048608 | tf_op jit(solution)/shard_map/all_to_all | solution.py:210
  69.2 0.1 reduce_sum.19
  69.3 0.6 fusion.3
  (14 shorter events, 0.1 us)
Async XLA Ops:
  2.2 7.4 %copy-start.8 = (s32[16]{0:T(128)S(1)}, s32[16]{0:T(128)}, u32[]{:S(2)}) copy-start(s32[16]{0:T(128)} %param.12) | copy-start | bytes 196
  2.2 7.4 %copy-start.9 = (s32[16]{0:T(128)S(1)}, s32[16]{0:T(128)}, u32[]{:S(2)}) copy-start(s32[16]{0:T(128)} %param.13) | copy-start | bytes 196
  2.2 8.2 %copy-start.4 = (bf16[128,768]{1,0:T(8,128)(2,1)S(1)}, bf16[128,768]{1,0:T(8,128)(2,1)}, u32[]{:S(2)}) copy-start(bf16[128,768]{1,0:T(8,128)(2,1)} %param.10) | copy-start | bytes 589828
  2.2 21.9 %all-to-all-start = ((bf16[8,128,256]{2,1,0:T(8,128)(2,1)}), bf16[8,128,256]{2,1,0:T(8,128)(2,1)S(1)}, u32[]{:S(2)}, u32[]{:S(2)}) async-start(bf16[8,128,256]{2,1,0:T(8,128)(2,1)} %broadcast_in_dim.24), calls=%async_computation | async-start | bytes 1048576 | tf_op jit(solution)/shard_map/all_to_all | solution.py:179
  9.7 0.7 copy-start.10
  10.4 0.9 %copy-start.5 = (bf16[128,768]{1,0:T(8,128)(2,1)S(1)}, bf16[128,768]{1,0:T(8,128)(2,1)}, u32[]{:S(2)}) copy-start(bf16[128,768]{1,0:T(8,128)(2,1)} %param.7) | copy-start | bytes 589828
  11.4 12.8 %copy-start.1 = (bf16[128,1536]{1,0:T(8,128)(2,1)}, bf16[128,1536]{1,0:T(8,128)(2,1)S(1)}, u32[]{:S(2)}) copy-start(bf16[128,1536]{1,0:T(8,128)(2,1)S(1)} %pad_maximum_fusion.own_ref) | copy-start | bytes 1179652
  11.4 1.8 %collective-permute-start = (bf16[128,1536]{1,0:T(8,128)(2,1)S(1)}, bf16[128,1536]{1,0:T(8,128)(2,1)S(1)}, u32[]{:S(2)}, u32[]{:S(2)}) collective-permute-start(bf16[128,1536]{1,0:T(8,128)(2,1)S(1)} %pad_maximum_fusion.own_ref), channel_id=1, source_target_pairs={{0,2},{2,0},{1,3},{3,1},{4,6},{6,4},{5,7},{7,5},{8,10},{10,8},{9,1... | collective-permute-start | bytes 1179656 | tf_op jit(solution)/shard_map/ppermute | solution.py:181
  13.2 11.0 %copy-start.3 = (bf16[128,1536]{1,0:T(8,128)(2,1)}, bf16[128,1536]{1,0:T(8,128)(2,1)S(1)}, u32[]{:S(2)}) copy-start(bf16[128,1536]{1,0:T(8,128)(2,1)S(1)} %collective-permute-done.partner_ref) | copy-start | bytes 1179652
  24.1 0.8 %copy-start = (bf16[8,128,256]{2,1,0:T(8,128)(2,1)}, bf16[8,128,256]{2,1,0:T(8,128)(2,1)S(1)}, u32[]{:S(2)}) copy-start(bf16[8,128,256]{2,1,0:T(8,128)(2,1)S(1)} %all-to-all-done) | copy-start | bytes 1572868
  28.8 1.4 %collective-permute-start.1 = (f32[8,1536]{1,0:T(8,128)}, f32[8,1536]{1,0:T(8,128)S(1)}, u32[]{:S(2)}, u32[]{:S(2)}) collective-permute-start(f32[8,1536]{1,0:T(8,128)} %shard_map.102.stats_ref), channel_id=1, source_target_pairs={{0,2},{2,0},{1,3},{3,1},{4,6},{6,4},{5,7},{7,5},{8,10},{10,8},{9,1... | collective-permute-start | bytes 147464 | tf_op jit(solution)/shard_map/ppermute | solution.py:197
  30.2 0.6 copy-start.6
  36.1 7.1 %copy-start.2 = (f32[256,768]{1,0:T(8,128)S(1)}, f32[256,768]{1,0:T(8,128)}, u32[]{:S(2)}) copy-start(f32[256,768]{1,0:T(8,128)} %get-tuple-element.8) | copy-start | bytes 2359300
  36.1 33.1 %all-to-all-start.1 = ((f32[8,128,256]{2,1,0:T(8,128)}), f32[8,128,256]{2,1,0:T(8,128)S(1)}, u32[]{:S(2)}, u32[]{:S(2)}) async-start(f32[8,128,256]{2,1,0:T(8,128)} %bitcast.9), calls=%async_computation.1 | async-start | bytes 2097152 | tf_op jit(solution)/shard_map/all_to_all | solution.py:210
  43.1 0.7 copy-start.7
  43.2 1.8 %collective-permute-start.2 = (f32[128,768]{1,0:T(8,128)S(1)}, f32[128,768]{1,0:T(8,128)S(1)}, u32[]{:S(2)}, u32[]{:S(2)}) collective-permute-start(f32[128,768]{1,0:T(8,128)S(1)} %slice_select_fusion), channel_id=1, source_target_pairs={{0,2},{2,0},{1,3},{3,1},{4,6},{6,4},{5,7},{7,5},{8,10},{10,8},{9,1... | collective-permute-start | bytes 1179656 | tf_op jit(solution)/shard_map/ppermute | solution.py:217
